TPU v7x, 128 devices: a whole 4x4x4 slice. The times are simulated.
128 devices in a mesh: req: 16 (over z, x), head: 8 (over y, core).
Axes of the slice: x: 4, y: 4, z: 4, core: 2. Of those that a mesh axis runs over, the one named last changes fastest.
Arguments:
- tokens: bfloat16 [768, 1024], P('req'), may hold values from -6 to 6
- cache_len: int32 [768], P('req'), may hold values from 1 to 1024, as said below
- page_table: int32 [768, 8], P('req'), may hold values from 0 to 159, as said below
- page_live: int32 [768, 8], P('req'), may hold values 0 or 1
- group_of: int32 [768], replicated, may hold values from 0 to 63, as said below
- kv_pool: bfloat16 [2560, 128, 2, 1024], P('req', None, None, 'head')
- enc_kv: bfloat16 [64, 2048, 2, 1024], P('req', None, None, 'head')
- w_self_in: bfloat16 [1024, 3, 1024], P('req', None, 'head'), may hold values from -0.1875 to 0.1875
- w_self_out: bfloat16 [1024, 1024], P('head', 'req'), may hold values from -0.75 to 0.75
- w_cross_q: bfloat16 [1024, 1024], P('req', 'head'), may hold values from -0.1875 to 0.1875
- w_cross_out: bfloat16 [1024, 1024], P('head', 'req'), may hold values from -0.75 to 0.75
- self_gain: float32 [1024], replicated, may hold values from 0.25 to 1.75
- self_bias: float32 [1024], replicated, may hold values from -1.75 to 1.75
- cross_gain: float32 [1024], replicated, may hold values from 0.25 to 1.75
- cross_bias: float32 [1024], replicated, may hold values from -1.75 to 1.75
Outputs:
- hidden_out: bfloat16 [768, 1024], P('req')
- new_kv: bfloat16 [768, 2, 1024], P('req', None, 'head')
Inputs may be any that keep to these rules, and one draw needn't show every extreme that they name: The pages of one device's requests, ceil(cache_len / 128) each, add up to at most 160; some request holds 1024 positions. `page_table`: for request r the slots j < ceil(cache_len[r] / 128) name pages of the pool part of r's index of req; no page is named by two such slots. Other slots hold any page number. `group_of`: every group has 8 to 16 requests; some group has exactly 16 and some exactly 8.
All inputs are finite; a program needn't handle non-finite values. No bound on the sum of `page_live` on one device may be relied on, other than what follows from the above.
Results may differ from a plain program's by a relative error of at most 0.019.
The roundings to bfloat16 on the way count: a program that leaves them out, or rounds other values in their place, can miss the bound.
Values may be sent and summed in bfloat16 or wider, within the bound.
No kernel may reach another device: no remote copies, remote signals or barrier semaphores. Data moves between devices by JAX's collectives and lax.ppermute only.
A program may use at most 128 MiB of HBM per device.

v0:
```python
import jax
import jax.numpy as jnp
from jax import lax
from jax.sharding import PartitionSpec as P

HEAD_DIM = 64
GMAX = 16


def layer_norm(summed, gain_row, bias_row):
    center = summed - jnp.mean(summed, axis=-1, keepdims=True)
    spread = jnp.mean(center * center, axis=-1, keepdims=True)
    return center * lax.rsqrt(spread + 1e-05) * gain_row + bias_row


def head_total(partial_value):
    return lax.psum(partial_value, "head")


def paged_attention(query, new_key, new_value, cache_len, page_table, page_live, kv_pool, scale):
    pages_here, page_rows, _, head_cols = kv_pool.shape
    heads_here = head_cols // HEAD_DIM
    rows_here = query.shape[0]
    slots = page_table.shape[1]
    counts = (cache_len + page_rows - 1) // page_rows
    slot_index = jnp.arange(slots, dtype=jnp.int32)
    in_use = slot_index[None, :] < counts[:, None]
    hits = (
        page_table[:, :, None] == jnp.arange(pages_here, dtype=jnp.int32)[None, None, :]
    ) & in_use[:, :, None]
    owners = jnp.any(hits, axis=1)
    page_slot = jnp.sum(jnp.where(hits, slot_index[None, :, None], 0), axis=(0, 1))
    page_flag = jnp.sum(jnp.where(hits, page_live[:, :, None], 0), axis=(0, 1))
    page_length = jnp.sum(jnp.where(owners, cache_len[:, None], 0), axis=0)
    offsets = page_slot[:, None] * page_rows + jnp.arange(page_rows, dtype=jnp.int32)[None, :]
    counted = (page_flag[:, None] == 1) & (offsets < page_length[:, None])
    owner_weights = owners.astype(jnp.float32)
    page_query = jnp.dot(owners.T.astype(jnp.bfloat16), query, preferred_element_type=jnp.float32)
    page_query = page_query.astype(jnp.bfloat16).reshape(pages_here, heads_here, HEAD_DIM)
    stored = kv_pool.reshape(pages_here, page_rows, 2, heads_here, HEAD_DIM)
    scores = (
        jnp.einsum("pthd,phd->pht", stored[:, :, 0], page_query, preferred_element_type=jnp.float32)
        * scale
    )
    scores = jnp.where(counted[:, None, :], scores, -1e30)
    q_heads = query.astype(jnp.float32).reshape(rows_here, heads_here, HEAD_DIM)
    new_score = (
        jnp.sum(
            q_heads * new_key.astype(jnp.float32).reshape(rows_here, heads_here, HEAD_DIM), axis=-1
        )
        * scale
    )
    page_top = jnp.max(scores, axis=2)
    owner_top = jnp.max(jnp.where(owners[:, :, None], page_top[None, :, :], -1e30), axis=1)
    top = jnp.maximum(owner_top, new_score)
    page_shift = jnp.dot(owner_weights.T, top, precision=lax.Precision.HIGHEST)
    weights = jnp.where(counted[:, None, :], jnp.exp(scores - page_shift[:, :, None]), 0.0)
    new_weight = jnp.exp(new_score - top)
    total = (
        jnp.dot(owner_weights, jnp.sum(weights, axis=2), precision=lax.Precision.HIGHEST)
        + new_weight
    )
    page_sum = jnp.einsum(
        "pht,pthd->phd",
        weights.astype(jnp.bfloat16),
        stored[:, :, 1],
        preferred_element_type=jnp.float32,
    )
    summed = jnp.dot(
        owner_weights, page_sum.reshape(pages_here, head_cols), precision=lax.Precision.HIGHEST
    )
    rounded_new = lax.optimization_barrier(new_weight.astype(jnp.bfloat16)).astype(jnp.float32)
    own_term = rounded_new[:, :, None] * new_value.astype(jnp.float32).reshape(
        rows_here, heads_here, HEAD_DIM
    )
    summed = summed.reshape(rows_here, heads_here, HEAD_DIM) + own_term
    return (summed / total[:, :, None]).reshape(rows_here, head_cols).astype(jnp.bfloat16)


def group_attention(cross_query, group_of, enc_kv, scale):
    groups_here, positions, _, head_cols = enc_kv.shape
    heads_here = head_cols // HEAD_DIM
    every_query = lax.all_gather(cross_query, "req", axis=0, tiled=True)
    local_groups = lax.axis_index("req") * groups_here + jnp.arange(groups_here, dtype=jnp.int32)
    member = group_of[None, :] == local_groups[:, None]
    member_rank = jnp.cumsum(member.astype(jnp.int32), axis=1) - 1
    picker = member[:, None, :] & (
        member_rank[:, None, :] == jnp.arange(GMAX, dtype=jnp.int32)[None, :, None]
    )
    picker = picker.astype(jnp.bfloat16)
    group_query = jnp.einsum("gkr,rc->gkc", picker, every_query, preferred_element_type=jnp.float32)
    group_query = group_query.astype(jnp.bfloat16).reshape(groups_here, GMAX, heads_here, HEAD_DIM)
    stored = enc_kv.reshape(groups_here, positions, 2, heads_here, HEAD_DIM)
    scores = (
        jnp.einsum(
            "gehd,gkhd->gkhe", stored[:, :, 0], group_query, preferred_element_type=jnp.float32
        )
        * scale
    )
    top = jnp.max(scores, axis=3)
    weights = jnp.exp(scores - top[:, :, :, None])
    total = jnp.sum(weights, axis=3)
    summed = jnp.einsum(
        "gkhe,gehd->gkhd",
        weights.astype(jnp.bfloat16),
        stored[:, :, 1],
        preferred_element_type=jnp.float32,
    )
    context = (
        (summed / total[:, :, :, None]).astype(jnp.bfloat16).reshape(groups_here, GMAX, head_cols)
    )
    placed = jnp.einsum("gkr,gkc->rc", picker, context, preferred_element_type=jnp.float32)
    return lax.psum_scatter(placed.astype(jnp.bfloat16), "req", scatter_dimension=0, tiled=True)


def on_device(
    tokens,
    cache_len,
    page_table,
    page_live,
    group_of,
    kv_pool,
    enc_kv,
    w_self_in,
    w_self_out,
    w_cross_q,
    w_cross_out,
    self_gain,
    self_bias,
    cross_gain,
    cross_bias,
):
    rows_here = tokens.shape[0]
    width = tokens.shape[1]
    head_cols = kv_pool.shape[3]
    scale = HEAD_DIM ** (-0.5)
    full_in, full_out, full_query, full_cross = (
        lax.all_gather(w_self_in, "req", axis=0, tiled=True),
        lax.all_gather(w_self_out, "req", axis=1, tiled=True),
        lax.all_gather(w_cross_q, "req", axis=0, tiled=True),
        lax.all_gather(w_cross_out, "req", axis=1, tiled=True),
    )
    projected = jnp.dot(
        tokens, full_in.reshape(width, 3 * head_cols), preferred_element_type=jnp.float32
    )
    qkv = projected.astype(jnp.bfloat16).reshape(rows_here, 3, head_cols)
    self_ctx = paged_attention(
        qkv[:, 0], qkv[:, 1], qkv[:, 2], cache_len, page_table, page_live, kv_pool, scale
    )
    self_proj = head_total(jnp.dot(self_ctx, full_out, preferred_element_type=jnp.float32))
    h_first = layer_norm(tokens.astype(jnp.float32) + self_proj, self_gain, self_bias).astype(
        jnp.bfloat16
    )
    cross_query = jnp.dot(h_first, full_query, preferred_element_type=jnp.float32)
    cross_query = cross_query.astype(jnp.bfloat16)
    cross_ctx = group_attention(cross_query, group_of, enc_kv, scale)
    cross_proj = head_total(jnp.dot(cross_ctx, full_cross, preferred_element_type=jnp.float32))
    hidden_out = layer_norm(
        h_first.astype(jnp.float32) + cross_proj, cross_gain, cross_bias
    ).astype(jnp.bfloat16)
    return (hidden_out, qkv[:, 1:3])


def solution(mesh):
    return jax.shard_map(
        on_device,
        mesh=mesh,
        in_specs=(
            P("req", None),
            P("req"),
            P("req", None),
            P("req", None),
            P(),
            P("req", None, None, "head"),
            P("req", None, None, "head"),
            P("req", None, "head"),
            P("head", "req"),
            P("req", "head"),
            P("head", "req"),
            P(),
            P(),
            P(),
            P(),
        ),
        out_specs=(P("req", None), P("req", None, "head")),
        check_vma=False,
    )
```

profile of v0, /device:TPU:1, one launch (start us, length us, event | category | flops | bytes accessed | tf_op | source)
XLA Modules:
  0.0 332.8 jit_solution(13916486938869011712)
XLA Ops:
  7.2 21.3 %all_gather.15 = bf16[1024,3,128]{2,0,1:T(8,128)(2,1)S(1)} all-gather(bf16[64,3,128]{2,0,1:T(8,128)(2,1)} %param.22), channel_id=1, replica_groups=mesh['req'=16,'head'=8] {'req'}, dimensions={0}, use_global_device_ids=true | all-gather | bytes 835584 | tf_op jit(solution)/shard_map/all_gather | solution.py:138
  28.5 0.3 copy.47
  28.8 1.2 convolution_convert_fusion.1
  30.1 0.2 fusion.36
  30.3 0.8 copy.45
  31.0 0.7 and_select_fusion
  31.8 0.2 fusion.15
  32.0 0.7 select_reduce_fusion.3
  32.8 0.8 copy.46
  33.5 0.2 select_reduce_fusion.1
  33.8 0.2 convolution_convert_fusion
  34.1 0.2 copy.56
  34.3 25.6 %copy.49 = bf16[160,128,2,128]{1,3,2,0:T(8,128)(2,1)} copy(bf16[160,128,2,128]{3,2,1,0:T(2,128)(2,1)} %param.20) | data formatting | bytes 20971520 | tf_op args[5]
  59.9 4.0 %fusion.1 = f32[160,2,1,128]{3,2,1,0:T(1,128)S(1)} fusion(bf16[160,2,64,1]{2,3,1,0:T(2,128)(2,1)S(1)} %copy.56, bf16[160,128,2,2,64]{1,4,3,2,0:T(8,128)(2,1)} %bitcast.92), kind=kOutput, calls=%fused_computation.3 | convolution fusion | flops 5242880 | bytes 5447680 | tf_op jit(solution)/shard_map/pthd,phd->pht/dot_general | solution.py:42
  63.9 0.1 fusion.31
  64.0 0.1 fusion.25
  64.6 0.1 fusion.41
  64.7 0.3 fusion.22
  65.0 0.1 convolution_add_fusion.1
  65.1 5.3 %fusion = f32[160,2,1,64]{3,2,1,0:T(1,128)S(1)} fusion(bf16[160,128,2,2,64]{1,4,3,2,0:T(8,128)(2,1)} %bitcast.93, bf16[160,2,128,1]{2,0,1,3:T(8,128)(2,1)S(1)} %get-tuple-element.7), kind=kOutput, calls=%fused_computation.1 | convolution fusion | flops 5242880 | bytes 5406720 | tf_op jit(solution)/shard_map/pht,pthd->phd/dot_general | solution.py:63
  70.4 0.2 copy.59
  70.7 0.2 fusion.9
  71.1 17.3 %all_gather.16 = bf16[128,1024]{0,1:T(8,128)(2,1)S(1)} all-gather(bf16[128,64]{0,1:T(8,128)(2,1)S(1)} %copy-done.1), channel_id=1, replica_groups=mesh['req'=16,'head'=8] {'req'}, dimensions={1}, use_global_device_ids=true | all-gather | bytes 278528 | tf_op jit(solution)/shard_map/all_gather | solution.py:139
  88.4 0.9 fusion.48
  89.5 1.1 reduce-window.6
  90.6 0.2 slice_reduce_fusion
  90.8 0.2 reduce-window.9
  91.1 11.2 %copy.53 = bf16[4,2048,2,128]{1,3,0,2:T(8,128)(2,1)} copy(bf16[4,2048,2,128]{3,2,1,0:T(2,128)(2,1)} %param.21) | data formatting | bytes 8388608 | tf_op args[6]
  102.4 17.3 %all_gather.17 = bf16[1024,128]{1,0:T(8,128)(2,1)S(1)} all-gather(bf16[64,128]{1,0:T(8,128)(2,1)S(1)} %copy-done.2), channel_id=1, replica_groups=mesh['req'=16,'head'=8] {'req'}, dimensions={0}, use_global_device_ids=true | all-gather | bytes 278528 | tf_op jit(solution)/shard_map/all_gather | solution.py:140
  119.7 37.6 %all-reduce.4.cloned.1.call-done = f32[48,1024]{1,0:T(8,128)} async-done(((f32[48,1024]{1,0:T(8,128)}), f32[48,1024]{1,0:T(8,128)}) %all-reduce.4.cloned.1.call-update) | async-done | bytes 196624 | tf_op jit(solution)/shard_map/psum | solution.py:17
  157.3 1.1 fusion.32
  158.4 1.1 multiply_reduce_fusion.1
  159.5 1.0 add_convert_fusion.1
  160.6 0.2 convolution_convert_fusion.3
  160.7 18.8 %all_gather.18 = bf16[768,128]{1,0:T(8,128)(2,1)S(1)} all-gather(bf16[48,128]{1,0:T(8,128)(2,1)S(1)} %convolution_convert_fusion.3), channel_id=1, replica_groups=mesh['req'=16,'head'=8] {'req'}, dimensions={0}, use_global_device_ids=true | all-gather | bytes 208896 | tf_op jit(solution)/shard_map/all_gather | solution.py:83
  179.6 0.2 convolution_convert_fusion.2
  179.8 2.1 fusion.47
  181.9 0.3 fusion.10
  182.2 2.3 fusion.7
  184.7 1.0 fusion.4
  185.7 17.9 %all_gather.19 = bf16[128,1024]{0,1:T(8,128)(2,1)S(1)} all-gather(bf16[128,64]{0,1:T(8,128)(2,1)S(1)} %copy-done.3), channel_id=1, replica_groups=mesh['req'=16,'head'=8] {'req'}, dimensions={1}, use_global_device_ids=true | all-gather | bytes 278528 | tf_op jit(solution)/shard_map/all_gather | solution.py:141
  203.6 57.1 %reduce-scatter.4.cloned.1.call-done = bf16[48,128]{1,0:T(8,128)(2,1)} async-done(((bf16[768,128]{1,0:T(8,128)(2,1)}), bf16[48,128]{1,0:T(8,128)(2,1)}) %reduce-scatter.4.cloned.1.call-update) | async-done | bytes 12304
  260.8 1.6 fusion.49
  262.4 0.6 slice.48
  263.0 59.3 %all-reduce.6.cloned.1.call-done = f32[48,1024]{1,0:T(8,128)} async-done(((f32[48,1024]{1,0:T(8,128)}), f32[48,1024]{1,0:T(8,128)}) %all-reduce.6.cloned.1.call-update) | async-done | bytes 196624 | tf_op jit(solution)/shard_map/psum | solution.py:17
  322.4 1.1 fusion.33
  323.4 1.1 multiply_reduce_fusion
  324.6 1.7 add_convert_fusion
  (51 shorter events, 1.5 us)
Async XLA Ops:
  7.2 150.1 %all-reduce.4.cloned.1.call-start = ((), (), s32[]{:S(2)}) async-start(), calls=%async_computation.1 | async-start | bytes 393216 | tf_op jit(solution)/shard_map/psum | solution.py:17
  59.8 11.2 %copy-start.1 = (bf16[128,64]{0,1:T(8,128)(2,1)S(1)}, bf16[128,64]{0,1:T(8,128)(2,1)}, u32[]{:S(2)}) copy-start(bf16[128,64]{0,1:T(8,128)(2,1)} %param.23) | copy-start | bytes 49156
  63.9 25.5 %copy-start.4 = (s32[768]{0:T(1024)S(1)}, s32[768]{0:T(1024)}, u32[]{:S(2)}) copy-start(s32[768]{0:T(1024)} %param.19) | copy-start | bytes 9220
  70.4 32.0 %copy-start.2 = (bf16[64,128]{1,0:T(8,128)(2,1)S(1)}, bf16[64,128]{1,0:T(8,128)(2,1)}, u32[]{:S(2)}) copy-start(bf16[64,128]{1,0:T(8,128)(2,1)} %param.24) | copy-start | bytes 49156
  70.4 86.9 %copy-start = (bf16[48,1024]{1,0:T(8,128)(2,1)S(1)}, bf16[48,1024]{1,0:T(8,128)(2,1)}, u32[]{:S(2)}) copy-start(bf16[48,1024]{1,0:T(8,128)(2,1)} %param.15) | copy-start | bytes 294916
  70.9 88.6 %copy-start.5 = (f32[1024]{0:T(1024)S(1)}, f32[1024]{0:T(1024)}, u32[]{:S(2)}) copy-start(f32[1024]{0:T(1024)} %param.27) | copy-start | bytes 12292
  71.0 88.6 %copy-start.6 = (f32[1024]{0:T(1024)S(1)}, f32[1024]{0:T(1024)}, u32[]{:S(2)}) copy-start(f32[1024]{0:T(1024)} %param.26) | copy-start | bytes 12292
  89.3 171.5 %reduce-scatter.4.cloned.1.call-start = ((), (), s32[]{:S(2)}) async-start(), calls=%async_computation.3 | async-start | bytes 208896
  119.7 66.0 %copy-start.3 = (bf16[128,64]{0,1:T(8,128)(2,1)S(1)}, bf16[128,64]{0,1:T(8,128)(2,1)}, u32[]{:S(2)}) copy-start(bf16[128,64]{0,1:T(8,128)(2,1)} %param.25) | copy-start | bytes 49156
  179.6 145.0 %copy-start.7 = (f32[1024]{0:T(1024)S(1)}, f32[1024]{0:T(1024)}, u32[]{:S(2)}) copy-start(f32[1024]{0:T(1024)} %param.29) | copy-start | bytes 12292
  179.6 145.0 %copy-start.8 = (f32[1024]{0:T(1024)S(1)}, f32[1024]{0:T(1024)}, u32[]{:S(2)}) copy-start(f32[1024]{0:T(1024)} %param.28) | copy-start | bytes 12292
  185.7 136.7 %all-reduce.6.cloned.1.call-start = ((), (), s32[]{:S(2)}) async-start(), calls=%async_computation.2 | async-start | bytes 393216 | tf_op jit(solution)/shard_map/psum | solution.py:17
Sparse Core Ops, SparseCore 0:
  89.4 67.8 all-reduce.3
  185.8 74.9 reduce-scatter.3
  263.1 59.2 all-reduce.5
where the time goes:
time: 336 us; the launch traced here: 333 us
  waiting for transfers between devices  154 us (46%)
  blocking collectives  92.7 us (28%)
  local copies, waits for them, and re-layouts  40.5 us (12%)
  matrix products  19.4 us (6%)
  between operations  14.1 us (4%)
  other arithmetic  11.8 us (4%)
    psum x2, waiting for transfers between devices, head_total(): return lax.psum(partial_value, 'head')  96.9 us
    unnamed x4, waiting for transfers between devices  57.2 us
    unnamed x23, local copies, waits for them, and re-layouts  38.4 us
    all_gather x1, blocking collectives, on_device(): lax.all_gather(w_self_in, 'req', axis=0, tiled=True)  21.3 us
    all_gather x1, blocking collectives, group_attention(): every_query = lax.all_gather(cross_query, 'req', axis=0, tiled=True)  18.8 us
    all_gather x1, blocking collectives, on_device(): lax.all_gather(w_cross_out, 'req', axis=1, tiled=True)  17.9 us
    all_gather x1, blocking collectives, on_device(): lax.all_gather(w_cross_q, 'req', axis=0, tiled=True)  17.3 us
    all_gather x1, blocking collectives, on_device(): lax.all_gather(w_self_out, 'req', axis=1, tiled=True)  17.3 us
  transfers between devices with their start and end apart: 3, of which 3 were waited for; matrix products, arithmetic and copies ran while one was open for 4% of the time, Pallas kernels for 0%

commit v1 on v0

--- a/solution.py
+++ b/solution.py
@@ -14,7 +14,18 @@
 
 
 def head_total(partial_value):
-    return lax.psum(partial_value, "head")
+    parts = lax.psum(1, "head")
+    rows, cols = partial_value.shape
+    pieces = lax.all_to_all(partial_value, "head", 1, 0, tiled=True)
+    reduced = jnp.sum(pieces.reshape(parts, rows, cols // parts), axis=0)
+    spread = jnp.tile(reduced, (parts, 1))
+    return lax.all_to_all(spread, "head", 0, 1, tiled=True)
+
+
+def gather_rows(block, axis_name):
+    parts = lax.psum(1, axis_name)
+    spread = jnp.tile(block, (parts,) + (1,) * (block.ndim - 1))
+    return lax.all_to_all(spread, axis_name, 0, 0, tiled=True)
 
 
 def paged_attention(query, new_key, new_value, cache_len, page_table, page_live, kv_pool, scale):
@@ -80,7 +91,7 @@
 def group_attention(cross_query, group_of, enc_kv, scale):
     groups_here, positions, _, head_cols = enc_kv.shape
     heads_here = head_cols // HEAD_DIM
-    every_query = lax.all_gather(cross_query, "req", axis=0, tiled=True)
+    every_query = gather_rows(cross_query, "req")
     local_groups = lax.axis_index("req") * groups_here + jnp.arange(groups_here, dtype=jnp.int32)
     member = group_of[None, :] == local_groups[:, None]
     member_rank = jnp.cumsum(member.astype(jnp.int32), axis=1) - 1
@@ -110,7 +121,10 @@
         (summed / total[:, :, :, None]).astype(jnp.bfloat16).reshape(groups_here, GMAX, head_cols)
     )
     placed = jnp.einsum("gkr,gkc->rc", picker, context, preferred_element_type=jnp.float32)
-    return lax.psum_scatter(placed.astype(jnp.bfloat16), "req", scatter_dimension=0, tiled=True)
+    parts = lax.psum(1, "req")
+    returned = lax.all_to_all(placed.astype(jnp.bfloat16), "req", 0, 0, tiled=True)
+    returned = returned.reshape(parts, returned.shape[0] // parts, head_cols)
+    return jnp.sum(returned.astype(jnp.float32), axis=0).astype(jnp.bfloat16)
 
 
 def on_device(
@@ -134,11 +148,35 @@
     width = tokens.shape[1]
     head_cols = kv_pool.shape[3]
     scale = HEAD_DIM ** (-0.5)
-    full_in, full_out, full_query, full_cross = (
-        lax.all_gather(w_self_in, "req", axis=0, tiled=True),
-        lax.all_gather(w_self_out, "req", axis=1, tiled=True),
-        lax.all_gather(w_cross_q, "req", axis=0, tiled=True),
-        lax.all_gather(w_cross_out, "req", axis=1, tiled=True),
+    req_parts = lax.psum(1, "req")
+    in_rows = w_self_in.shape[0]
+    out_rows, out_cols = w_self_out.shape
+    packed = jnp.concatenate(
+        [
+            w_self_in.reshape(1, -1),
+            w_cross_q.reshape(1, -1),
+            w_self_out.reshape(1, -1),
+            w_cross_out.reshape(1, -1),
+        ],
+        axis=1,
+    )
+    gathered = gather_rows(packed, "req")
+    cut_a = w_self_in.size
+    cut_b = cut_a + w_cross_q.size
+    cut_c = cut_b + w_self_out.size
+    full_in = gathered[:, :cut_a].reshape(req_parts * in_rows, 3, head_cols)
+    full_query = gathered[:, cut_a:cut_b].reshape(req_parts * in_rows, head_cols)
+    full_out = (
+        gathered[:, cut_b:cut_c]
+        .reshape(req_parts, out_rows, out_cols)
+        .transpose(1, 0, 2)
+        .reshape(out_rows, req_parts * out_cols)
+    )
+    full_cross = (
+        gathered[:, cut_c:]
+        .reshape(req_parts, out_rows, out_cols)
+        .transpose(1, 0, 2)
+        .reshape(out_rows, req_parts * out_cols)
     )
     projected = jnp.dot(
         tokens, full_in.reshape(width, 3 * head_cols), preferred_element_type=jnp.float32

time: 336 us -> 169 us (0.50)
  waiting for transfers between devices: 154 us -> 23.6 us
  blocking collectives: 92.7 us -> 12.5 us
  starting transfers between devices: 0.12 us -> 32.8 us
  local copies, waits for them, and re-layouts: 40.5 us -> 64 us
  between operations: 14.1 us -> 1.08 us
  other arithmetic: 11.8 us -> 17.1 us
  matrix products: 19.4 us -> 15.5 us
    psum x2 -> x0, waiting for transfers between devices: 96.9 us -> none  [head_total(): return lax.psum(partial_value, 'head')]
    all_gather x5 -> x0, blocking collectives: 92.7 us -> none  [the longest x1 21.3 us: on_device(): lax.all_gather(w_self_in, 'req', axis=0, tiled=True)]
    unnamed x4 -> x0, waiting for transfers between devices: 57.2 us -> none
    all_to_all x0 -> x6, starting transfers between devices: none -> 32.8 us  [the longest x2 15.4 us: gather_rows(): return lax.all_to_all(spread, axis_name, 0, 0, tiled=True)]
    all_to_all x0 -> x6, waiting for transfers between devices: none -> 23.6 us  [the longest x2 7.61 us: gather_rows(): return lax.all_to_all(spread, axis_name, 0, 0, tiled=True)]
    unnamed x23 -> x36, local copies, waits for them, and re-layouts: 38.4 us -> 54.8 us
    all_to_all x0 -> x1, blocking collectives: none -> 12.5 us  [head_total(): pieces = lax.all_to_all(partial_value, 'head', 1, 0, tiled=True)]
    another operation x2 -> x3, other arithmetic: 1.31 us -> 12.9 us  [the longest x1 11.6 us: gather_rows(): spread = jnp.tile(block, (parts,) + (1,) * (block.ndim - 1))]
  transfers between devices with their start and end apart: 3 -> 6, of which waited for: 3 -> 4; matrix products, arithmetic and copies ran while one was open for 4% -> 25% of each run, Pallas kernels for 0% -> 0%
where the time goes in v1:
time: 169 us; the launch traced here: 167 us
  local copies, waits for them, and re-layouts  64 us (38%)
  starting transfers between devices  32.8 us (19%)
  waiting for transfers between devices  23.6 us (14%)
  other arithmetic  17.1 us (10%)
  matrix products  15.5 us (9%)
  blocking collectives  12.5 us (7%)
    unnamed x36, local copies, waits for them, and re-layouts  54.8 us
    all_to_all x2, starting transfers between devices, gather_rows(): return lax.all_to_all(spread, axis_name, 0, 0, tiled=True)  15.4 us
    all_to_all x1, blocking collectives, head_total(): pieces = lax.all_to_all(partial_value, 'head', 1, 0, tiled=True)  12.5 us
    another operation x1, other arithmetic, gather_rows(): spread = jnp.tile(block, (parts,) + (1,) * (block.ndim - 1))  11.6 us
    all_to_all x2, starting transfers between devices, head_total(): return lax.all_to_all(spread, 'head', 0, 1, tiled=True)  8.49 us
    all_to_all x2, waiting for transfers between devices, gather_rows(): return lax.all_to_all(spread, axis_name, 0, 0, tiled=True)  7.61 us
    all_to_all x1, waiting for transfers between devices, group_attention(): lax.all_to_all(placed.astype(jnp.bfloat16), 'req', 0, 0, tiled=True)  6.45 us
    all_to_all x1, starting transfers between devices, head_total(): pieces = lax.all_to_all(partial_value, 'head', 1, 0, tiled=True)  5.42 us
  transfers between devices with their start and end apart: 6, of which 4 were waited for; matrix products, arithmetic and copies ran while one was open for 25% of the time, Pallas kernels for 0%

profile of v1, /device:TPU:1, one launch (start us, length us, event | category | flops | bytes accessed | tf_op | source)
XLA Modules:
  0.0 166.6 jit_solution(8493008843084266220)
XLA Ops:
  0.6 0.8 copy.86
  1.5 0.8 copy.87
  2.5 0.8 copy.88
  3.4 0.7 copy.151
  4.1 0.6 maximum_reduce_fusion
  4.7 2.4 %tile.8 = bf16[16,1,49152]{2,1,0:T(2,128)(2,1)S(1)} broadcast(bf16[49152]{0:T(1024)(128)(2,1)S(1)} %maximum_reduce_fusion), dimensions={2} | broadcast | bytes 1671168 | tf_op jit(solution)/shard_map/tile | solution.py:27
  7.1 0.5 broadcast.193
  7.7 11.6 %reduce.18 = bf16[16,49152]{1,0:T(8,128)(2,1)} reduce(bf16[16,1,49152]{2,1,0:T(2,128)(2,1)S(1)} %tile.8, bf16[]{:T(256)} %broadcast.193), dimensions={1}, to_apply=%tile.8.reduce_sub_computation | reduce | bytes 3145730 | tf_op jit(solution)/shard_map/tile | solution.py:27
  19.2 3.3 %reshape.321 = bf16[16,2,24576]{2,1,0:T(2,128)(2,1)} reshape(bf16[16,49152]{1,0:T(8,128)(2,1)} %reduce.18) | data formatting | bytes 3145728
  22.5 8.5 %all-to-all-start = ((bf16[16,2,24576]{2,1,0:T(2,128)(2,1)}), bf16[16,2,24576]{2,1,0:T(2,128)(2,1)}, u32[]{:S(2)}, u32[]{:S(2)}) async-start(bf16[16,2,24576]{2,1,0:T(2,128)(2,1)} %reshape.321), calls=%async_computation | async-start | bytes 3145728 | tf_op jit(solution)/shard_map/all_to_all | solution.py:28
  31.2 25.6 %copy.90 = bf16[160,128,2,128]{1,3,2,0:T(8,128)(2,1)} copy(bf16[160,128,2,128]{3,2,1,0:T(2,128)(2,1)} %param.20) | data formatting | bytes 20971520 | tf_op args[5]
  56.8 0.2 fusion.16
  57.2 0.2 select_reduce_fusion.1
  57.6 8.1 %reshape.322 = bf16[16,1,49152]{2,1,0:T(2,128)(2,1)S(1)} reshape(bf16[16,2,24576]{2,1,0:T(2,128)(2,1)} %all-to-all-done) | data formatting | bytes 3145728
  65.7 1.7 %copy.150 = bf16[16,1,49152]{2,0,1:T(8,128)(2,1)S(1)} copy(bf16[16,1,49152]{2,1,0:T(2,128)(2,1)S(1)} %reshape.322) | data formatting | bytes 3145728
  67.4 1.1 copy-done.1
  68.6 0.4 reshape_reshape.3
  69.0 0.2 fusion.10
  69.9 4.0 %fusion.1 = f32[160,2,1,128]{3,2,1,0:T(1,128)S(1)} fusion(bf16[160,2,64,1]{2,3,1,0:T(2,128)(2,1)S(1)} %copy.101, bf16[160,128,2,2,64]{1,4,3,2,0:T(8,128)(2,1)} %bitcast.148), kind=kOutput, calls=%fused_computation.3 | convolution fusion | flops 5242880 | bytes 5447680 | tf_op jit(solution)/shard_map/pthd,phd->pht/dot_general | solution.py:53
  74.7 0.3 fusion.22
  75.1 5.3 %fusion = f32[160,2,1,64]{3,2,1,0:T(1,128)S(1)} fusion(bf16[160,128,2,2,64]{1,4,3,2,0:T(8,128)(2,1)} %bitcast.149, bf16[160,2,128,1]{2,0,1,3:T(8,128)(2,1)S(1)} %get-tuple-element.10), kind=kOutput, calls=%fused_computation.1 | convolution fusion | flops 5242880 | bytes 5406720 | tf_op jit(solution)/shard_map/pht,pthd->phd/dot_general | solution.py:74
  80.7 0.2 fusion.9
  81.1 0.5 reshape.287
  81.6 0.2 copy.94
  81.8 0.9 fusion.51
  82.7 5.4 %all-to-all-start.1 = ((f32[48,8,128]{2,0,1:T(8,128)}), f32[48,8,128]{2,0,1:T(8,128)S(1)}, u32[]{:S(2)}, u32[]{:S(2)}) async-start(f32[48,8,128]{2,0,1:T(8,128)} %fusion.51), calls=%async_computation.1 | async-start | bytes 393216 | tf_op jit(solution)/shard_map/all_to_all | solution.py:19
  88.2 1.1 reduce-window.6
  89.7 4.3 %all-to-all-done.1 = f32[48,8,128]{2,0,1:T(8,128)S(1)} async-done(((f32[48,8,128]{2,0,1:T(8,128)}), f32[48,8,128]{2,0,1:T(8,128)S(1)}, u32[]{:S(2)}, u32[]{:S(2)}) %all-to-all-start.1) | async-done | bytes 196640 | tf_op jit(solution)/shard_map/all_to_all | solution.py:19
  94.0 0.7 tile.9
  94.7 4.2 %all-to-all-start.2 = ((f32[8,48,128]{2,1,0:T(8,128)}), f32[8,48,128]{2,1,0:T(8,128)S(1)}, u32[]{:S(2)}, u32[]{:S(2)}) async-start(f32[8,48,128]{2,1,0:T(8,128)} %tile.9), calls=%async_computation.2 | async-start | bytes 393216 | tf_op jit(solution)/shard_map/all_to_all | solution.py:22
  99.0 11.2 %copy.96 = bf16[4,2048,2,128]{1,3,0,2:T(8,128)(2,1)} copy(bf16[4,2048,2,128]{3,2,1,0:T(2,128)(2,1)} %param.21) | data formatting | bytes 8388608 | tf_op args[6]
  111.1 0.7 tile.10
  111.8 6.9 %all-to-all-start.3 = ((bf16[16,48,128]{2,1,0:T(8,128)(2,1)}), bf16[16,48,128]{2,1,0:T(8,128)(2,1)S(1)}, u32[]{:S(2)}, u32[]{:S(2)}) async-start(bf16[16,48,128]{2,1,0:T(8,128)(2,1)} %tile.10), calls=%async_computation.3 | async-start | bytes 393216 | tf_op jit(solution)/shard_map/all_to_all | solution.py:28
  118.7 7.6 %all-to-all-done.3 = bf16[16,48,128]{2,1,0:T(8,128)(2,1)S(1)} async-done(((bf16[16,48,128]{2,1,0:T(8,128)(2,1)}), bf16[16,48,128]{2,1,0:T(8,128)(2,1)S(1)}, u32[]{:S(2)}, u32[]{:S(2)}) %all-to-all-start.3) | async-done | bytes 196640 | tf_op jit(solution)/shard_map/all_to_all | solution.py:28
  126.6 2.2 %fusion.50 = (f32[4,16,2]{1,2,0:T(2,128)S(1)}, f32[4,16,2,2048]{3,1,2,0:T(8,128)S(1)}) fusion(bf16[4,2048,2,2,64]{1,4,3,0,2:T(8,128)(2,1)} %bitcast.150, bf16[4,16,2,64]{3,2,1,0:T(2,128)(2,1)S(1)} %reshape.291), kind=kOutput, calls=%fused_computation.99 | convolution fusion | flops 34078592 | bytes 3162624 | tf_op jit(solution)/shard_map/gehd,gkhd->gkhe/dot_general | solution.py:106
  128.8 0.3 fusion.11
  129.1 0.3 copy-done
  129.4 0.7 fusion.7
  130.3 1.0 fusion.4
  131.2 3.5 %all-to-all-start.4 = ((bf16[16,48,128]{2,1,0:T(8,128)(2,1)}), bf16[16,48,128]{2,1,0:T(8,128)(2,1)S(1)}, u32[]{:S(2)}, u32[]{:S(2)}) async-start(bf16[16,48,128]{2,1,0:T(8,128)(2,1)} %bitcast.27), calls=%async_computation.4 | async-start | bytes 393216 | tf_op jit(solution)/shard_map/all_to_all | solution.py:125
  134.8 0.5 reshape.294
  135.5 6.4 %all-to-all-done.4 = bf16[16,48,128]{2,1,0:T(8,128)(2,1)S(1)} async-done(((bf16[16,48,128]{2,1,0:T(8,128)(2,1)}), bf16[16,48,128]{2,1,0:T(8,128)(2,1)S(1)}, u32[]{:S(2)}, u32[]{:S(2)}) %all-to-all-start.4) | async-done | bytes 196640 | tf_op jit(solution)/shard_map/all_to_all | solution.py:125
  142.2 12.5 %all_to_all.79 = f32[48,8,128]{2,0,1:T(8,128)S(1)} all-to-all(f32[48,8,128]{2,0,1:T(8,128)S(1)} %fusion.41), channel_id=1, replica_groups=mesh['req'=16,'head'=8] {'head'}, dimensions={1} | all-to-all | bytes 393216 | tf_op jit(solution)/shard_map/all_to_all | solution.py:19
  154.7 0.7 tile.11
  155.4 4.2 %all-to-all-start.6 = ((f32[8,48,128]{2,1,0:T(8,128)}), f32[8,48,128]{2,1,0:T(8,128)S(1)}, u32[]{:S(2)}, u32[]{:S(2)}) async-start(f32[8,48,128]{2,1,0:T(8,128)} %tile.11), calls=%async_computation.6 | async-start | bytes 393216 | tf_op jit(solution)/shard_map/all_to_all | solution.py:22
  159.7 0.6 slice.68
  160.3 5.2 %all-to-all-done.6 = f32[8,48,128]{2,1,0:T(8,128)S(1)} async-done(((f32[8,48,128]{2,1,0:T(8,128)}), f32[8,48,128]{2,1,0:T(8,128)S(1)}, u32[]{:S(2)}, u32[]{:S(2)}) %all-to-all-start.6) | async-done | bytes 196640 | tf_op jit(solution)/shard_map/all_to_all | solution.py:22
  165.9 0.7 add_convert_fusion
  (83 shorter events, 5.3 us)
Async XLA Ops:
  19.2 11.8 %copy-start.9 = (s32[48,8]{0,1:T(8,128)S(1)}, s32[48,8]{0,1:T(8,128)}, u32[]{:S(2)}) copy-start(s32[48,8]{0,1:T(8,128)} %param.17) | copy-start | bytes 4612
  19.2 11.9 %copy-start.10 = (s32[48,8]{0,1:T(8,128)S(1)}, s32[48,8]{0,1:T(8,128)}, u32[]{:S(2)}) copy-start(s32[48,8]{0,1:T(8,128)} %param.18) | copy-start | bytes 4612
  22.5 35.0 %all-to-all-start = ((bf16[16,2,24576]{2,1,0:T(2,128)(2,1)}), bf16[16,2,24576]{2,1,0:T(2,128)(2,1)}, u32[]{:S(2)}, u32[]{:S(2)}) async-start(bf16[16,2,24576]{2,1,0:T(2,128)(2,1)} %reshape.321), calls=%async_computation | async-start | bytes 3145728 | tf_op jit(solution)/shard_map/all_to_all | solution.py:28
  31.2 25.6 %copy-start.11 = (s32[48]{0:T(128)S(1)}, s32[48]{0:T(128)}, u32[]{:S(2)}) copy-start(s32[48]{0:T(128)} %param.16) | copy-start | bytes 580
  65.7 3.3 %copy-start.3 = (bf16[48,1024]{1,0:T(8,128)(2,1)S(1)}, bf16[48,1024]{1,0:T(8,128)(2,1)}, u32[]{:S(2)}) copy-start(bf16[48,1024]{1,0:T(8,128)(2,1)} %param.15) | copy-start | bytes 294916
  67.4 1.1 copy-start.1
  68.6 6.0 %copy-start.2 = (bf16[16,1,49152]{2,0,1:T(8,128)(2,1)S(1)}, bf16[16,1,49152]{2,0,1:T(8,128)(2,1)}, u32[]{:S(2)}) copy-start(bf16[16,1,49152]{2,0,1:T(8,128)(2,1)} %copy-done.1) | copy-start | bytes 4718596
  75.1 13.0 %copy-start.4 = (s32[768]{0:T(1024)S(1)}, s32[768]{0:T(1024)}, u32[]{:S(2)}) copy-start(s32[768]{0:T(1024)} %param.19) | copy-start | bytes 9220
  82.7 11.3 %all-to-all-start.1 = ((f32[48,8,128]{2,0,1:T(8,128)}), f32[48,8,128]{2,0,1:T(8,128)S(1)}, u32[]{:S(2)}, u32[]{:S(2)}) async-start(f32[48,8,128]{2,0,1:T(8,128)} %fusion.51), calls=%async_computation.1 | async-start | bytes 393216 | tf_op jit(solution)/shard_map/all_to_all | solution.py:19
  94.7 15.7 %all-to-all-start.2 = ((f32[8,48,128]{2,1,0:T(8,128)}), f32[8,48,128]{2,1,0:T(8,128)S(1)}, u32[]{:S(2)}, u32[]{:S(2)}) async-start(f32[8,48,128]{2,1,0:T(8,128)} %tile.9), calls=%async_computation.2 | async-start | bytes 393216 | tf_op jit(solution)/shard_map/all_to_all | solution.py:22
  99.0 11.7 %copy-start.5 = (f32[1024]{0:T(1024)S(1)}, f32[1024]{0:T(1024)}, u32[]{:S(2)}) copy-start(f32[1024]{0:T(1024)} %param.27) | copy-start | bytes 12292
  99.0 11.7 %copy-start.6 = (f32[1024]{0:T(1024)S(1)}, f32[1024]{0:T(1024)}, u32[]{:S(2)}) copy-start(f32[1024]{0:T(1024)} %param.26) | copy-start | bytes 12292
  111.8 14.6 %all-to-all-start.3 = ((bf16[16,48,128]{2,1,0:T(8,128)(2,1)}), bf16[16,48,128]{2,1,0:T(8,128)(2,1)S(1)}, u32[]{:S(2)}, u32[]{:S(2)}) async-start(bf16[16,48,128]{2,1,0:T(8,128)(2,1)} %tile.10), calls=%async_computation.3 | async-start | bytes 393216 | tf_op jit(solution)/shard_map/all_to_all | solution.py:28
  126.6 2.8 %copy-start = (bf16[4,2048,2,128]{1,3,0,2:T(8,128)(2,1)S(1)}, bf16[4,2048,2,128]{1,3,0,2:T(8,128)(2,1)}, u32[]{:S(2)}) copy-start(bf16[4,2048,2,128]{1,3,0,2:T(8,128)(2,1)} %copy.96) | copy-start | bytes 12582916
  129.4 36.5 %copy-start.7 = (f32[1024]{0:T(1024)S(1)}, f32[1024]{0:T(1024)}, u32[]{:S(2)}) copy-start(f32[1024]{0:T(1024)} %param.29) | copy-start | bytes 12292
  129.4 36.5 %copy-start.8 = (f32[1024]{0:T(1024)S(1)}, f32[1024]{0:T(1024)}, u32[]{:S(2)}) copy-start(f32[1024]{0:T(1024)} %param.28) | copy-start | bytes 12292
  131.2 10.7 %all-to-all-start.4 = ((bf16[16,48,128]{2,1,0:T(8,128)(2,1)}), bf16[16,48,128]{2,1,0:T(8,128)(2,1)S(1)}, u32[]{:S(2)}, u32[]{:S(2)}) async-start(bf16[16,48,128]{2,1,0:T(8,128)(2,1)} %bitcast.27), calls=%async_computation.4 | async-start | bytes 393216 | tf_op jit(solution)/shard_map/all_to_all | solution.py:125
  155.4 10.1 %all-to-all-start.6 = ((f32[8,48,128]{2,1,0:T(8,128)}), f32[8,48,128]{2,1,0:T(8,128)S(1)}, u32[]{:S(2)}, u32[]{:S(2)}) async-start(f32[8,48,128]{2,1,0:T(8,128)} %tile.11), calls=%async_computation.6 | async-start | bytes 393216 | tf_op jit(solution)/shard_map/all_to_all | solution.py:22

commit v2 on v0

--- a/solution.py
+++ b/solution.py
@@ -14,7 +14,30 @@
 
 
 def head_total(partial_value):
-    return lax.psum(partial_value, "head")
+    parts = lax.psum(1, "head")
+    rows, cols = partial_value.shape
+    pieces = lax.all_to_all(partial_value, "head", 1, 0, tiled=True)
+    reduced = jnp.sum(pieces.reshape(parts, rows, cols // parts), axis=0)
+    spread = jnp.tile(reduced, (parts, 1))
+    return lax.all_to_all(spread, "head", 0, 1, tiled=True)
+
+
+def gather_rows(block, axis_name):
+    parts = lax.psum(1, axis_name)
+    spread = jnp.tile(block, (parts,) + (1,) * (block.ndim - 1))
+    return lax.all_to_all(spread, axis_name, 0, 0, tiled=True)
+
+
+def head_blocks(query_rows, head_cols):
+    heads_here = head_cols // HEAD_DIM
+    lane_head = jnp.arange(head_cols, dtype=jnp.int32) // HEAD_DIM
+    mask = lane_head[None, :] == jnp.arange(heads_here, dtype=jnp.int32)[:, None]
+    return jnp.where(mask, query_rows[..., None, :], jnp.zeros((), query_rows.dtype)), mask
+
+
+def shift_to_values(weights):
+    zero = jnp.zeros(weights.shape[:-1] + (1,), weights.dtype)
+    return jnp.concatenate([zero, weights[..., :-1]], axis=-1)
 
 
 def paged_attention(query, new_key, new_value, cache_len, page_table, page_live, kv_pool, scale):
@@ -32,14 +55,16 @@
     page_slot = jnp.sum(jnp.where(hits, slot_index[None, :, None], 0), axis=(0, 1))
     page_flag = jnp.sum(jnp.where(hits, page_live[:, :, None], 0), axis=(0, 1))
     page_length = jnp.sum(jnp.where(owners, cache_len[:, None], 0), axis=0)
-    offsets = page_slot[:, None] * page_rows + jnp.arange(page_rows, dtype=jnp.int32)[None, :]
-    counted = (page_flag[:, None] == 1) & (offsets < page_length[:, None])
+    lane = jnp.arange(2 * page_rows, dtype=jnp.int32)
+    offsets = page_slot[:, None] * page_rows + (lane // 2)[None, :]
+    counted = (page_flag[:, None] == 1) & (offsets < page_length[:, None]) & (lane % 2 == 0)[None, :]
     owner_weights = owners.astype(jnp.float32)
     page_query = jnp.dot(owners.T.astype(jnp.bfloat16), query, preferred_element_type=jnp.float32)
-    page_query = page_query.astype(jnp.bfloat16).reshape(pages_here, heads_here, HEAD_DIM)
-    stored = kv_pool.reshape(pages_here, page_rows, 2, heads_here, HEAD_DIM)
+    page_query = page_query.astype(jnp.bfloat16)
+    query_blocks, head_mask = head_blocks(page_query, head_cols)
+    stored = kv_pool.reshape(pages_here, 2 * page_rows, head_cols)
     scores = (
-        jnp.einsum("pthd,phd->pht", stored[:, :, 0], page_query, preferred_element_type=jnp.float32)
+        jnp.einsum("phc,pnc->phn", query_blocks, stored, preferred_element_type=jnp.float32)
         * scale
     )
     scores = jnp.where(counted[:, None, :], scores, -1e30)
@@ -60,15 +85,12 @@
         jnp.dot(owner_weights, jnp.sum(weights, axis=2), precision=lax.Precision.HIGHEST)
         + new_weight
     )
+    value_weights = shift_to_values(weights.astype(jnp.bfloat16))
     page_sum = jnp.einsum(
-        "pht,pthd->phd",
-        weights.astype(jnp.bfloat16),
-        stored[:, :, 1],
-        preferred_element_type=jnp.float32,
-    )
-    summed = jnp.dot(
-        owner_weights, page_sum.reshape(pages_here, head_cols), precision=lax.Precision.HIGHEST
-    )
+        "phn,pnc->phc", value_weights, stored, preferred_element_type=jnp.float32
+    )
+    page_sum = jnp.sum(jnp.where(head_mask[None], page_sum, 0.0), axis=1)
+    summed = jnp.dot(owner_weights, page_sum, precision=lax.Precision.HIGHEST)
     rounded_new = lax.optimization_barrier(new_weight.astype(jnp.bfloat16)).astype(jnp.float32)
     own_term = rounded_new[:, :, None] * new_value.astype(jnp.float32).reshape(
         rows_here, heads_here, HEAD_DIM
@@ -80,7 +102,7 @@
 def group_attention(cross_query, group_of, enc_kv, scale):
     groups_here, positions, _, head_cols = enc_kv.shape
     heads_here = head_cols // HEAD_DIM
-    every_query = lax.all_gather(cross_query, "req", axis=0, tiled=True)
+    every_query = gather_rows(cross_query, "req")
     local_groups = lax.axis_index("req") * groups_here + jnp.arange(groups_here, dtype=jnp.int32)
     member = group_of[None, :] == local_groups[:, None]
     member_rank = jnp.cumsum(member.astype(jnp.int32), axis=1) - 1
@@ -89,28 +111,31 @@
     )
     picker = picker.astype(jnp.bfloat16)
     group_query = jnp.einsum("gkr,rc->gkc", picker, every_query, preferred_element_type=jnp.float32)
-    group_query = group_query.astype(jnp.bfloat16).reshape(groups_here, GMAX, heads_here, HEAD_DIM)
-    stored = enc_kv.reshape(groups_here, positions, 2, heads_here, HEAD_DIM)
+    group_query = group_query.astype(jnp.bfloat16)
+    query_blocks, head_mask = head_blocks(group_query, head_cols)
+    query_blocks = query_blocks.reshape(groups_here, GMAX * heads_here, head_cols)
+    stored = enc_kv.reshape(groups_here, 2 * positions, head_cols)
+    lane = jnp.arange(2 * positions, dtype=jnp.int32)
+    is_key = (lane % 2 == 0)[None, None, :]
     scores = (
-        jnp.einsum(
-            "gehd,gkhd->gkhe", stored[:, :, 0], group_query, preferred_element_type=jnp.float32
-        )
+        jnp.einsum("gmc,gnc->gmn", query_blocks, stored, preferred_element_type=jnp.float32)
         * scale
     )
-    top = jnp.max(scores, axis=3)
-    weights = jnp.exp(scores - top[:, :, :, None])
-    total = jnp.sum(weights, axis=3)
+    scores = jnp.where(is_key, scores, -1e30)
+    top = jnp.max(scores, axis=2)
+    weights = jnp.where(is_key, jnp.exp(scores - top[:, :, None]), 0.0)
+    total = jnp.sum(weights, axis=2)
+    value_weights = shift_to_values(weights.astype(jnp.bfloat16))
     summed = jnp.einsum(
-        "gkhe,gehd->gkhd",
-        weights.astype(jnp.bfloat16),
-        stored[:, :, 1],
-        preferred_element_type=jnp.float32,
-    )
-    context = (
-        (summed / total[:, :, :, None]).astype(jnp.bfloat16).reshape(groups_here, GMAX, head_cols)
-    )
+        "gmn,gnc->gmc", value_weights, stored, preferred_element_type=jnp.float32
+    )
+    summed = (summed / total[:, :, None]).reshape(groups_here, GMAX, heads_here, head_cols)
+    context = jnp.sum(jnp.where(head_mask[None, None], summed, 0.0), axis=2).astype(jnp.bfloat16)
     placed = jnp.einsum("gkr,gkc->rc", picker, context, preferred_element_type=jnp.float32)
-    return lax.psum_scatter(placed.astype(jnp.bfloat16), "req", scatter_dimension=0, tiled=True)
+    parts = lax.psum(1, "req")
+    returned = lax.all_to_all(placed.astype(jnp.bfloat16), "req", 0, 0, tiled=True)
+    returned = returned.reshape(parts, returned.shape[0] // parts, head_cols)
+    return jnp.sum(returned.astype(jnp.float32), axis=0).astype(jnp.bfloat16)
 
 
 def on_device(
@@ -134,27 +159,33 @@
     width = tokens.shape[1]
     head_cols = kv_pool.shape[3]
     scale = HEAD_DIM ** (-0.5)
-    full_in, full_out, full_query, full_cross = (
-        lax.all_gather(w_self_in, "req", axis=0, tiled=True),
-        lax.all_gather(w_self_out, "req", axis=1, tiled=True),
-        lax.all_gather(w_cross_q, "req", axis=0, tiled=True),
-        lax.all_gather(w_cross_out, "req", axis=1, tiled=True),
-    )
-    projected = jnp.dot(
-        tokens, full_in.reshape(width, 3 * head_cols), preferred_element_type=jnp.float32
-    )
-    qkv = projected.astype(jnp.bfloat16).reshape(rows_here, 3, head_cols)
+    in_rows = w_self_in.shape[0]
+    first = gather_rows(w_self_in.transpose(1, 0, 2).reshape(-1, head_cols)[None], "req")
+    rest = jnp.concatenate([w_cross_q, w_self_out.T, w_cross_out.T], axis=0)
+    rest = gather_rows(rest[None], "req")
+    full_in = [first[:, k * in_rows : (k + 1) * in_rows].reshape(-1, head_cols) for k in range(3)]
+    full_query = rest[:, :in_rows].reshape(-1, head_cols)
+    full_out = rest[:, in_rows : 2 * in_rows].reshape(-1, head_cols)
+    full_cross = rest[:, 2 * in_rows :].reshape(-1, head_cols)
+    contract_cols = (((1,), (1,)), ((), ()))
+    qkv = jnp.stack(
+        [jnp.dot(tokens, part, preferred_element_type=jnp.float32) for part in full_in], axis=1
+    ).astype(jnp.bfloat16)
     self_ctx = paged_attention(
         qkv[:, 0], qkv[:, 1], qkv[:, 2], cache_len, page_table, page_live, kv_pool, scale
     )
-    self_proj = head_total(jnp.dot(self_ctx, full_out, preferred_element_type=jnp.float32))
+    self_proj = head_total(
+        lax.dot_general(self_ctx, full_out, contract_cols, preferred_element_type=jnp.float32)
+    )
     h_first = layer_norm(tokens.astype(jnp.float32) + self_proj, self_gain, self_bias).astype(
         jnp.bfloat16
     )
     cross_query = jnp.dot(h_first, full_query, preferred_element_type=jnp.float32)
     cross_query = cross_query.astype(jnp.bfloat16)
     cross_ctx = group_attention(cross_query, group_of, enc_kv, scale)
-    cross_proj = head_total(jnp.dot(cross_ctx, full_cross, preferred_element_type=jnp.float32))
+    cross_proj = head_total(
+        lax.dot_general(cross_ctx, full_cross, contract_cols, preferred_element_type=jnp.float32)
+    )
     hidden_out = layer_norm(
         h_first.astype(jnp.float32) + cross_proj, cross_gain, cross_bias
     ).astype(jnp.bfloat16)

time: 336 us -> 127 us (0.38)
  waiting for transfers between devices: 154 us -> 31.2 us
  blocking collectives: 92.7 us -> 21.9 us
  starting transfers between devices: 0.12 us -> 34.1 us
  local copies, waits for them, and re-layouts: 40.5 us -> 8.08 us
  between operations: 14.1 us -> 0.99 us
  other arithmetic: 11.8 us -> 6.91 us
    psum x2 -> x0, waiting for transfers between devices: 96.9 us -> none  [head_total(): return lax.psum(partial_value, 'head')]
    all_gather x5 -> x0, blocking collectives: 92.7 us -> none  [the longest x1 21.3 us: on_device(): lax.all_gather(w_self_in, 'req', axis=0, tiled=True)]
    unnamed x4 -> x0, waiting for transfers between devices: 57.2 us -> none
    unnamed x23 -> x16, local copies, waits for them, and re-layouts: 38.4 us -> 2.2 us
    all_to_all x0 -> x6, starting transfers between devices: none -> 34.1 us  [the longest x3 19 us: gather_rows(): return lax.all_to_all(spread, axis_name, 0, 0, tiled=True)]
    all_to_all x0 -> x6, waiting for transfers between devices: none -> 31.2 us  [the longest x3 15.9 us: gather_rows(): return lax.all_to_all(spread, axis_name, 0, 0, tiled=True)]
    all_to_all x0 -> x2, blocking collectives: none -> 21.9 us  [the longest x1 11.7 us: head_total(): pieces = lax.all_to_all(partial_value, 'head', 1, 0, tiled=True)]
    another operation x0 -> x5, local copies, waits for them, and re-layouts: none -> 4.96 us  [the longest x3 3.59 us: gather_rows(): spread = jnp.tile(block, (parts,) + (1,) * (block.ndim - 1))]
  transfers between devices with their start and end apart: 3 -> 6, of which waited for: 3 -> 5; matrix products, arithmetic and copies ran while one was open for 4% -> 18% of each run, Pallas kernels for 0% -> 0%
where the time goes in v2:
time: 127 us; the launch traced here: 126 us
  starting transfers between devices  34.1 us (27%)
  waiting for transfers between devices  31.2 us (25%)
  matrix products  22.6 us (18%)
  blocking collectives  21.9 us (17%)
  local copies, waits for them, and re-layouts  8.08 us (6%)
  other arithmetic  6.91 us (5%)
    all_to_all x3, starting transfers between devices, gather_rows(): return lax.all_to_all(spread, axis_name, 0, 0, tiled=True)  19 us
    all_to_all x3, waiting for transfers between devices, gather_rows(): return lax.all_to_all(spread, axis_name, 0, 0, tiled=True)  15.9 us
    all_to_all x1, blocking collectives, head_total(): pieces = lax.all_to_all(partial_value, 'head', 1, 0, tiled=True)  11.7 us
    all_to_all x2, waiting for transfers between devices, head_total(): return lax.all_to_all(spread, 'head', 0, 1, tiled=True)  11 us
    all_to_all x1, blocking collectives, group_attention(): lax.all_to_all(placed.astype(jnp.bfloat16), 'req', 0, 0, tiled=True)  10.2 us
    all_to_all x2, starting transfers between devices, head_total(): return lax.all_to_all(spread, 'head', 0, 1, tiled=True)  8.49 us
    dot_general x1, matrix products, paged_attention(): jnp.einsum('phc,pnc->phn', query_blocks, stored, preferred_element_type=j...  6.88 us
    all_to_all x1, starting transfers between devices, head_total(): pieces = lax.all_to_all(partial_value, 'head', 1, 0, tiled=True)  6.62 us
  transfers between devices with their start and end apart: 6, of which 5 were waited for; matrix products, arithmetic and copies ran while one was open for 18% of the time, Pallas kernels for 0%

profile of v2, /device:TPU:1, one launch (start us, length us, event | category | flops | bytes accessed | tf_op | source)
XLA Modules:
  0.0 125.7 jit_solution(11746890876373769785)
XLA Ops:
  0.6 1.9 %tile.13 = bf16[16,192,128]{2,1,0:T(8,128)(2,1)} broadcast(bf16[192,128]{1,0:T(8,128)(2,1)} %bitcast.120), dimensions={1,2} | broadcast | bytes 835584 | tf_op jit(solution)/shard_map/tile | solution.py:27
  2.5 8.4 %all-to-all-start = ((bf16[16,192,128]{2,1,0:T(8,128)(2,1)}), bf16[16,192,128]{2,1,0:T(8,128)(2,1)S(1)}, u32[]{:S(2)}, u32[]{:S(2)}) async-start(bf16[16,192,128]{2,1,0:T(8,128)(2,1)} %tile.13), calls=%async_computation | async-start | bytes 1572864 | tf_op jit(solution)/shard_map/all_to_all | solution.py:28
  11.0 0.8 copy.56
  11.7 0.7 and_select_fusion.3
  12.5 0.2 fusion.13
  12.7 0.7 select_reduce_fusion.4
  13.5 0.8 copy.57
  14.2 0.2 select_reduce_fusion.1
  14.5 0.8 pad_maximum_fusion
  15.4 8.8 %all-to-all-done = bf16[16,192,128]{2,1,0:T(8,128)(2,1)S(1)} async-done(((bf16[16,192,128]{2,1,0:T(8,128)(2,1)}), bf16[16,192,128]{2,1,0:T(8,128)(2,1)S(1)}, u32[]{:S(2)}, u32[]{:S(2)}) %all-to-all-start) | async-done | bytes 786464 | tf_op jit(solution)/shard_map/all_to_all | solution.py:28
  24.2 1.0 tile.14
  25.2 3.7 %all-to-all-start.1 = ((bf16[16,192,128]{2,1,0:T(8,128)(2,1)}), bf16[16,192,128]{2,1,0:T(8,128)(2,1)S(1)}, u32[]{:S(2)}, u32[]{:S(2)}) async-start(bf16[16,192,128]{2,1,0:T(8,128)(2,1)} %tile.14), calls=%async_computation.1 | async-start | bytes 1572864 | tf_op jit(solution)/shard_map/all_to_all | solution.py:28
  29.0 0.2 convolution_convert_fusion.5
  29.1 0.2 convolution_convert_fusion
  29.4 6.9 %fusion.56 = (f32[160,2]{1,0:T(8,128)S(1)}, f32[160,2,256]{2,1,0:T(2,128)S(1)}) fusion(bf16[160,256,128]{2,1,0:T(8,128)(2,1)} %bitcast.102, pred[2,128]{1,0:T(4,128)(4,1)S(1)} %iota_compare_fusion.3, bf16[160,128]{1,0:T(8,128)(2,1)S(1)} %convolution_convert_fusion, pred[160,256]{1,0:T(8,128)(4,1)S(1)} %fusion.19), kind=kOutput, calls=%fused_computation.119 | convolution fusion | flops 21257920 | bytes 10896896 | tf_op jit(solution)/shard_map/phc,pnc->phn/dot_general | solution.py:67
  36.4 0.2 convert_multiply_fusion
  36.9 0.3 fusion.31
  37.2 0.6 fusion.53
  37.8 5.5 %fusion.7 = f32[160,128]{1,0:T(8,128)S(1)} fusion(bf16[160,256,128]{2,1,0:T(8,128)(2,1)} %bitcast.103, bf16[160,2,255]{2,1,0:T(2,128)(2,1)S(1)} %bitcast.113, pred[2,128]{1,0:T(4,128)(4,1)S(1)} %iota_compare_fusion.3), kind=kOutput, calls=%fused_computation.12 | convolution fusion | flops 21032960 | bytes 10731136 | tf_op jit(solution)/shard_map/phn,pnc->phc/dot_general | solution.py:89
  43.3 0.2 convolution_convert_fusion.3
  43.7 0.2 convolution_add_fusion.1
  44.0 0.2 fusion.9
  44.4 0.9 fusion.60
  45.3 6.6 %all-to-all-start.2 = ((f32[48,8,128]{2,0,1:T(8,128)}), f32[48,8,128]{2,0,1:T(8,128)S(1)}, u32[]{:S(2)}, u32[]{:S(2)}) async-start(f32[48,8,128]{2,0,1:T(8,128)} %fusion.60), calls=%async_computation.2 | async-start | bytes 393216 | tf_op jit(solution)/shard_map/all_to_all | solution.py:19
  52.0 1.1 reduce-window.6
  53.1 0.2 slice_reduce_fusion
  53.3 0.2 reduce-window.9
  53.5 4.3 %all-to-all-done.2 = f32[48,8,128]{2,0,1:T(8,128)S(1)} async-done(((f32[48,8,128]{2,0,1:T(8,128)}), f32[48,8,128]{2,0,1:T(8,128)S(1)}, u32[]{:S(2)}, u32[]{:S(2)}) %all-to-all-start.2) | async-done | bytes 196640 | tf_op jit(solution)/shard_map/all_to_all | solution.py:19
  57.8 0.7 tile.15
  58.5 4.2 %all-to-all-start.3 = ((f32[8,48,128]{2,1,0:T(8,128)}), f32[8,48,128]{2,1,0:T(8,128)S(1)}, u32[]{:S(2)}, u32[]{:S(2)}) async-start(f32[8,48,128]{2,1,0:T(8,128)} %tile.15), calls=%async_computation.3 | async-start | bytes 393216 | tf_op jit(solution)/shard_map/all_to_all | solution.py:22
  62.8 5.8 %all-to-all-done.3 = f32[8,48,128]{2,1,0:T(8,128)S(1)} async-done(((f32[8,48,128]{2,1,0:T(8,128)}), f32[8,48,128]{2,1,0:T(8,128)S(1)}, u32[]{:S(2)}, u32[]{:S(2)}) %all-to-all-start.3) | async-done | bytes 196640 | tf_op jit(solution)/shard_map/all_to_all | solution.py:22
  68.7 0.2 multiply_reduce_fusion.1
  69.0 0.2 convolution_convert_fusion.2
  69.2 0.7 tile.16
  69.9 6.9 %all-to-all-start.4 = ((bf16[16,48,128]{2,1,0:T(8,128)(2,1)}), bf16[16,48,128]{2,1,0:T(8,128)(2,1)S(1)}, u32[]{:S(2)}, u32[]{:S(2)}) async-start(bf16[16,48,128]{2,1,0:T(8,128)(2,1)} %tile.16), calls=%async_computation.4 | async-start | bytes 393216 | tf_op jit(solution)/shard_map/all_to_all | solution.py:28
  76.9 7.2 %all-to-all-done.4 = bf16[16,48,128]{2,1,0:T(8,128)(2,1)S(1)} async-done(((bf16[16,48,128]{2,1,0:T(8,128)(2,1)}), bf16[16,48,128]{2,1,0:T(8,128)(2,1)S(1)}, u32[]{:S(2)}, u32[]{:S(2)}) %all-to-all-start.4) | async-done | bytes 196640 | tf_op jit(solution)/shard_map/all_to_all | solution.py:28
  84.2 4.0 %fusion.57 = (f32[4,32]{1,0:T(4,128)S(1)}, bf16[4,32,4096]{2,1,0:T(8,128)(2,1)S(1)}) fusion(pred[4096]{0:T(1024)(128)(4,1)S(1)} %fusion.33, bf16[4,4096,128]{2,1,0:T(8,128)(2,1)} %bitcast.104, bf16[4,32,128]{2,1,0:T(8,128)(2,1)S(1)} %bitcast.121, pred[32,128]{1,0:T(8,128)(4,1)S(1)} %broadcast_in_dim.218), kind=kOutput, calls=%fused_computation.120 | convolution fusion | flops 137383936 | bytes 5284352 | tf_op jit(solution)/shard_map/sub | solution.py:126
  88.3 3.0 %convolution_divide_fusion = f32[4,32,128]{2,1,0:T(8,128)S(1)} fusion(bf16[4,4096,128]{2,1,0:T(8,128)(2,1)} %bitcast.105, bf16[4,32,4095]{2,1,0:T(8,128)(2,1)S(1)} %bitcast.112, f32[4,32]{1,0:T(4,128)S(1)} %get-tuple-element.28), kind=kOutput, calls=%fused_computation.13 | convolution fusion | flops 134234112 | bytes 5308672 | tf_op jit(solution)/shard_map/gmn,gnc->gmc/dot_general | solution.py:129
  91.3 0.3 fusion.6
  91.6 10.2 %all_to_all.80 = bf16[16,48,128]{2,1,0:T(8,128)(2,1)S(1)} all-to-all(bf16[16,48,128]{2,1,0:T(8,128)(2,1)S(1)} %bitcast.117), channel_id=1, replica_groups=mesh['req'=16,'head'=8] {'req'}, dimensions={0} | all-to-all | bytes 393216 | tf_op jit(solution)/shard_map/all_to_all | solution.py:136
  101.9 0.2 fusion.39
  102.1 11.7 %all_to_all.81 = f32[48,8,128]{2,0,1:T(8,128)S(1)} all-to-all(f32[48,8,128]{2,0,1:T(8,128)S(1)} %fusion.39), channel_id=1, replica_groups=mesh['req'=16,'head'=8] {'head'}, dimensions={1} | all-to-all | bytes 393216 | tf_op jit(solution)/shard_map/all_to_all | solution.py:19
  113.8 0.7 tile.17
  114.5 4.2 %all-to-all-start.7 = ((f32[8,48,128]{2,1,0:T(8,128)}), f32[8,48,128]{2,1,0:T(8,128)S(1)}, u32[]{:S(2)}, u32[]{:S(2)}) async-start(f32[8,48,128]{2,1,0:T(8,128)} %tile.17), calls=%async_computation.7 | async-start | bytes 393216 | tf_op jit(solution)/shard_map/all_to_all | solution.py:22
  118.7 0.6 copy.66
  119.4 5.2 %all-to-all-done.7 = f32[8,48,128]{2,1,0:T(8,128)S(1)} async-done(((f32[8,48,128]{2,1,0:T(8,128)}), f32[8,48,128]{2,1,0:T(8,128)S(1)}, u32[]{:S(2)}, u32[]{:S(2)}) %all-to-all-start.7) | async-done | bytes 196640 | tf_op jit(solution)/shard_map/all_to_all | solution.py:22
  124.8 0.2 multiply_reduce_fusion
  125.0 0.7 add_convert_fusion
  (56 shorter events, 2.2 us)
Async XLA Ops:
  0.6 28.3 %copy-start = (bf16[48,1024]{1,0:T(8,128)(2,1)S(1)}, bf16[48,1024]{1,0:T(8,128)(2,1)}, u32[]{:S(2)}) copy-start(bf16[48,1024]{1,0:T(8,128)(2,1)} %param.15) | copy-start | bytes 294916
  2.5 21.7 %all-to-all-start = ((bf16[16,192,128]{2,1,0:T(8,128)(2,1)}), bf16[16,192,128]{2,1,0:T(8,128)(2,1)S(1)}, u32[]{:S(2)}, u32[]{:S(2)}) async-start(bf16[16,192,128]{2,1,0:T(8,128)(2,1)} %tile.13), calls=%async_computation | async-start | bytes 1572864 | tf_op jit(solution)/shard_map/all_to_all | solution.py:28
  25.2 19.1 %all-to-all-start.1 = ((bf16[16,192,128]{2,1,0:T(8,128)(2,1)}), bf16[16,192,128]{2,1,0:T(8,128)(2,1)S(1)}, u32[]{:S(2)}, u32[]{:S(2)}) async-start(bf16[16,192,128]{2,1,0:T(8,128)(2,1)} %tile.14), calls=%async_computation.1 | async-start | bytes 1572864 | tf_op jit(solution)/shard_map/all_to_all | solution.py:28
  37.8 14.1 %copy-start.1 = (s32[768]{0:T(1024)S(1)}, s32[768]{0:T(1024)}, u32[]{:S(2)}) copy-start(s32[768]{0:T(1024)} %param.19) | copy-start | bytes 9220
  43.3 25.6 %copy-start.2 = (f32[1024]{0:T(1024)S(1)}, f32[1024]{0:T(1024)}, u32[]{:S(2)}) copy-start(f32[1024]{0:T(1024)} %param.27) | copy-start | bytes 12292
  43.3 25.6 %copy-start.3 = (f32[1024]{0:T(1024)S(1)}, f32[1024]{0:T(1024)}, u32[]{:S(2)}) copy-start(f32[1024]{0:T(1024)} %param.26) | copy-start | bytes 12292
  45.3 12.5 %all-to-all-start.2 = ((f32[48,8,128]{2,0,1:T(8,128)}), f32[48,8,128]{2,0,1:T(8,128)S(1)}, u32[]{:S(2)}, u32[]{:S(2)}) async-start(f32[48,8,128]{2,0,1:T(8,128)} %fusion.60), calls=%async_computation.2 | async-start | bytes 393216 | tf_op jit(solution)/shard_map/all_to_all | solution.py:19
  58.5 10.1 %all-to-all-start.3 = ((f32[8,48,128]{2,1,0:T(8,128)}), f32[8,48,128]{2,1,0:T(8,128)S(1)}, u32[]{:S(2)}, u32[]{:S(2)}) async-start(f32[8,48,128]{2,1,0:T(8,128)} %tile.15), calls=%async_computation.3 | async-start | bytes 393216 | tf_op jit(solution)/shard_map/all_to_all | solution.py:22
  69.9 14.1 %all-to-all-start.4 = ((bf16[16,48,128]{2,1,0:T(8,128)(2,1)}), bf16[16,48,128]{2,1,0:T(8,128)(2,1)S(1)}, u32[]{:S(2)}, u32[]{:S(2)}) async-start(bf16[16,48,128]{2,1,0:T(8,128)(2,1)} %tile.16), calls=%async_computation.4 | async-start | bytes 393216 | tf_op jit(solution)/shard_map/all_to_all | solution.py:28
  88.3 36.7 %copy-start.4 = (f32[1024]{0:T(1024)S(1)}, f32[1024]{0:T(1024)}, u32[]{:S(2)}) copy-start(f32[1024]{0:T(1024)} %param.29) | copy-start | bytes 12292
  88.3 36.7 %copy-start.5 = (f32[1024]{0:T(1024)S(1)}, f32[1024]{0:T(1024)}, u32[]{:S(2)}) copy-start(f32[1024]{0:T(1024)} %param.28) | copy-start | bytes 12292
  114.5 10.1 %all-to-all-start.7 = ((f32[8,48,128]{2,1,0:T(8,128)}), f32[8,48,128]{2,1,0:T(8,128)S(1)}, u32[]{:S(2)}, u32[]{:S(2)}) async-start(f32[8,48,128]{2,1,0:T(8,128)} %tile.17), calls=%async_computation.7 | async-start | bytes 393216 | tf_op jit(solution)/shard_map/all_to_all | solution.py:22

commit v3 on v2

--- a/solution.py
+++ b/solution.py
@@ -16,8 +16,8 @@
 def head_total(partial_value):
     parts = lax.psum(1, "head")
     rows, cols = partial_value.shape
-    pieces = lax.all_to_all(partial_value, "head", 1, 0, tiled=True)
-    reduced = jnp.sum(pieces.reshape(parts, rows, cols // parts), axis=0)
+    pieces = lax.all_to_all(partial_value.astype(jnp.bfloat16), "head", 1, 0, tiled=True)
+    reduced = jnp.sum(pieces.reshape(parts, rows, cols // parts).astype(jnp.float32), axis=0)
     spread = jnp.tile(reduced, (parts, 1))
     return lax.all_to_all(spread, "head", 0, 1, tiled=True)
 
@@ -160,10 +160,16 @@
     head_cols = kv_pool.shape[3]
     scale = HEAD_DIM ** (-0.5)
     in_rows = w_self_in.shape[0]
-    first = gather_rows(w_self_in.transpose(1, 0, 2).reshape(-1, head_cols)[None], "req")
-    rest = jnp.concatenate([w_cross_q, w_self_out.T, w_cross_out.T], axis=0)
+    stacked_in = w_self_in.transpose(1, 0, 2)
+    first = gather_rows(stacked_in[0][None], "req")
+    rest = jnp.concatenate(
+        [stacked_in[1], stacked_in[2], w_cross_q, w_self_out.T, w_cross_out.T], axis=0
+    )
     rest = gather_rows(rest[None], "req")
-    full_in = [first[:, k * in_rows : (k + 1) * in_rows].reshape(-1, head_cols) for k in range(3)]
+    full_in = [first.reshape(-1, head_cols)] + [
+        rest[:, k * in_rows : (k + 1) * in_rows].reshape(-1, head_cols) for k in range(2)
+    ]
+    rest = rest[:, 2 * in_rows :]
     full_query = rest[:, :in_rows].reshape(-1, head_cols)
     full_out = rest[:, in_rows : 2 * in_rows].reshape(-1, head_cols)
     full_cross = rest[:, 2 * in_rows :].reshape(-1, head_cols)

time: 127 us -> 131 us (1.031)
  local copies, waits for them, and re-layouts: 8.08 us -> 12.3 us
    unnamed x16 -> x20, local copies, waits for them, and re-layouts: 2.2 us -> 5.1 us
    another operation x3 -> x4, local copies, waits for them, and re-layouts: 3.59 us -> 3.51 us  [gather_rows(): spread = jnp.tile(block, (parts,) + (1,) * (block.ndim - 1))]
  transfers between devices with their start and end apart: 6 -> 6, of which waited for: 5 -> 5; matrix products, arithmetic and copies ran while one was open for 18% -> 14% of each run, Pallas kernels for 0% -> 0%
where the time goes in v3:
time: 131 us; the launch traced here: 130 us
  starting transfers between devices  34.7 us (26%)
  waiting for transfers between devices  32.3 us (25%)
  matrix products  21.9 us (17%)
  blocking collectives  20.8 us (16%)
  local copies, waits for them, and re-layouts  12.3 us (9%)
  other arithmetic  6.86 us (5%)
    all_to_all x3, starting transfers between devices, gather_rows(): return lax.all_to_all(spread, axis_name, 0, 0, tiled=True)  18.6 us
    all_to_all x3, waiting for transfers between devices, gather_rows(): return lax.all_to_all(spread, axis_name, 0, 0, tiled=True)  16.7 us
    all_to_all x2, waiting for transfers between devices, head_total(): return lax.all_to_all(spread, 'head', 0, 1, tiled=True)  11 us
    all_to_all x1, blocking collectives, head_total(): lax.all_to_all(partial_value.astype(jnp.bfloat16), 'head', 1, 0, tiled=True)  10.6 us
    all_to_all x1, blocking collectives, group_attention(): lax.all_to_all(placed.astype(jnp.bfloat16), 'req', 0, 0, tiled=True)  10.2 us
    all_to_all x2, starting transfers between devices, head_total(): return lax.all_to_all(spread, 'head', 0, 1, tiled=True)  8.23 us
    all_to_all x1, starting transfers between devices, head_total(): lax.all_to_all(partial_value.astype(jnp.bfloat16), 'head', 1, 0, tiled=True)  7.85 us
    dot_general x1, matrix products, paged_attention(): jnp.einsum('phc,pnc->phn', query_blocks, stored, preferred_element_type=j...  6.88 us
  transfers between devices with their start and end apart: 6, of which 5 were waited for; matrix products, arithmetic and copies ran while one was open for 14% of the time, Pallas kernels for 0%

profile of v3, /device:TPU:1, one launch (start us, length us, event | category | flops | bytes accessed | tf_op | source)
XLA Modules:
  0.0 129.8 jit_solution(14382876208891122627)
XLA Ops:
  0.6 0.8 slice_bitcast_fusion.2
  1.4 0.7 tile.13
  2.1 8.4 %all-to-all-start = ((bf16[16,64,128]{2,1,0:T(8,128)(2,1)}), bf16[16,64,128]{2,1,0:T(8,128)(2,1)S(1)}, u32[]{:S(2)}, u32[]{:S(2)}) async-start(bf16[16,64,128]{2,1,0:T(8,128)(2,1)} %tile.13), calls=%async_computation | async-start | bytes 524288 | tf_op jit(solution)/shard_map/all_to_all | solution.py:28
  10.6 0.7 fusion.37
  11.3 0.8 copy.62
  12.1 0.7 and_select_fusion.3
  12.8 0.2 fusion.15
  13.0 0.7 select_reduce_fusion.4
  13.8 0.8 copy.63
  14.6 0.2 select_reduce_fusion.1
  14.8 0.7 fusion.36
  15.5 0.7 constant_dynamic-update-slice_fusion
  16.3 0.7 bitcast_dynamic-update-slice_fusion.1
  17.0 0.7 bitcast_dynamic-update-slice_fusion
  17.7 0.8 compare_convert_fusion
  18.6 1.3 %tile.14 = bf16[16,320,128]{2,1,0:T(8,128)(2,1)} broadcast(bf16[320,128]{1,0:T(8,128)(2,1)S(1)} %bitcast_dynamic-update-slice_fusion), dimensions={1,2} | broadcast | bytes 1392640 | tf_op jit(solution)/shard_map/tile | solution.py:27
  20.0 6.7 %all-to-all-start.1 = ((bf16[16,320,128]{2,1,0:T(8,128)(2,1)}), bf16[16,320,128]{2,1,0:T(8,128)(2,1)S(1)}, u32[]{:S(2)}, u32[]{:S(2)}) async-start(bf16[16,320,128]{2,1,0:T(8,128)(2,1)} %tile.14), calls=%async_computation.1 | async-start | bytes 2621440 | tf_op jit(solution)/shard_map/all_to_all | solution.py:28
  26.6 1.1 reduce-window.6
  28.0 0.2 convolution_convert_fusion.2
  28.2 6.9 %fusion.57 = (f32[160,2]{1,0:T(8,128)S(1)}, f32[160,2,256]{2,1,0:T(2,128)S(1)}) fusion(bf16[160,256,128]{2,1,0:T(8,128)(2,1)} %bitcast.125, pred[2,128]{1,0:T(4,128)(4,1)S(1)} %iota_compare_fusion.3, bf16[160,128]{1,0:T(8,128)(2,1)S(1)} %convolution_convert_fusion.2, pred[160,256]{1,0:T(8,128)(4,1)S(1)} %fusion.21), kind=kOutput, calls=%fused_computation.132 | convolution fusion | flops 21257920 | bytes 10896896 | tf_op jit(solution)/shard_map/phc,pnc->phn/dot_general | solution.py:67
  35.3 9.7 %all-to-all-done.1 = bf16[16,320,128]{2,1,0:T(8,128)(2,1)S(1)} async-done(((bf16[16,320,128]{2,1,0:T(8,128)(2,1)}), bf16[16,320,128]{2,1,0:T(8,128)(2,1)S(1)}, u32[]{:S(2)}, u32[]{:S(2)}) %all-to-all-start.1) | async-done | bytes 1310752 | tf_op jit(solution)/shard_map/all_to_all | solution.py:28
  45.5 0.3 fusion.33
  45.8 0.6 fusion.55
  46.4 5.5 %fusion.7 = f32[160,128]{1,0:T(8,128)S(1)} fusion(bf16[160,256,128]{2,1,0:T(8,128)(2,1)} %bitcast.126, bf16[160,2,255]{2,1,0:T(2,128)(2,1)S(1)} %bitcast.136, pred[2,128]{1,0:T(4,128)(4,1)S(1)} %iota_compare_fusion.3), kind=kOutput, calls=%fused_computation.14 | convolution fusion | flops 21032960 | bytes 10731136 | tf_op jit(solution)/shard_map/phn,pnc->phc/dot_general | solution.py:89
  52.3 0.2 convolution_add_fusion.1
  52.5 0.2 fusion.11
  52.9 0.2 fusion.8
  53.1 0.7 copy.102
  53.8 7.8 %all-to-all-start.2 = ((bf16[48,8,128]{2,0,1:T(8,128)(2,1)}), bf16[48,8,128]{2,0,1:T(8,128)(2,1)S(1)}, u32[]{:S(2)}, u32[]{:S(2)}) async-start(bf16[48,8,128]{2,0,1:T(8,128)(2,1)} %bitcast.120), calls=%async_computation.2 | async-start | bytes 196608 | tf_op jit(solution)/shard_map/all_to_all | solution.py:19
  61.6 0.2 slice_reduce_fusion
  62.0 4.6 %all-to-all-done.2 = bf16[48,8,128]{2,0,1:T(8,128)(2,1)S(1)} async-done(((bf16[48,8,128]{2,0,1:T(8,128)(2,1)}), bf16[48,8,128]{2,0,1:T(8,128)(2,1)S(1)}, u32[]{:S(2)}, u32[]{:S(2)}) %all-to-all-start.2) | async-done | bytes 98336 | tf_op jit(solution)/shard_map/all_to_all | solution.py:19
  66.6 0.7 tile.15
  67.3 4.1 %all-to-all-start.3 = ((f32[8,48,128]{2,1,0:T(8,128)}), f32[8,48,128]{2,1,0:T(8,128)S(1)}, u32[]{:S(2)}, u32[]{:S(2)}) async-start(f32[8,48,128]{2,1,0:T(8,128)} %tile.15), calls=%async_computation.3 | async-start | bytes 393216 | tf_op jit(solution)/shard_map/all_to_all | solution.py:22
  71.5 5.8 %all-to-all-done.3 = f32[8,48,128]{2,1,0:T(8,128)S(1)} async-done(((f32[8,48,128]{2,1,0:T(8,128)}), f32[8,48,128]{2,1,0:T(8,128)S(1)}, u32[]{:S(2)}, u32[]{:S(2)}) %all-to-all-start.3) | async-done | bytes 196640 | tf_op jit(solution)/shard_map/all_to_all | solution.py:22
  77.9 0.7 tile.16
  78.6 3.5 %all-to-all-start.4 = ((bf16[16,48,128]{2,1,0:T(8,128)(2,1)}), bf16[16,48,128]{2,1,0:T(8,128)(2,1)S(1)}, u32[]{:S(2)}, u32[]{:S(2)}) async-start(bf16[16,48,128]{2,1,0:T(8,128)(2,1)} %tile.16), calls=%async_computation.4 | async-start | bytes 393216 | tf_op jit(solution)/shard_map/all_to_all | solution.py:28
  82.3 7.1 %all-to-all-done.4 = bf16[16,48,128]{2,1,0:T(8,128)(2,1)S(1)} async-done(((bf16[16,48,128]{2,1,0:T(8,128)(2,1)}), bf16[16,48,128]{2,1,0:T(8,128)(2,1)S(1)}, u32[]{:S(2)}, u32[]{:S(2)}) %all-to-all-start.4) | async-done | bytes 196640 | tf_op jit(solution)/shard_map/all_to_all | solution.py:28
  89.5 4.0 %fusion.58 = (f32[4,32]{1,0:T(4,128)S(1)}, bf16[4,32,4096]{2,1,0:T(8,128)(2,1)S(1)}) fusion(pred[4096]{0:T(1024)(128)(4,1)S(1)} %fusion.35, bf16[4,4096,128]{2,1,0:T(8,128)(2,1)} %bitcast.127, bf16[4,32,128]{2,1,0:T(8,128)(2,1)S(1)} %bitcast.147, pred[32,128]{1,0:T(8,128)(4,1)S(1)} %broadcast_in_dim.218), kind=kOutput, calls=%fused_computation.133 | convolution fusion | flops 137383936 | bytes 5284352 | tf_op jit(solution)/shard_map/sub | solution.py:126
  93.6 3.0 %convolution_divide_fusion = f32[4,32,128]{2,1,0:T(8,128)S(1)} fusion(bf16[4,4096,128]{2,1,0:T(8,128)(2,1)} %bitcast.128, bf16[4,32,4095]{2,1,0:T(8,128)(2,1)S(1)} %bitcast.135, f32[4,32]{1,0:T(4,128)S(1)} %get-tuple-element.29), kind=kOutput, calls=%fused_computation.17 | convolution fusion | flops 134234112 | bytes 5308672 | tf_op jit(solution)/shard_map/gmn,gnc->gmc/dot_general | solution.py:129
  96.6 0.3 fusion.6
  96.9 10.2 %all_to_all.86 = bf16[16,48,128]{2,1,0:T(8,128)(2,1)S(1)} all-to-all(bf16[16,48,128]{2,1,0:T(8,128)(2,1)S(1)} %bitcast.141), channel_id=1, replica_groups=mesh['req'=16,'head'=8] {'req'}, dimensions={0} | all-to-all | bytes 393216 | tf_op jit(solution)/shard_map/all_to_all | solution.py:136
  107.2 0.2 fusion.9
  107.4 10.6 %all_to_all.87 = bf16[48,8,128]{2,0,1:T(8,128)(2,1)S(1)} all-to-all(bf16[48,8,128]{2,0,1:T(8,128)(2,1)S(1)} %bitcast.138), channel_id=1, replica_groups=mesh['req'=16,'head'=8] {'head'}, dimensions={1} | all-to-all | bytes 196608 | tf_op jit(solution)/shard_map/all_to_all | solution.py:19
  118.0 0.7 tile.17
  118.7 4.1 %all-to-all-start.7 = ((f32[8,48,128]{2,1,0:T(8,128)}), f32[8,48,128]{2,1,0:T(8,128)S(1)}, u32[]{:S(2)}, u32[]{:S(2)}) async-start(f32[8,48,128]{2,1,0:T(8,128)} %tile.17), calls=%async_computation.7 | async-start | bytes 393216 | tf_op jit(solution)/shard_map/all_to_all | solution.py:22
  122.8 0.6 copy.74
  123.5 5.2 %all-to-all-done.7 = f32[8,48,128]{2,1,0:T(8,128)S(1)} async-done(((f32[8,48,128]{2,1,0:T(8,128)}), f32[8,48,128]{2,1,0:T(8,128)S(1)}, u32[]{:S(2)}, u32[]{:S(2)}) %all-to-all-start.7) | async-done | bytes 196640 | tf_op jit(solution)/shard_map/all_to_all | solution.py:22
  129.1 0.7 add_convert_fusion
  (62 shorter events, 3.4 us)
Async XLA Ops:
  0.6 27.2 %copy-start = (bf16[48,1024]{1,0:T(8,128)(2,1)S(1)}, bf16[48,1024]{1,0:T(8,128)(2,1)}, u32[]{:S(2)}) copy-start(bf16[48,1024]{1,0:T(8,128)(2,1)} %param.15) | copy-start | bytes 294916
  2.1 16.5 %all-to-all-start = ((bf16[16,64,128]{2,1,0:T(8,128)(2,1)}), bf16[16,64,128]{2,1,0:T(8,128)(2,1)S(1)}, u32[]{:S(2)}, u32[]{:S(2)}) async-start(bf16[16,64,128]{2,1,0:T(8,128)(2,1)} %tile.13), calls=%async_computation | async-start | bytes 524288 | tf_op jit(solution)/shard_map/all_to_all | solution.py:28
  20.0 25.0 %all-to-all-start.1 = ((bf16[16,320,128]{2,1,0:T(8,128)(2,1)}), bf16[16,320,128]{2,1,0:T(8,128)(2,1)S(1)}, u32[]{:S(2)}, u32[]{:S(2)}) async-start(bf16[16,320,128]{2,1,0:T(8,128)(2,1)} %tile.14), calls=%async_computation.1 | async-start | bytes 2621440 | tf_op jit(solution)/shard_map/all_to_all | solution.py:28
  46.4 31.3 %copy-start.2 = (f32[1024]{0:T(1024)S(1)}, f32[1024]{0:T(1024)}, u32[]{:S(2)}) copy-start(f32[1024]{0:T(1024)} %param.27) | copy-start | bytes 12292
  46.4 31.3 %copy-start.3 = (f32[1024]{0:T(1024)S(1)}, f32[1024]{0:T(1024)}, u32[]{:S(2)}) copy-start(f32[1024]{0:T(1024)} %param.26) | copy-start | bytes 12292
  51.9 30.2 %copy-start.1 = (s32[768]{0:T(1024)S(1)}, s32[768]{0:T(1024)}, u32[]{:S(2)}) copy-start(s32[768]{0:T(1024)} %param.19) | copy-start | bytes 9220
  53.8 12.8 %all-to-all-start.2 = ((bf16[48,8,128]{2,0,1:T(8,128)(2,1)}), bf16[48,8,128]{2,0,1:T(8,128)(2,1)S(1)}, u32[]{:S(2)}, u32[]{:S(2)}) async-start(bf16[48,8,128]{2,0,1:T(8,128)(2,1)} %bitcast.120), calls=%async_computation.2 | async-start | bytes 196608 | tf_op jit(solution)/shard_map/all_to_all | solution.py:19
  67.3 10.0 %all-to-all-start.3 = ((f32[8,48,128]{2,1,0:T(8,128)}), f32[8,48,128]{2,1,0:T(8,128)S(1)}, u32[]{:S(2)}, u32[]{:S(2)}) async-start(f32[8,48,128]{2,1,0:T(8,128)} %tile.15), calls=%async_computation.3 | async-start | bytes 393216 | tf_op jit(solution)/shard_map/all_to_all | solution.py:22
  78.6 10.7 %all-to-all-start.4 = ((bf16[16,48,128]{2,1,0:T(8,128)(2,1)}), bf16[16,48,128]{2,1,0:T(8,128)(2,1)S(1)}, u32[]{:S(2)}, u32[]{:S(2)}) async-start(bf16[16,48,128]{2,1,0:T(8,128)(2,1)} %tile.16), calls=%async_computation.4 | async-start | bytes 393216 | tf_op jit(solution)/shard_map/all_to_all | solution.py:28
  93.6 35.5 %copy-start.4 = (f32[1024]{0:T(1024)S(1)}, f32[1024]{0:T(1024)}, u32[]{:S(2)}) copy-start(f32[1024]{0:T(1024)} %param.29) | copy-start | bytes 12292
  93.6 35.5 %copy-start.5 = (f32[1024]{0:T(1024)S(1)}, f32[1024]{0:T(1024)}, u32[]{:S(2)}) copy-start(f32[1024]{0:T(1024)} %param.28) | copy-start | bytes 12292
  118.7 10.0 %all-to-all-start.7 = ((f32[8,48,128]{2,1,0:T(8,128)}), f32[8,48,128]{2,1,0:T(8,128)S(1)}, u32[]{:S(2)}, u32[]{:S(2)}) async-start(f32[8,48,128]{2,1,0:T(8,128)} %tile.17), calls=%async_computation.7 | async-start | bytes 393216 | tf_op jit(solution)/shard_map/all_to_all | solution.py:22

commit v4 on v2

--- a/solution.py
+++ b/solution.py
@@ -33,6 +33,16 @@
     lane_head = jnp.arange(head_cols, dtype=jnp.int32) // HEAD_DIM
     mask = lane_head[None, :] == jnp.arange(heads_here, dtype=jnp.int32)[:, None]
     return jnp.where(mask, query_rows[..., None, :], jnp.zeros((), query_rows.dtype)), mask
+
+
+def weighted_rows(value_weights, stored):
+    heads_here = value_weights.shape[1]
+    lane_head = jnp.arange(stored.shape[2], dtype=jnp.int32) // HEAD_DIM
+    per_row = jnp.swapaxes(value_weights, 1, 2).astype(jnp.float32)
+    lanes = per_row[:, :, :1]
+    for head in range(1, heads_here):
+        lanes = jnp.where(lane_head[None, None, :] == head, per_row[:, :, head : head + 1], lanes)
+    return jnp.sum(lanes * stored.astype(jnp.float32), axis=1)
 
 
 def shift_to_values(weights):
@@ -86,10 +96,7 @@
         + new_weight
     )
     value_weights = shift_to_values(weights.astype(jnp.bfloat16))
-    page_sum = jnp.einsum(
-        "phn,pnc->phc", value_weights, stored, preferred_element_type=jnp.float32
-    )
-    page_sum = jnp.sum(jnp.where(head_mask[None], page_sum, 0.0), axis=1)
+    page_sum = weighted_rows(value_weights, stored)
     summed = jnp.dot(owner_weights, page_sum, precision=lax.Precision.HIGHEST)
     rounded_new = lax.optimization_barrier(new_weight.astype(jnp.bfloat16)).astype(jnp.float32)
     own_term = rounded_new[:, :, None] * new_value.astype(jnp.float32).reshape(

time: 127 us -> 198 us (1.56)
  other arithmetic: 6.91 us -> 59.3 us
  local copies, waits for them, and re-layouts: 8.08 us -> 32.6 us
  matrix products: 22.6 us -> 17 us
    reduce_sum x0 -> x1, other arithmetic: none -> 52.1 us  [weighted_rows(): return jnp.sum(lanes * stored.astype(jnp.float32), axis=1)]
    broadcast_in_dim x0 -> x2, local copies, waits for them, and re-layouts: none -> 23.7 us  [weighted_rows(): jnp.where(lane_head[None, None, :] == head, per_row[:, :, head:head + 1],...]
    dot_general x1 -> x0, matrix products: 5.53 us -> none  [paged_attention(): jnp.einsum('phn,pnc->phc', value_weights, stored, preferred_element_type=...]
  transfers between devices with their start and end apart: 6 -> 6, of which waited for: 5 -> 5; matrix products, arithmetic and copies ran while one was open for 18% -> 47% of each run, Pallas kernels for 0% -> 0%
where the time goes in v4:
time: 198 us; the launch traced here: 197 us
  other arithmetic  59.3 us (30%)
  starting transfers between devices  34.1 us (17%)
  local copies, waits for them, and re-layouts  32.6 us (16%)
  waiting for transfers between devices  31.2 us (16%)
  blocking collectives  21.9 us (11%)
  matrix products  17 us (9%)
    reduce_sum x1, other arithmetic, weighted_rows(): return jnp.sum(lanes * stored.astype(jnp.float32), axis=1)  52.1 us
    broadcast_in_dim x2, local copies, waits for them, and re-layouts, weighted_rows(): jnp.where(lane_head[None, None, :] == head, per_row[:, :, head:head + 1],...  23.7 us
    all_to_all x3, starting transfers between devices, gather_rows(): return lax.all_to_all(spread, axis_name, 0, 0, tiled=True)  19 us
    all_to_all x3, waiting for transfers between devices, gather_rows(): return lax.all_to_all(spread, axis_name, 0, 0, tiled=True)  15.9 us
    all_to_all x1, blocking collectives, head_total(): pieces = lax.all_to_all(partial_value, 'head', 1, 0, tiled=True)  11.7 us
    all_to_all x2, waiting for transfers between devices, head_total(): return lax.all_to_all(spread, 'head', 0, 1, tiled=True)  11 us
    all_to_all x1, blocking collectives, group_attention(): lax.all_to_all(placed.astype(jnp.bfloat16), 'req', 0, 0, tiled=True)  10.2 us
    all_to_all x2, starting transfers between devices, head_total(): return lax.all_to_all(spread, 'head', 0, 1, tiled=True)  8.49 us
  transfers between devices with their start and end apart: 6, of which 5 were waited for; matrix products, arithmetic and copies ran while one was open for 47% of the time, Pallas kernels for 0%

profile of v4, /device:TPU:1, one launch (start us, length us, event | category | flops | bytes accessed | tf_op | source)
XLA Modules:
  0.0 197.1 jit_solution(7324236432865661050)
XLA Ops:
  0.6 1.9 tile.13
  2.5 8.4 %all-to-all-start = ((bf16[16,192,128]{2,1,0:T(8,128)(2,1)}), bf16[16,192,128]{2,1,0:T(8,128)(2,1)S(1)}, u32[]{:S(2)}, u32[]{:S(2)}) async-start(bf16[16,192,128]{2,1,0:T(8,128)(2,1)} %tile.13), calls=%async_computation | async-start | bytes 1572864 | tf_op jit(solution)/shard_map/all_to_all | solution.py:28
  11.0 0.8 copy.72
  11.7 0.7 and_select_fusion.3
  12.5 0.2 fusion.12
  12.7 0.7 select_reduce_fusion.4
  13.5 0.8 copy.73
  14.2 0.2 select_reduce_fusion.1
  14.5 0.8 pad_maximum_fusion
  15.4 8.8 %all-to-all-done = bf16[16,192,128]{2,1,0:T(8,128)(2,1)S(1)} async-done(((bf16[16,192,128]{2,1,0:T(8,128)(2,1)}), bf16[16,192,128]{2,1,0:T(8,128)(2,1)S(1)}, u32[]{:S(2)}, u32[]{:S(2)}) %all-to-all-start) | async-done | bytes 786464 | tf_op jit(solution)/shard_map/all_to_all | solution.py:28
  24.2 1.0 tile.14
  25.2 3.7 %all-to-all-start.1 = ((bf16[16,192,128]{2,1,0:T(8,128)(2,1)}), bf16[16,192,128]{2,1,0:T(8,128)(2,1)S(1)}, u32[]{:S(2)}, u32[]{:S(2)}) async-start(bf16[16,192,128]{2,1,0:T(8,128)(2,1)} %tile.14), calls=%async_computation.1 | async-start | bytes 1572864 | tf_op jit(solution)/shard_map/all_to_all | solution.py:28
  29.1 0.2 convolution_convert_fusion
  29.4 6.9 %fusion.53 = (f32[160,2]{1,0:T(8,128)S(1)}, f32[160,2,256]{2,1,0:T(2,128)S(1)}) fusion(bf16[160,256,128]{2,1,0:T(8,128)(2,1)} %bitcast.103, pred[2,128]{1,0:T(4,128)(4,1)S(1)} %iota_compare_fusion.3, bf16[160,128]{1,0:T(8,128)(2,1)S(1)} %convolution_convert_fusion, pred[160,256]{1,0:T(8,128)(4,1)S(1)} %fusion.17), kind=kOutput, calls=%fused_computation.120 | convolution fusion | flops 21257920 | bytes 10896896 | tf_op jit(solution)/shard_map/phc,pnc->phn/dot_general | solution.py:77
  36.9 0.3 fusion.29
  37.2 0.6 fusion.50
  37.8 0.3 convert_bitcast_fusion
  38.1 0.8 slice_reduce_fusion.1
  38.9 11.8 %reshape.378 = f32[160,128,2]{2,1,0:T(8,128)} reshape(f32[160,256]{1,0:T(8,128)S(1)} %get-tuple-element.14) | data formatting | bytes 327680 | tf_op jit(solution)/shard_map/jit(_where)/broadcast_in_dim | solution.py:44
  50.7 11.9 %reshape.379 = f32[160,128,2]{2,1,0:T(8,128)} reshape(f32[160,256]{1,0:T(8,128)S(1)} %get-tuple-element.15) | data formatting | bytes 327680 | tf_op jit(solution)/shard_map/jit(_where)/broadcast_in_dim | solution.py:44
  62.6 52.1 %multiply_reduce_fusion = f32[160,128]{1,0:T(8,128)S(1)} fusion(bf16[160,128,2,128]{3,2,1,0:T(2,128)(2,1)} %param.20, pred[128]{0:T(512)(128)(4,1)S(1)} %broadcast_compare_fusion.2, f32[160,128,2]{2,1,0:T(8,128)} %reshape.379, f32[160,128,2]{2,1,0:T(8,128)} %reshape.378), kind=kLoop, calls=%fused_computation.1 | loop fusion | flops 20951040 | bytes 10895488 | tf_op jit(solution)/shard_map/reduce_sum | solution.py:45
  115.1 0.2 convolution_add_fusion.1
  115.3 0.2 fusion.8
  115.8 0.9 fusion.57
  116.7 6.6 %all-to-all-start.2 = ((f32[48,8,128]{2,0,1:T(8,128)}), f32[48,8,128]{2,0,1:T(8,128)S(1)}, u32[]{:S(2)}, u32[]{:S(2)}) async-start(f32[48,8,128]{2,0,1:T(8,128)} %fusion.57), calls=%async_computation.2 | async-start | bytes 393216 | tf_op jit(solution)/shard_map/all_to_all | solution.py:19
  123.4 1.1 reduce-window.6
  124.5 0.2 slice_reduce_fusion.2
  124.7 0.2 reduce-window.9
  124.9 4.3 %all-to-all-done.2 = f32[48,8,128]{2,0,1:T(8,128)S(1)} async-done(((f32[48,8,128]{2,0,1:T(8,128)}), f32[48,8,128]{2,0,1:T(8,128)S(1)}, u32[]{:S(2)}, u32[]{:S(2)}) %all-to-all-start.2) | async-done | bytes 196640 | tf_op jit(solution)/shard_map/all_to_all | solution.py:19
  129.2 0.7 tile.15
  129.8 4.2 %all-to-all-start.3 = ((f32[8,48,128]{2,1,0:T(8,128)}), f32[8,48,128]{2,1,0:T(8,128)S(1)}, u32[]{:S(2)}, u32[]{:S(2)}) async-start(f32[8,48,128]{2,1,0:T(8,128)} %tile.15), calls=%async_computation.3 | async-start | bytes 393216 | tf_op jit(solution)/shard_map/all_to_all | solution.py:22
  134.2 5.8 %all-to-all-done.3 = f32[8,48,128]{2,1,0:T(8,128)S(1)} async-done(((f32[8,48,128]{2,1,0:T(8,128)}), f32[8,48,128]{2,1,0:T(8,128)S(1)}, u32[]{:S(2)}, u32[]{:S(2)}) %all-to-all-start.3) | async-done | bytes 196640 | tf_op jit(solution)/shard_map/all_to_all | solution.py:22
  140.1 0.2 multiply_reduce_fusion.2
  140.6 0.7 tile.16
  141.3 6.9 %all-to-all-start.4 = ((bf16[16,48,128]{2,1,0:T(8,128)(2,1)}), bf16[16,48,128]{2,1,0:T(8,128)(2,1)S(1)}, u32[]{:S(2)}, u32[]{:S(2)}) async-start(bf16[16,48,128]{2,1,0:T(8,128)(2,1)} %tile.16), calls=%async_computation.4 | async-start | bytes 393216 | tf_op jit(solution)/shard_map/all_to_all | solution.py:28
  148.3 7.2 %all-to-all-done.4 = bf16[16,48,128]{2,1,0:T(8,128)(2,1)S(1)} async-done(((bf16[16,48,128]{2,1,0:T(8,128)(2,1)}), bf16[16,48,128]{2,1,0:T(8,128)(2,1)S(1)}, u32[]{:S(2)}, u32[]{:S(2)}) %all-to-all-start.4) | async-done | bytes 196640 | tf_op jit(solution)/shard_map/all_to_all | solution.py:28
  155.6 4.0 %fusion.54 = (f32[4,32]{1,0:T(4,128)S(1)}, bf16[4,32,4096]{2,1,0:T(8,128)(2,1)S(1)}) fusion(pred[4096]{0:T(1024)(128)(4,1)S(1)} %fusion.31, bf16[4,4096,128]{2,1,0:T(8,128)(2,1)} %bitcast.104, bf16[4,32,128]{2,1,0:T(8,128)(2,1)S(1)} %bitcast.121, pred[32,128]{1,0:T(8,128)(4,1)S(1)} %broadcast_in_dim.238), kind=kOutput, calls=%fused_computation.121 | convolution fusion | flops 137383936 | bytes 5284352 | tf_op jit(solution)/shard_map/sub | solution.py:133
  159.7 3.0 %convolution_divide_fusion = f32[4,32,128]{2,1,0:T(8,128)S(1)} fusion(bf16[4,4096,128]{2,1,0:T(8,128)(2,1)} %bitcast.105, bf16[4,32,4095]{2,1,0:T(8,128)(2,1)S(1)} %bitcast.112, f32[4,32]{1,0:T(4,128)S(1)} %get-tuple-element.30), kind=kOutput, calls=%fused_computation.12 | convolution fusion | flops 134234112 | bytes 5308672 | tf_op jit(solution)/shard_map/gmn,gnc->gmc/dot_general | solution.py:136
  162.7 0.3 fusion.6
  163.0 10.2 %all_to_all.80 = bf16[16,48,128]{2,1,0:T(8,128)(2,1)S(1)} all-to-all(bf16[16,48,128]{2,1,0:T(8,128)(2,1)S(1)} %bitcast.117), channel_id=1, replica_groups=mesh['req'=16,'head'=8] {'req'}, dimensions={0} | all-to-all | bytes 393216 | tf_op jit(solution)/shard_map/all_to_all | solution.py:143
  173.3 0.2 fusion.37
  173.5 11.7 %all_to_all.81 = f32[48,8,128]{2,0,1:T(8,128)S(1)} all-to-all(f32[48,8,128]{2,0,1:T(8,128)S(1)} %fusion.37), channel_id=1, replica_groups=mesh['req'=16,'head'=8] {'head'}, dimensions={1} | all-to-all | bytes 393216 | tf_op jit(solution)/shard_map/all_to_all | solution.py:19
  185.2 0.7 tile.17
  185.9 4.2 %all-to-all-start.7 = ((f32[8,48,128]{2,1,0:T(8,128)}), f32[8,48,128]{2,1,0:T(8,128)S(1)}, u32[]{:S(2)}, u32[]{:S(2)}) async-start(f32[8,48,128]{2,1,0:T(8,128)} %tile.17), calls=%async_computation.7 | async-start | bytes 393216 | tf_op jit(solution)/shard_map/all_to_all | solution.py:22
  190.1 0.6 copy.86
  190.8 5.2 %all-to-all-done.7 = f32[8,48,128]{2,1,0:T(8,128)S(1)} async-done(((f32[8,48,128]{2,1,0:T(8,128)}), f32[8,48,128]{2,1,0:T(8,128)S(1)}, u32[]{:S(2)}, u32[]{:S(2)}) %all-to-all-start.7) | async-done | bytes 196640 | tf_op jit(solution)/shard_map/all_to_all | solution.py:22
  196.1 0.2 multiply_reduce_fusion.1
  196.4 0.7 add_convert_fusion
  (61 shorter events, 2.9 us)
Async XLA Ops:
  0.6 28.3 %copy-start = (bf16[48,1024]{1,0:T(8,128)(2,1)S(1)}, bf16[48,1024]{1,0:T(8,128)(2,1)}, u32[]{:S(2)}) copy-start(bf16[48,1024]{1,0:T(8,128)(2,1)} %param.15) | copy-start | bytes 294916
  2.5 21.7 %all-to-all-start = ((bf16[16,192,128]{2,1,0:T(8,128)(2,1)}), bf16[16,192,128]{2,1,0:T(8,128)(2,1)S(1)}, u32[]{:S(2)}, u32[]{:S(2)}) async-start(bf16[16,192,128]{2,1,0:T(8,128)(2,1)} %tile.13), calls=%async_computation | async-start | bytes 1572864 | tf_op jit(solution)/shard_map/all_to_all | solution.py:28
  25.2 90.5 %all-to-all-start.1 = ((bf16[16,192,128]{2,1,0:T(8,128)(2,1)}), bf16[16,192,128]{2,1,0:T(8,128)(2,1)S(1)}, u32[]{:S(2)}, u32[]{:S(2)}) async-start(bf16[16,192,128]{2,1,0:T(8,128)(2,1)} %tile.14), calls=%async_computation.1 | async-start | bytes 1572864 | tf_op jit(solution)/shard_map/all_to_all | solution.py:28
  62.6 60.7 %copy-start.1 = (s32[768]{0:T(1024)S(1)}, s32[768]{0:T(1024)}, u32[]{:S(2)}) copy-start(s32[768]{0:T(1024)} %param.19) | copy-start | bytes 9220
  114.7 25.6 %copy-start.2 = (f32[1024]{0:T(1024)S(1)}, f32[1024]{0:T(1024)}, u32[]{:S(2)}) copy-start(f32[1024]{0:T(1024)} %param.27) | copy-start | bytes 12292
  114.7 25.6 %copy-start.3 = (f32[1024]{0:T(1024)S(1)}, f32[1024]{0:T(1024)}, u32[]{:S(2)}) copy-start(f32[1024]{0:T(1024)} %param.26) | copy-start | bytes 12292
  116.7 12.5 %all-to-all-start.2 = ((f32[48,8,128]{2,0,1:T(8,128)}), f32[48,8,128]{2,0,1:T(8,128)S(1)}, u32[]{:S(2)}, u32[]{:S(2)}) async-start(f32[48,8,128]{2,0,1:T(8,128)} %fusion.57), calls=%async_computation.2 | async-start | bytes 393216 | tf_op jit(solution)/shard_map/all_to_all | solution.py:19
  129.8 10.1 %all-to-all-start.3 = ((f32[8,48,128]{2,1,0:T(8,128)}), f32[8,48,128]{2,1,0:T(8,128)S(1)}, u32[]{:S(2)}, u32[]{:S(2)}) async-start(f32[8,48,128]{2,1,0:T(8,128)} %tile.15), calls=%async_computation.3 | async-start | bytes 393216 | tf_op jit(solution)/shard_map/all_to_all | solution.py:22
  141.3 14.1 %all-to-all-start.4 = ((bf16[16,48,128]{2,1,0:T(8,128)(2,1)}), bf16[16,48,128]{2,1,0:T(8,128)(2,1)S(1)}, u32[]{:S(2)}, u32[]{:S(2)}) async-start(bf16[16,48,128]{2,1,0:T(8,128)(2,1)} %tile.16), calls=%async_computation.4 | async-start | bytes 393216 | tf_op jit(solution)/shard_map/all_to_all | solution.py:28
  159.7 36.7 %copy-start.4 = (f32[1024]{0:T(1024)S(1)}, f32[1024]{0:T(1024)}, u32[]{:S(2)}) copy-start(f32[1024]{0:T(1024)} %param.29) | copy-start | bytes 12292
  159.7 36.7 %copy-start.5 = (f32[1024]{0:T(1024)S(1)}, f32[1024]{0:T(1024)}, u32[]{:S(2)}) copy-start(f32[1024]{0:T(1024)} %param.28) | copy-start | bytes 12292
  185.9 10.1 %all-to-all-start.7 = ((f32[8,48,128]{2,1,0:T(8,128)}), f32[8,48,128]{2,1,0:T(8,128)S(1)}, u32[]{:S(2)}, u32[]{:S(2)}) async-start(f32[8,48,128]{2,1,0:T(8,128)} %tile.17), calls=%async_computation.7 | async-start | bytes 393216 | tf_op jit(solution)/shard_map/all_to_all | solution.py:22

commit v5 on v2

--- a/solution.py
+++ b/solution.py
@@ -1,6 +1,10 @@
+import functools
+
 import jax
 import jax.numpy as jnp
 from jax import lax
+from jax.experimental import pallas as pl
+from jax.experimental.pallas import tpu as pltpu
 from jax.sharding import PartitionSpec as P
 
 HEAD_DIM = 64
@@ -99,6 +103,42 @@
     return (summed / total[:, :, None]).reshape(rows_here, head_cols).astype(jnp.bfloat16)
 
 
+def cross_kernel(q_ref, kv_ref, out_ref, *, scale):
+    query = q_ref[0]
+    stored = kv_ref[0]
+    scores = (
+        lax.dot_general(
+            query, stored, (((1,), (1,)), ((), ())), preferred_element_type=jnp.float32
+        )
+        * scale
+    )
+    lane = lax.broadcasted_iota(jnp.int32, scores.shape, 1)
+    is_key = lane % 2 == 0
+    scores = jnp.where(is_key, scores, -1e30)
+    top = jnp.max(scores, axis=1, keepdims=True)
+    weights = jnp.where(is_key, jnp.exp(scores - top), 0.0)
+    total = jnp.sum(weights, axis=1, keepdims=True)
+    rounded = weights.astype(jnp.bfloat16).astype(jnp.float32)
+    moved = pltpu.roll(rounded, 1, 1).astype(jnp.bfloat16)
+    summed = jnp.dot(moved, stored, preferred_element_type=jnp.float32)
+    out_ref[0] = summed / total
+
+
+def cross_call(query_blocks, stored, scale):
+    groups, rows, cols = query_blocks.shape
+    positions = stored.shape[1]
+    return pl.pallas_call(
+        functools.partial(cross_kernel, scale=scale),
+        grid=(groups,),
+        in_specs=[
+            pl.BlockSpec((1, rows, cols), lambda g: (g, 0, 0)),
+            pl.BlockSpec((1, positions, cols), lambda g: (g, 0, 0)),
+        ],
+        out_specs=pl.BlockSpec((1, rows, cols), lambda g: (g, 0, 0)),
+        out_shape=jax.ShapeDtypeStruct((groups, rows, cols), jnp.float32),
+    )(query_blocks, stored)
+
+
 def group_attention(cross_query, group_of, enc_kv, scale):
     groups_here, positions, _, head_cols = enc_kv.shape
     heads_here = head_cols // HEAD_DIM
@@ -115,21 +155,8 @@
     query_blocks, head_mask = head_blocks(group_query, head_cols)
     query_blocks = query_blocks.reshape(groups_here, GMAX * heads_here, head_cols)
     stored = enc_kv.reshape(groups_here, 2 * positions, head_cols)
-    lane = jnp.arange(2 * positions, dtype=jnp.int32)
-    is_key = (lane % 2 == 0)[None, None, :]
-    scores = (
-        jnp.einsum("gmc,gnc->gmn", query_blocks, stored, preferred_element_type=jnp.float32)
-        * scale
-    )
-    scores = jnp.where(is_key, scores, -1e30)
-    top = jnp.max(scores, axis=2)
-    weights = jnp.where(is_key, jnp.exp(scores - top[:, :, None]), 0.0)
-    total = jnp.sum(weights, axis=2)
-    value_weights = shift_to_values(weights.astype(jnp.bfloat16))
-    summed = jnp.einsum(
-        "gmn,gnc->gmc", value_weights, stored, preferred_element_type=jnp.float32
-    )
-    summed = (summed / total[:, :, None]).reshape(groups_here, GMAX, heads_here, head_cols)
+    summed = cross_call(query_blocks, stored, scale)
+    summed = summed.reshape(groups_here, GMAX, heads_here, head_cols)
     context = jnp.sum(jnp.where(head_mask[None, None], summed, 0.0), axis=2).astype(jnp.bfloat16)
     placed = jnp.einsum("gkr,gkc->rc", picker, context, preferred_element_type=jnp.float32)
     parts = lax.psum(1, "req")

time: 127 us -> 128 us (level)
  matrix products: 22.6 us -> 16.5 us
  Pallas kernels: 0 us -> 5.84 us
  other arithmetic: 6.91 us -> 8.35 us
    pallas_call x0 -> x1, Pallas kernels: none -> 5.84 us  [cross_call(): pl.pallas_call(functools.partial(cross_kernel, scale=scale), grid=(groups...]
    sub x1 -> x0, matrix products: 4.04 us -> none  [group_attention(): weights = jnp.where(is_key, jnp.exp(scores - top[:, :, None]), 0.0)]
    dot_general x1 -> x0, matrix products: 2.95 us -> none  [group_attention(): jnp.einsum('gmn,gnc->gmc', value_weights, stored, preferred_element_type=...]
where the time goes in v5:
time: 128 us; the launch traced here: 127 us
  starting transfers between devices  34.1 us (27%)
  waiting for transfers between devices  31.2 us (24%)
  blocking collectives  21.9 us (17%)
  matrix products  16.5 us (13%)
  other arithmetic  8.35 us (7%)
  local copies, waits for them, and re-layouts  8.09 us (6%)
  Pallas kernels  5.84 us (5%)
    all_to_all x3, starting transfers between devices, gather_rows(): return lax.all_to_all(spread, axis_name, 0, 0, tiled=True)  19 us
    all_to_all x3, waiting for transfers between devices, gather_rows(): return lax.all_to_all(spread, axis_name, 0, 0, tiled=True)  15.9 us
    all_to_all x1, blocking collectives, head_total(): pieces = lax.all_to_all(partial_value, 'head', 1, 0, tiled=True)  11.7 us
    all_to_all x2, waiting for transfers between devices, head_total(): return lax.all_to_all(spread, 'head', 0, 1, tiled=True)  11 us
    all_to_all x1, blocking collectives, group_attention(): lax.all_to_all(placed.astype(jnp.bfloat16), 'req', 0, 0, tiled=True)  10.2 us
    all_to_all x2, starting transfers between devices, head_total(): return lax.all_to_all(spread, 'head', 0, 1, tiled=True)  8.49 us
    dot_general x1, matrix products, paged_attention(): jnp.einsum('phc,pnc->phn', query_blocks, stored, preferred_element_type=j...  6.88 us
    all_to_all x1, starting transfers between devices, head_total(): pieces = lax.all_to_all(partial_value, 'head', 1, 0, tiled=True)  6.62 us
  transfers between devices with their start and end apart: 6, of which 5 were waited for; matrix products, arithmetic and copies ran while one was open for 18% of the time, Pallas kernels for 0%

profile of v5, /device:TPU:1, one launch (start us, length us, event | category | flops | bytes accessed | tf_op | source)
XLA Modules:
  0.0 126.9 jit_solution(6059064402751788813)
XLA Ops:
  0.6 1.9 %tile.13 = bf16[16,192,128]{2,1,0:T(8,128)(2,1)} broadcast(bf16[192,128]{1,0:T(8,128)(2,1)} %bitcast.116), dimensions={1,2} | broadcast | bytes 835584 | tf_op jit(solution)/shard_map/tile | solution.py:31
  2.5 8.4 %all-to-all-start = ((bf16[16,192,128]{2,1,0:T(8,128)(2,1)}), bf16[16,192,128]{2,1,0:T(8,128)(2,1)S(1)}, u32[]{:S(2)}, u32[]{:S(2)}) async-start(bf16[16,192,128]{2,1,0:T(8,128)(2,1)} %tile.13), calls=%async_computation | async-start | bytes 1572864 | tf_op jit(solution)/shard_map/all_to_all | solution.py:32
  11.0 0.8 copy.56
  11.7 0.7 and_select_fusion.3
  12.5 0.2 fusion.7
  12.7 0.7 select_reduce_fusion.4
  13.5 0.8 copy.57
  14.2 0.2 select_reduce_fusion.1
  14.5 0.8 pad_maximum_fusion
  15.4 8.8 %all-to-all-done = bf16[16,192,128]{2,1,0:T(8,128)(2,1)S(1)} async-done(((bf16[16,192,128]{2,1,0:T(8,128)(2,1)}), bf16[16,192,128]{2,1,0:T(8,128)(2,1)S(1)}, u32[]{:S(2)}, u32[]{:S(2)}) %all-to-all-start) | async-done | bytes 786464 | tf_op jit(solution)/shard_map/all_to_all | solution.py:32
  24.2 1.0 tile.14
  25.2 3.7 %all-to-all-start.1 = ((bf16[16,192,128]{2,1,0:T(8,128)(2,1)}), bf16[16,192,128]{2,1,0:T(8,128)(2,1)S(1)}, u32[]{:S(2)}, u32[]{:S(2)}) async-start(bf16[16,192,128]{2,1,0:T(8,128)(2,1)} %tile.14), calls=%async_computation.1 | async-start | bytes 1572864 | tf_op jit(solution)/shard_map/all_to_all | solution.py:32
  29.0 1.1 convolution_convert_fusion.5
  30.0 0.2 convolution_convert_fusion
  30.3 6.9 %fusion.41 = (f32[160,2]{1,0:T(8,128)S(1)}, f32[160,2,256]{2,1,0:T(2,128)S(1)}) fusion(bf16[160,256,128]{2,1,0:T(8,128)(2,1)} %bitcast.99, pred[2,128]{1,0:T(4,128)(4,1)S(1)} %iota_compare_fusion.3, bf16[160,128]{1,0:T(8,128)(2,1)S(1)} %convolution_convert_fusion, pred[160,256]{1,0:T(8,128)(4,1)S(1)} %fusion.13), kind=kOutput, calls=%fused_computation.100 | convolution fusion | flops 21257920 | bytes 10896896 | tf_op jit(solution)/shard_map/phc,pnc->phn/dot_general | solution.py:71
  37.3 0.2 convert_multiply_fusion
  37.8 0.3 fusion.23
  38.1 0.6 fusion.38
  38.7 5.5 %fusion.2 = f32[160,128]{1,0:T(8,128)S(1)} fusion(bf16[160,256,128]{2,1,0:T(8,128)(2,1)} %bitcast.100, bf16[160,2,255]{2,1,0:T(2,128)(2,1)S(1)} %bitcast.108, pred[2,128]{1,0:T(4,128)(4,1)S(1)} %iota_compare_fusion.3), kind=kOutput, calls=%fused_computation.5 | convolution fusion | flops 21032960 | bytes 10731136 | tf_op jit(solution)/shard_map/phn,pnc->phc/dot_general | solution.py:93
  44.3 0.2 convolution_convert_fusion.3
  44.7 0.2 convolution_add_fusion.1
  44.9 0.2 fusion.4
  45.3 0.9 fusion.42
  46.2 6.6 %all-to-all-start.2 = ((f32[48,8,128]{2,0,1:T(8,128)}), f32[48,8,128]{2,0,1:T(8,128)S(1)}, u32[]{:S(2)}, u32[]{:S(2)}) async-start(f32[48,8,128]{2,0,1:T(8,128)} %fusion.42), calls=%async_computation.2 | async-start | bytes 393216 | tf_op jit(solution)/shard_map/all_to_all | solution.py:23
  52.9 1.1 reduce-window.6
  54.0 0.2 slice_reduce_fusion
  54.2 0.2 reduce-window.9
  54.4 4.3 %all-to-all-done.2 = f32[48,8,128]{2,0,1:T(8,128)S(1)} async-done(((f32[48,8,128]{2,0,1:T(8,128)}), f32[48,8,128]{2,0,1:T(8,128)S(1)}, u32[]{:S(2)}, u32[]{:S(2)}) %all-to-all-start.2) | async-done | bytes 196640 | tf_op jit(solution)/shard_map/all_to_all | solution.py:23
  58.7 0.7 tile.15
  59.4 4.2 %all-to-all-start.3 = ((f32[8,48,128]{2,1,0:T(8,128)}), f32[8,48,128]{2,1,0:T(8,128)S(1)}, u32[]{:S(2)}, u32[]{:S(2)}) async-start(f32[8,48,128]{2,1,0:T(8,128)} %tile.15), calls=%async_computation.3 | async-start | bytes 393216 | tf_op jit(solution)/shard_map/all_to_all | solution.py:26
  63.7 5.8 %all-to-all-done.3 = f32[8,48,128]{2,1,0:T(8,128)S(1)} async-done(((f32[8,48,128]{2,1,0:T(8,128)}), f32[8,48,128]{2,1,0:T(8,128)S(1)}, u32[]{:S(2)}, u32[]{:S(2)}) %all-to-all-start.3) | async-done | bytes 196640 | tf_op jit(solution)/shard_map/all_to_all | solution.py:26
  69.6 0.2 multiply_reduce_fusion.1
  70.1 0.7 tile.16
  70.8 6.9 %all-to-all-start.4 = ((bf16[16,48,128]{2,1,0:T(8,128)(2,1)}), bf16[16,48,128]{2,1,0:T(8,128)(2,1)S(1)}, u32[]{:S(2)}, u32[]{:S(2)}) async-start(bf16[16,48,128]{2,1,0:T(8,128)(2,1)} %tile.16), calls=%async_computation.4 | async-start | bytes 393216 | tf_op jit(solution)/shard_map/all_to_all | solution.py:32
  77.8 7.2 %all-to-all-done.4 = bf16[16,48,128]{2,1,0:T(8,128)(2,1)S(1)} async-done(((bf16[16,48,128]{2,1,0:T(8,128)(2,1)}), bf16[16,48,128]{2,1,0:T(8,128)(2,1)S(1)}, u32[]{:S(2)}, u32[]{:S(2)}) %all-to-all-start.4) | async-done | bytes 196640 | tf_op jit(solution)/shard_map/all_to_all | solution.py:32
  85.2 0.6 broadcast_select_fusion.2.q_ref
  85.8 5.8 %shard_map.158 = f32[4,32,128]{2,1,0:T(8,128)} custom-call(bf16[4,32,128]{2,1,0:T(8,128)(2,1)} %broadcast_select_fusion.2.q_ref, bf16[4,4096,128]{2,1,0:T(8,128)(2,1)} %bitcast.101), custom_call_target="tpu_custom_call" | custom-call | tf_op jit(solution)/shard_map/pallas_call | solution.py:130
  91.6 0.9 select_reduce_fusion.3
  92.6 0.3 fusion.1
  92.8 10.2 %all_to_all.80 = bf16[16,48,128]{2,1,0:T(8,128)(2,1)S(1)} all-to-all(bf16[16,48,128]{2,1,0:T(8,128)(2,1)S(1)} %bitcast.112), channel_id=1, replica_groups=mesh['req'=16,'head'=8] {'req'}, dimensions={0} | all-to-all | bytes 393216 | tf_op jit(solution)/shard_map/all_to_all | solution.py:163
  103.1 0.2 fusion.26
  103.3 11.7 %all_to_all.81 = f32[48,8,128]{2,0,1:T(8,128)S(1)} all-to-all(f32[48,8,128]{2,0,1:T(8,128)S(1)} %fusion.26), channel_id=1, replica_groups=mesh['req'=16,'head'=8] {'head'}, dimensions={1} | all-to-all | bytes 393216 | tf_op jit(solution)/shard_map/all_to_all | solution.py:23
  115.0 0.7 tile.17
  115.7 4.2 %all-to-all-start.7 = ((f32[8,48,128]{2,1,0:T(8,128)}), f32[8,48,128]{2,1,0:T(8,128)S(1)}, u32[]{:S(2)}, u32[]{:S(2)}) async-start(f32[8,48,128]{2,1,0:T(8,128)} %tile.17), calls=%async_computation.7 | async-start | bytes 393216 | tf_op jit(solution)/shard_map/all_to_all | solution.py:26
  120.0 0.6 copy.66
  120.6 5.2 %all-to-all-done.7 = f32[8,48,128]{2,1,0:T(8,128)S(1)} async-done(((f32[8,48,128]{2,1,0:T(8,128)}), f32[8,48,128]{2,1,0:T(8,128)S(1)}, u32[]{:S(2)}, u32[]{:S(2)}) %all-to-all-start.7) | async-done | bytes 196640 | tf_op jit(solution)/shard_map/all_to_all | solution.py:26
  126.0 0.2 multiply_reduce_fusion
  126.2 0.7 add_convert_fusion
  (55 shorter events, 2.2 us)
Async XLA Ops:
  0.6 36.7 %copy-start = (bf16[48,1024]{1,0:T(8,128)(2,1)S(1)}, bf16[48,1024]{1,0:T(8,128)(2,1)}, u32[]{:S(2)}) copy-start(bf16[48,1024]{1,0:T(8,128)(2,1)} %param.15) | copy-start | bytes 294916
  2.5 21.7 %all-to-all-start = ((bf16[16,192,128]{2,1,0:T(8,128)(2,1)}), bf16[16,192,128]{2,1,0:T(8,128)(2,1)S(1)}, u32[]{:S(2)}, u32[]{:S(2)}) async-start(bf16[16,192,128]{2,1,0:T(8,128)(2,1)} %tile.13), calls=%async_computation | async-start | bytes 1572864 | tf_op jit(solution)/shard_map/all_to_all | solution.py:32
  25.2 20.1 %all-to-all-start.1 = ((bf16[16,192,128]{2,1,0:T(8,128)(2,1)}), bf16[16,192,128]{2,1,0:T(8,128)(2,1)S(1)}, u32[]{:S(2)}, u32[]{:S(2)}) async-start(bf16[16,192,128]{2,1,0:T(8,128)(2,1)} %tile.14), calls=%async_computation.1 | async-start | bytes 1572864 | tf_op jit(solution)/shard_map/all_to_all | solution.py:32
  38.7 14.1 %copy-start.1 = (s32[768]{0:T(1024)S(1)}, s32[768]{0:T(1024)}, u32[]{:S(2)}) copy-start(s32[768]{0:T(1024)} %param.19) | copy-start | bytes 9220
  38.7 31.2 %copy-start.2 = (f32[1024]{0:T(1024)S(1)}, f32[1024]{0:T(1024)}, u32[]{:S(2)}) copy-start(f32[1024]{0:T(1024)} %param.27) | copy-start | bytes 12292
  38.7 31.2 %copy-start.3 = (f32[1024]{0:T(1024)S(1)}, f32[1024]{0:T(1024)}, u32[]{:S(2)}) copy-start(f32[1024]{0:T(1024)} %param.26) | copy-start | bytes 12292
  44.2 81.9 %copy-start.4 = (f32[1024]{0:T(1024)S(1)}, f32[1024]{0:T(1024)}, u32[]{:S(2)}) copy-start(f32[1024]{0:T(1024)} %param.29) | copy-start | bytes 12292
  44.3 81.9 %copy-start.5 = (f32[1024]{0:T(1024)S(1)}, f32[1024]{0:T(1024)}, u32[]{:S(2)}) copy-start(f32[1024]{0:T(1024)} %param.28) | copy-start | bytes 12292
  46.2 12.5 %all-to-all-start.2 = ((f32[48,8,128]{2,0,1:T(8,128)}), f32[48,8,128]{2,0,1:T(8,128)S(1)}, u32[]{:S(2)}, u32[]{:S(2)}) async-start(f32[48,8,128]{2,0,1:T(8,128)} %fusion.42), calls=%async_computation.2 | async-start | bytes 393216 | tf_op jit(solution)/shard_map/all_to_all | solution.py:23
  59.4 10.1 %all-to-all-start.3 = ((f32[8,48,128]{2,1,0:T(8,128)}), f32[8,48,128]{2,1,0:T(8,128)S(1)}, u32[]{:S(2)}, u32[]{:S(2)}) async-start(f32[8,48,128]{2,1,0:T(8,128)} %tile.15), calls=%async_computation.3 | async-start | bytes 393216 | tf_op jit(solution)/shard_map/all_to_all | solution.py:26
  70.8 14.1 %all-to-all-start.4 = ((bf16[16,48,128]{2,1,0:T(8,128)(2,1)}), bf16[16,48,128]{2,1,0:T(8,128)(2,1)S(1)}, u32[]{:S(2)}, u32[]{:S(2)}) async-start(bf16[16,48,128]{2,1,0:T(8,128)(2,1)} %tile.16), calls=%async_computation.4 | async-start | bytes 393216 | tf_op jit(solution)/shard_map/all_to_all | solution.py:32
  115.7 10.1 %all-to-all-start.7 = ((f32[8,48,128]{2,1,0:T(8,128)}), f32[8,48,128]{2,1,0:T(8,128)S(1)}, u32[]{:S(2)}, u32[]{:S(2)}) async-start(f32[8,48,128]{2,1,0:T(8,128)} %tile.17), calls=%async_computation.7 | async-start | bytes 393216 | tf_op jit(solution)/shard_map/all_to_all | solution.py:26

commit v6 on v2

--- a/solution.py
+++ b/solution.py
@@ -17,9 +17,12 @@
     parts = lax.psum(1, "head")
     rows, cols = partial_value.shape
     pieces = lax.all_to_all(partial_value, "head", 1, 0, tiled=True)
-    reduced = jnp.sum(pieces.reshape(parts, rows, cols // parts), axis=0)
-    spread = jnp.tile(reduced, (parts, 1))
-    return lax.all_to_all(spread, "head", 0, 1, tiled=True)
+    pieces = pieces.reshape(parts, rows, cols // parts)
+    reduced = pieces[0]
+    for part in range(1, parts):
+        reduced = reduced + pieces[part]
+    spread = jnp.broadcast_to(reduced[None], (parts, rows, cols // parts))
+    return lax.all_to_all(spread.reshape(parts * rows, cols // parts), "head", 0, 1, tiled=True)
 
 
 def gather_rows(block, axis_name):

time: 127 us -> 127 us (level)
    broadcast_in_dim x0 -> x2, local copies, waits for them, and re-layouts: none -> 1.37 us  [head_total(): spread = jnp.broadcast_to(reduced[None], (parts, rows, cols // parts))]
    another operation x2 -> x0, local copies, waits for them, and re-layouts: 1.37 us -> none  [head_total(): spread = jnp.tile(reduced, (parts, 1))]
where the time goes in v6:
time: 127 us; the launch traced here: 126 us
  starting transfers between devices  34.1 us (27%)
  waiting for transfers between devices  31.2 us (25%)
  matrix products  22.6 us (18%)
  blocking collectives  21.9 us (17%)
  local copies, waits for them, and re-layouts  8.08 us (6%)
  other arithmetic  6.91 us (5%)
    all_to_all x3, starting transfers between devices, gather_rows(): return lax.all_to_all(spread, axis_name, 0, 0, tiled=True)  19 us
    all_to_all x3, waiting for transfers between devices, gather_rows(): return lax.all_to_all(spread, axis_name, 0, 0, tiled=True)  15.9 us
    all_to_all x1, blocking collectives, head_total(): pieces = lax.all_to_all(partial_value, 'head', 1, 0, tiled=True)  11.7 us
    all_to_all x2, waiting for transfers between devices, head_total(): lax.all_to_all(spread.reshape(parts * rows, cols // parts), 'head', 0, 1,...  11 us
    all_to_all x1, blocking collectives, group_attention(): lax.all_to_all(placed.astype(jnp.bfloat16), 'req', 0, 0, tiled=True)  10.2 us
    all_to_all x2, starting transfers between devices, head_total(): lax.all_to_all(spread.reshape(parts * rows, cols // parts), 'head', 0, 1,...  8.49 us
    dot_general x1, matrix products, paged_attention(): jnp.einsum('phc,pnc->phn', query_blocks, stored, preferred_element_type=j...  6.88 us
    all_to_all x1, starting transfers between devices, head_total(): pieces = lax.all_to_all(partial_value, 'head', 1, 0, tiled=True)  6.62 us
  transfers between devices with their start and end apart: 6, of which 5 were waited for; matrix products, arithmetic and copies ran while one was open for 18% of the time, Pallas kernels for 0%

profile of v6, /device:TPU:1, one launch (start us, length us, event | category | flops | bytes accessed | tf_op | source)
XLA Modules:
  0.0 125.7 jit_solution(8180045302199200629)
XLA Ops:
  0.6 1.9 %tile.9 = bf16[16,192,128]{2,1,0:T(8,128)(2,1)} broadcast(bf16[192,128]{1,0:T(8,128)(2,1)} %bitcast.128), dimensions={1,2} | broadcast | bytes 835584 | tf_op jit(solution)/shard_map/tile | solution.py:30
  2.5 8.4 %all-to-all-start = ((bf16[16,192,128]{2,1,0:T(8,128)(2,1)}), bf16[16,192,128]{2,1,0:T(8,128)(2,1)S(1)}, u32[]{:S(2)}, u32[]{:S(2)}) async-start(bf16[16,192,128]{2,1,0:T(8,128)(2,1)} %tile.9), calls=%async_computation | async-start | bytes 1572864 | tf_op jit(solution)/shard_map/all_to_all | solution.py:31
  11.0 0.8 copy.56
  11.7 0.7 and_select_fusion.3
  12.5 0.2 fusion.13
  12.7 0.7 select_reduce_fusion.4
  13.5 0.8 copy.57
  14.2 0.2 select_reduce_fusion.1
  14.5 0.8 pad_maximum_fusion
  15.4 8.8 %all-to-all-done = bf16[16,192,128]{2,1,0:T(8,128)(2,1)S(1)} async-done(((bf16[16,192,128]{2,1,0:T(8,128)(2,1)}), bf16[16,192,128]{2,1,0:T(8,128)(2,1)S(1)}, u32[]{:S(2)}, u32[]{:S(2)}) %all-to-all-start) | async-done | bytes 786464 | tf_op jit(solution)/shard_map/all_to_all | solution.py:31
  24.2 1.0 tile.10
  25.2 3.7 %all-to-all-start.1 = ((bf16[16,192,128]{2,1,0:T(8,128)(2,1)}), bf16[16,192,128]{2,1,0:T(8,128)(2,1)S(1)}, u32[]{:S(2)}, u32[]{:S(2)}) async-start(bf16[16,192,128]{2,1,0:T(8,128)(2,1)} %tile.10), calls=%async_computation.1 | async-start | bytes 1572864 | tf_op jit(solution)/shard_map/all_to_all | solution.py:31
  29.0 0.2 convolution_convert_fusion.5
  29.1 0.2 convolution_convert_fusion
  29.4 6.9 %fusion.58 = (f32[160,2]{1,0:T(8,128)S(1)}, f32[160,2,256]{2,1,0:T(2,128)S(1)}) fusion(bf16[160,256,128]{2,1,0:T(8,128)(2,1)} %bitcast.108, pred[2,128]{1,0:T(4,128)(4,1)S(1)} %iota_compare_fusion.3, bf16[160,128]{1,0:T(8,128)(2,1)S(1)} %convolution_convert_fusion, pred[160,256]{1,0:T(8,128)(4,1)S(1)} %fusion.19), kind=kOutput, calls=%fused_computation.135 | convolution fusion | flops 21257920 | bytes 10896896 | tf_op jit(solution)/shard_map/phc,pnc->phn/dot_general | solution.py:70
  36.4 0.2 convert_multiply_fusion
  36.9 0.3 fusion.33
  37.2 0.6 fusion.55
  37.8 5.5 %fusion.7 = f32[160,128]{1,0:T(8,128)S(1)} fusion(bf16[160,256,128]{2,1,0:T(8,128)(2,1)} %bitcast.109, bf16[160,2,255]{2,1,0:T(2,128)(2,1)S(1)} %bitcast.121, pred[2,128]{1,0:T(4,128)(4,1)S(1)} %iota_compare_fusion.3), kind=kOutput, calls=%fused_computation.12 | convolution fusion | flops 21032960 | bytes 10731136 | tf_op jit(solution)/shard_map/phn,pnc->phc/dot_general | solution.py:92
  43.3 0.2 convolution_convert_fusion.3
  43.7 0.2 convolution_add_fusion.1
  44.0 0.2 fusion.9
  44.4 0.9 fusion.62
  45.3 6.6 %all-to-all-start.2 = ((f32[48,8,128]{2,0,1:T(8,128)}), f32[48,8,128]{2,0,1:T(8,128)S(1)}, u32[]{:S(2)}, u32[]{:S(2)}) async-start(f32[48,8,128]{2,0,1:T(8,128)} %fusion.62), calls=%async_computation.2 | async-start | bytes 393216 | tf_op jit(solution)/shard_map/all_to_all | solution.py:19
  52.0 1.1 reduce-window.6
  53.1 0.2 slice_reduce_fusion
  53.3 0.2 reduce-window.9
  53.5 4.3 %all-to-all-done.2 = f32[48,8,128]{2,0,1:T(8,128)S(1)} async-done(((f32[48,8,128]{2,0,1:T(8,128)}), f32[48,8,128]{2,0,1:T(8,128)S(1)}, u32[]{:S(2)}, u32[]{:S(2)}) %all-to-all-start.2) | async-done | bytes 196640 | tf_op jit(solution)/shard_map/all_to_all | solution.py:19
  57.8 0.7 broadcast_in_dim.232
  58.5 4.2 %all-to-all-start.3 = ((f32[8,48,128]{2,1,0:T(8,128)}), f32[8,48,128]{2,1,0:T(8,128)S(1)}, u32[]{:S(2)}, u32[]{:S(2)}) async-start(f32[8,48,128]{2,1,0:T(8,128)} %broadcast_in_dim.232), calls=%async_computation.3 | async-start | bytes 393216 | tf_op jit(solution)/shard_map/all_to_all | solution.py:25
  62.8 5.8 %all-to-all-done.3 = f32[8,48,128]{2,1,0:T(8,128)S(1)} async-done(((f32[8,48,128]{2,1,0:T(8,128)}), f32[8,48,128]{2,1,0:T(8,128)S(1)}, u32[]{:S(2)}, u32[]{:S(2)}) %all-to-all-start.3) | async-done | bytes 196640 | tf_op jit(solution)/shard_map/all_to_all | solution.py:25
  68.7 0.2 multiply_reduce_fusion.1
  69.0 0.2 convolution_convert_fusion.2
  69.2 0.7 tile.11
  69.9 6.9 %all-to-all-start.4 = ((bf16[16,48,128]{2,1,0:T(8,128)(2,1)}), bf16[16,48,128]{2,1,0:T(8,128)(2,1)S(1)}, u32[]{:S(2)}, u32[]{:S(2)}) async-start(bf16[16,48,128]{2,1,0:T(8,128)(2,1)} %tile.11), calls=%async_computation.4 | async-start | bytes 393216 | tf_op jit(solution)/shard_map/all_to_all | solution.py:31
  76.9 7.2 %all-to-all-done.4 = bf16[16,48,128]{2,1,0:T(8,128)(2,1)S(1)} async-done(((bf16[16,48,128]{2,1,0:T(8,128)(2,1)}), bf16[16,48,128]{2,1,0:T(8,128)(2,1)S(1)}, u32[]{:S(2)}, u32[]{:S(2)}) %all-to-all-start.4) | async-done | bytes 196640 | tf_op jit(solution)/shard_map/all_to_all | solution.py:31
  84.2 4.0 %fusion.59 = (f32[4,32]{1,0:T(4,128)S(1)}, bf16[4,32,4096]{2,1,0:T(8,128)(2,1)S(1)}) fusion(pred[4096]{0:T(1024)(128)(4,1)S(1)} %fusion.35, bf16[4,4096,128]{2,1,0:T(8,128)(2,1)} %bitcast.110, bf16[4,32,128]{2,1,0:T(8,128)(2,1)S(1)} %bitcast.129, pred[32,128]{1,0:T(8,128)(4,1)S(1)} %broadcast_in_dim.236), kind=kOutput, calls=%fused_computation.136 | convolution fusion | flops 137383936 | bytes 5284352 | tf_op jit(solution)/shard_map/sub | solution.py:129
  88.3 3.0 %convolution_divide_fusion = f32[4,32,128]{2,1,0:T(8,128)S(1)} fusion(bf16[4,4096,128]{2,1,0:T(8,128)(2,1)} %bitcast.111, bf16[4,32,4095]{2,1,0:T(8,128)(2,1)S(1)} %bitcast.118, f32[4,32]{1,0:T(4,128)S(1)} %get-tuple-element.28), kind=kOutput, calls=%fused_computation.13 | convolution fusion | flops 134234112 | bytes 5308672 | tf_op jit(solution)/shard_map/gmn,gnc->gmc/dot_general | solution.py:132
  91.3 0.3 fusion.6
  91.6 10.2 %all_to_all.86 = bf16[16,48,128]{2,1,0:T(8,128)(2,1)S(1)} all-to-all(bf16[16,48,128]{2,1,0:T(8,128)(2,1)S(1)} %bitcast.125), channel_id=1, replica_groups=mesh['req'=16,'head'=8] {'req'}, dimensions={0} | all-to-all | bytes 393216 | tf_op jit(solution)/shard_map/all_to_all | solution.py:139
  101.9 0.2 fusion.41
  102.1 11.7 %all_to_all.87 = f32[48,8,128]{2,0,1:T(8,128)S(1)} all-to-all(f32[48,8,128]{2,0,1:T(8,128)S(1)} %fusion.41), channel_id=1, replica_groups=mesh['req'=16,'head'=8] {'head'}, dimensions={1} | all-to-all | bytes 393216 | tf_op jit(solution)/shard_map/all_to_all | solution.py:19
  113.8 0.7 broadcast_in_dim.245
  114.5 4.2 %all-to-all-start.7 = ((f32[8,48,128]{2,1,0:T(8,128)}), f32[8,48,128]{2,1,0:T(8,128)S(1)}, u32[]{:S(2)}, u32[]{:S(2)}) async-start(f32[8,48,128]{2,1,0:T(8,128)} %broadcast_in_dim.245), calls=%async_computation.7 | async-start | bytes 393216 | tf_op jit(solution)/shard_map/all_to_all | solution.py:25
  118.7 0.6 copy.66
  119.4 5.2 %all-to-all-done.7 = f32[8,48,128]{2,1,0:T(8,128)S(1)} async-done(((f32[8,48,128]{2,1,0:T(8,128)}), f32[8,48,128]{2,1,0:T(8,128)S(1)}, u32[]{:S(2)}, u32[]{:S(2)}) %all-to-all-start.7) | async-done | bytes 196640 | tf_op jit(solution)/shard_map/all_to_all | solution.py:25
  124.8 0.2 multiply_reduce_fusion
  125.0 0.7 add_convert_fusion
  (56 shorter events, 2.2 us)
Async XLA Ops:
  0.6 28.3 %copy-start = (bf16[48,1024]{1,0:T(8,128)(2,1)S(1)}, bf16[48,1024]{1,0:T(8,128)(2,1)}, u32[]{:S(2)}) copy-start(bf16[48,1024]{1,0:T(8,128)(2,1)} %param.15) | copy-start | bytes 294916
  2.5 21.7 %all-to-all-start = ((bf16[16,192,128]{2,1,0:T(8,128)(2,1)}), bf16[16,192,128]{2,1,0:T(8,128)(2,1)S(1)}, u32[]{:S(2)}, u32[]{:S(2)}) async-start(bf16[16,192,128]{2,1,0:T(8,128)(2,1)} %tile.9), calls=%async_computation | async-start | bytes 1572864 | tf_op jit(solution)/shard_map/all_to_all | solution.py:31
  25.2 19.1 %all-to-all-start.1 = ((bf16[16,192,128]{2,1,0:T(8,128)(2,1)}), bf16[16,192,128]{2,1,0:T(8,128)(2,1)S(1)}, u32[]{:S(2)}, u32[]{:S(2)}) async-start(bf16[16,192,128]{2,1,0:T(8,128)(2,1)} %tile.10), calls=%async_computation.1 | async-start | bytes 1572864 | tf_op jit(solution)/shard_map/all_to_all | solution.py:31
  37.8 14.1 %copy-start.1 = (s32[768]{0:T(1024)S(1)}, s32[768]{0:T(1024)}, u32[]{:S(2)}) copy-start(s32[768]{0:T(1024)} %param.19) | copy-start | bytes 9220
  43.3 25.6 %copy-start.2 = (f32[1024]{0:T(1024)S(1)}, f32[1024]{0:T(1024)}, u32[]{:S(2)}) copy-start(f32[1024]{0:T(1024)} %param.27) | copy-start | bytes 12292
  43.3 25.6 %copy-start.3 = (f32[1024]{0:T(1024)S(1)}, f32[1024]{0:T(1024)}, u32[]{:S(2)}) copy-start(f32[1024]{0:T(1024)} %param.26) | copy-start | bytes 12292
  45.3 12.5 %all-to-all-start.2 = ((f32[48,8,128]{2,0,1:T(8,128)}), f32[48,8,128]{2,0,1:T(8,128)S(1)}, u32[]{:S(2)}, u32[]{:S(2)}) async-start(f32[48,8,128]{2,0,1:T(8,128)} %fusion.62), calls=%async_computation.2 | async-start | bytes 393216 | tf_op jit(solution)/shard_map/all_to_all | solution.py:19
  58.5 10.1 %all-to-all-start.3 = ((f32[8,48,128]{2,1,0:T(8,128)}), f32[8,48,128]{2,1,0:T(8,128)S(1)}, u32[]{:S(2)}, u32[]{:S(2)}) async-start(f32[8,48,128]{2,1,0:T(8,128)} %broadcast_in_dim.232), calls=%async_computation.3 | async-start | bytes 393216 | tf_op jit(solution)/shard_map/all_to_all | solution.py:25
  69.9 14.1 %all-to-all-start.4 = ((bf16[16,48,128]{2,1,0:T(8,128)(2,1)}), bf16[16,48,128]{2,1,0:T(8,128)(2,1)S(1)}, u32[]{:S(2)}, u32[]{:S(2)}) async-start(bf16[16,48,128]{2,1,0:T(8,128)(2,1)} %tile.11), calls=%async_computation.4 | async-start | bytes 393216 | tf_op jit(solution)/shard_map/all_to_all | solution.py:31
  88.3 36.7 %copy-start.4 = (f32[1024]{0:T(1024)S(1)}, f32[1024]{0:T(1024)}, u32[]{:S(2)}) copy-start(f32[1024]{0:T(1024)} %param.29) | copy-start | bytes 12292
  88.3 36.7 %copy-start.5 = (f32[1024]{0:T(1024)S(1)}, f32[1024]{0:T(1024)}, u32[]{:S(2)}) copy-start(f32[1024]{0:T(1024)} %param.28) | copy-start | bytes 12292
  114.5 10.1 %all-to-all-start.7 = ((f32[8,48,128]{2,1,0:T(8,128)}), f32[8,48,128]{2,1,0:T(8,128)S(1)}, u32[]{:S(2)}, u32[]{:S(2)}) async-start(f32[8,48,128]{2,1,0:T(8,128)} %broadcast_in_dim.245), calls=%async_computation.7 | async-start | bytes 393216 | tf_op jit(solution)/shard_map/all_to_all | solution.py:25

commit v7 on v6

--- a/solution.py
+++ b/solution.py
@@ -2,6 +2,7 @@
 import jax.numpy as jnp
 from jax import lax
 from jax.sharding import PartitionSpec as P
+
 
 HEAD_DIM = 64
 GMAX = 16
@@ -158,14 +159,14 @@
     cross_gain,
     cross_bias,
 ):
-    rows_here = tokens.shape[0]
-    width = tokens.shape[1]
     head_cols = kv_pool.shape[3]
     scale = HEAD_DIM ** (-0.5)
     in_rows = w_self_in.shape[0]
     first = gather_rows(w_self_in.transpose(1, 0, 2).reshape(-1, head_cols)[None], "req")
     rest = jnp.concatenate([w_cross_q, w_self_out.T, w_cross_out.T], axis=0)
-    rest = gather_rows(rest[None], "req")
+    parts = lax.psum(1, "req")
+    rest = jnp.tile(rest[None], (parts, 1, 1))
+    rest = lax.all_to_all(rest, "req", 0, 0, tiled=True)
     full_in = [first[:, k * in_rows : (k + 1) * in_rows].reshape(-1, head_cols) for k in range(3)]
     full_query = rest[:, :in_rows].reshape(-1, head_cols)
     full_out = rest[:, in_rows : 2 * in_rows].reshape(-1, head_cols)

time: 127 us -> 127 us (level)
    all_to_all x3 -> x2, starting transfers between devices: 19 us -> 15.3 us  [gather_rows(): return lax.all_to_all(spread, axis_name, 0, 0, tiled=True)]
    all_to_all x0 -> x1, starting transfers between devices: none -> 3.7 us  [on_device(): rest = lax.all_to_all(rest, 'req', 0, 0, tiled=True)]
    another operation x3 -> x2, local copies, waits for them, and re-layouts: 3.59 us -> 2.56 us  [gather_rows(): spread = jnp.tile(block, (parts,) + (1,) * (block.ndim - 1))]
    all_to_all x3 -> x2, waiting for transfers between devices: 15.9 us -> 15.9 us  [gather_rows(): return lax.all_to_all(spread, axis_name, 0, 0, tiled=True)]
where the time goes in v7:
time: 127 us; the launch traced here: 126 us
  starting transfers between devices  34.1 us (27%)
  waiting for transfers between devices  31.2 us (25%)
  matrix products  22.6 us (18%)
  blocking collectives  21.9 us (17%)
  local copies, waits for them, and re-layouts  8.08 us (6%)
  other arithmetic  6.91 us (5%)
    all_to_all x2, waiting for transfers between devices, gather_rows(): return lax.all_to_all(spread, axis_name, 0, 0, tiled=True)  15.9 us
    all_to_all x2, starting transfers between devices, gather_rows(): return lax.all_to_all(spread, axis_name, 0, 0, tiled=True)  15.3 us
    all_to_all x1, blocking collectives, head_total(): pieces = lax.all_to_all(partial_value, 'head', 1, 0, tiled=True)  11.7 us
    all_to_all x2, waiting for transfers between devices, head_total(): lax.all_to_all(spread.reshape(parts * rows, cols // parts), 'head', 0, 1,...  11 us
    all_to_all x1, blocking collectives, group_attention(): lax.all_to_all(placed.astype(jnp.bfloat16), 'req', 0, 0, tiled=True)  10.2 us
    all_to_all x2, starting transfers between devices, head_total(): lax.all_to_all(spread.reshape(parts * rows, cols // parts), 'head', 0, 1,...  8.49 us
    dot_general x1, matrix products, paged_attention(): jnp.einsum('phc,pnc->phn', query_blocks, stored, preferred_element_type=j...  6.88 us
    all_to_all x1, starting transfers between devices, head_total(): pieces = lax.all_to_all(partial_value, 'head', 1, 0, tiled=True)  6.62 us
  transfers between devices with their start and end apart: 6, of which 5 were waited for; matrix products, arithmetic and copies ran while one was open for 18% of the time, Pallas kernels for 0%

profile of v7, /device:TPU:1, one launch (start us, length us, event | category | flops | bytes accessed | tf_op | source)
XLA Modules:
  0.0 125.7 jit_solution(8180045302199200629)
XLA Ops:
  0.6 1.9 %tile.9 = bf16[16,192,128]{2,1,0:T(8,128)(2,1)} broadcast(bf16[192,128]{1,0:T(8,128)(2,1)} %bitcast.128), dimensions={1,2} | broadcast | bytes 835584 | tf_op jit(solution)/shard_map/tile | solution.py:31
  2.5 8.4 %all-to-all-start = ((bf16[16,192,128]{2,1,0:T(8,128)(2,1)}), bf16[16,192,128]{2,1,0:T(8,128)(2,1)S(1)}, u32[]{:S(2)}, u32[]{:S(2)}) async-start(bf16[16,192,128]{2,1,0:T(8,128)(2,1)} %tile.9), calls=%async_computation | async-start | bytes 1572864 | tf_op jit(solution)/shard_map/all_to_all | solution.py:32
  11.0 0.8 copy.56
  11.7 0.7 and_select_fusion.3
  12.5 0.2 fusion.13
  12.7 0.7 select_reduce_fusion.4
  13.5 0.8 copy.57
  14.2 0.2 select_reduce_fusion.1
  14.5 0.8 pad_maximum_fusion
  15.4 8.8 %all-to-all-done = bf16[16,192,128]{2,1,0:T(8,128)(2,1)S(1)} async-done(((bf16[16,192,128]{2,1,0:T(8,128)(2,1)}), bf16[16,192,128]{2,1,0:T(8,128)(2,1)S(1)}, u32[]{:S(2)}, u32[]{:S(2)}) %all-to-all-start) | async-done | bytes 786464 | tf_op jit(solution)/shard_map/all_to_all | solution.py:32
  24.2 1.0 tile.10
  25.2 3.7 %all-to-all-start.1 = ((bf16[16,192,128]{2,1,0:T(8,128)(2,1)}), bf16[16,192,128]{2,1,0:T(8,128)(2,1)S(1)}, u32[]{:S(2)}, u32[]{:S(2)}) async-start(bf16[16,192,128]{2,1,0:T(8,128)(2,1)} %tile.10), calls=%async_computation.1 | async-start | bytes 1572864 | tf_op jit(solution)/shard_map/all_to_all | solution.py:169
  29.0 0.2 convolution_convert_fusion.5
  29.1 0.2 convolution_convert_fusion
  29.4 6.9 %fusion.58 = (f32[160,2]{1,0:T(8,128)S(1)}, f32[160,2,256]{2,1,0:T(2,128)S(1)}) fusion(bf16[160,256,128]{2,1,0:T(8,128)(2,1)} %bitcast.108, pred[2,128]{1,0:T(4,128)(4,1)S(1)} %iota_compare_fusion.3, bf16[160,128]{1,0:T(8,128)(2,1)S(1)} %convolution_convert_fusion, pred[160,256]{1,0:T(8,128)(4,1)S(1)} %fusion.19), kind=kOutput, calls=%fused_computation.135 | convolution fusion | flops 21257920 | bytes 10896896 | tf_op jit(solution)/shard_map/phc,pnc->phn/dot_general | solution.py:71
  36.4 0.2 convert_multiply_fusion
  36.9 0.3 fusion.33
  37.2 0.6 fusion.55
  37.8 5.5 %fusion.7 = f32[160,128]{1,0:T(8,128)S(1)} fusion(bf16[160,256,128]{2,1,0:T(8,128)(2,1)} %bitcast.109, bf16[160,2,255]{2,1,0:T(2,128)(2,1)S(1)} %bitcast.121, pred[2,128]{1,0:T(4,128)(4,1)S(1)} %iota_compare_fusion.3), kind=kOutput, calls=%fused_computation.12 | convolution fusion | flops 21032960 | bytes 10731136 | tf_op jit(solution)/shard_map/phn,pnc->phc/dot_general | solution.py:93
  43.3 0.2 convolution_convert_fusion.3
  43.7 0.2 convolution_add_fusion.1
  44.0 0.2 fusion.9
  44.4 0.9 fusion.62
  45.3 6.6 %all-to-all-start.2 = ((f32[48,8,128]{2,0,1:T(8,128)}), f32[48,8,128]{2,0,1:T(8,128)S(1)}, u32[]{:S(2)}, u32[]{:S(2)}) async-start(f32[48,8,128]{2,0,1:T(8,128)} %fusion.62), calls=%async_computation.2 | async-start | bytes 393216 | tf_op jit(solution)/shard_map/all_to_all | solution.py:20
  52.0 1.1 reduce-window.6
  53.1 0.2 slice_reduce_fusion
  53.3 0.2 reduce-window.9
  53.5 4.3 %all-to-all-done.2 = f32[48,8,128]{2,0,1:T(8,128)S(1)} async-done(((f32[48,8,128]{2,0,1:T(8,128)}), f32[48,8,128]{2,0,1:T(8,128)S(1)}, u32[]{:S(2)}, u32[]{:S(2)}) %all-to-all-start.2) | async-done | bytes 196640 | tf_op jit(solution)/shard_map/all_to_all | solution.py:20
  57.8 0.7 broadcast_in_dim.232
  58.5 4.2 %all-to-all-start.3 = ((f32[8,48,128]{2,1,0:T(8,128)}), f32[8,48,128]{2,1,0:T(8,128)S(1)}, u32[]{:S(2)}, u32[]{:S(2)}) async-start(f32[8,48,128]{2,1,0:T(8,128)} %broadcast_in_dim.232), calls=%async_computation.3 | async-start | bytes 393216 | tf_op jit(solution)/shard_map/all_to_all | solution.py:26
  62.8 5.8 %all-to-all-done.3 = f32[8,48,128]{2,1,0:T(8,128)S(1)} async-done(((f32[8,48,128]{2,1,0:T(8,128)}), f32[8,48,128]{2,1,0:T(8,128)S(1)}, u32[]{:S(2)}, u32[]{:S(2)}) %all-to-all-start.3) | async-done | bytes 196640 | tf_op jit(solution)/shard_map/all_to_all | solution.py:26
  68.7 0.2 multiply_reduce_fusion.1
  69.0 0.2 convolution_convert_fusion.2
  69.2 0.7 tile.11
  69.9 6.9 %all-to-all-start.4 = ((bf16[16,48,128]{2,1,0:T(8,128)(2,1)}), bf16[16,48,128]{2,1,0:T(8,128)(2,1)S(1)}, u32[]{:S(2)}, u32[]{:S(2)}) async-start(bf16[16,48,128]{2,1,0:T(8,128)(2,1)} %tile.11), calls=%async_computation.4 | async-start | bytes 393216 | tf_op jit(solution)/shard_map/all_to_all | solution.py:32
  76.9 7.2 %all-to-all-done.4 = bf16[16,48,128]{2,1,0:T(8,128)(2,1)S(1)} async-done(((bf16[16,48,128]{2,1,0:T(8,128)(2,1)}), bf16[16,48,128]{2,1,0:T(8,128)(2,1)S(1)}, u32[]{:S(2)}, u32[]{:S(2)}) %all-to-all-start.4) | async-done | bytes 196640 | tf_op jit(solution)/shard_map/all_to_all | solution.py:32
  84.2 4.0 %fusion.59 = (f32[4,32]{1,0:T(4,128)S(1)}, bf16[4,32,4096]{2,1,0:T(8,128)(2,1)S(1)}) fusion(pred[4096]{0:T(1024)(128)(4,1)S(1)} %fusion.35, bf16[4,4096,128]{2,1,0:T(8,128)(2,1)} %bitcast.110, bf16[4,32,128]{2,1,0:T(8,128)(2,1)S(1)} %bitcast.129, pred[32,128]{1,0:T(8,128)(4,1)S(1)} %broadcast_in_dim.236), kind=kOutput, calls=%fused_computation.136 | convolution fusion | flops 137383936 | bytes 5284352 | tf_op jit(solution)/shard_map/sub | solution.py:130
  88.3 3.0 %convolution_divide_fusion = f32[4,32,128]{2,1,0:T(8,128)S(1)} fusion(bf16[4,4096,128]{2,1,0:T(8,128)(2,1)} %bitcast.111, bf16[4,32,4095]{2,1,0:T(8,128)(2,1)S(1)} %bitcast.118, f32[4,32]{1,0:T(4,128)S(1)} %get-tuple-element.28), kind=kOutput, calls=%fused_computation.13 | convolution fusion | flops 134234112 | bytes 5308672 | tf_op jit(solution)/shard_map/gmn,gnc->gmc/dot_general | solution.py:133
  91.3 0.3 fusion.6
  91.6 10.2 %all_to_all.86 = bf16[16,48,128]{2,1,0:T(8,128)(2,1)S(1)} all-to-all(bf16[16,48,128]{2,1,0:T(8,128)(2,1)S(1)} %bitcast.125), channel_id=1, replica_groups=mesh['req'=16,'head'=8] {'req'}, dimensions={0} | all-to-all | bytes 393216 | tf_op jit(solution)/shard_map/all_to_all | solution.py:140
  101.9 0.2 fusion.41
  102.1 11.7 %all_to_all.87 = f32[48,8,128]{2,0,1:T(8,128)S(1)} all-to-all(f32[48,8,128]{2,0,1:T(8,128)S(1)} %fusion.41), channel_id=1, replica_groups=mesh['req'=16,'head'=8] {'head'}, dimensions={1} | all-to-all | bytes 393216 | tf_op jit(solution)/shard_map/all_to_all | solution.py:20
  113.8 0.7 broadcast_in_dim.245
  114.5 4.2 %all-to-all-start.7 = ((f32[8,48,128]{2,1,0:T(8,128)}), f32[8,48,128]{2,1,0:T(8,128)S(1)}, u32[]{:S(2)}, u32[]{:S(2)}) async-start(f32[8,48,128]{2,1,0:T(8,128)} %broadcast_in_dim.245), calls=%async_computation.7 | async-start | bytes 393216 | tf_op jit(solution)/shard_map/all_to_all | solution.py:26
  118.7 0.6 copy.66
  119.4 5.2 %all-to-all-done.7 = f32[8,48,128]{2,1,0:T(8,128)S(1)} async-done(((f32[8,48,128]{2,1,0:T(8,128)}), f32[8,48,128]{2,1,0:T(8,128)S(1)}, u32[]{:S(2)}, u32[]{:S(2)}) %all-to-all-start.7) | async-done | bytes 196640 | tf_op jit(solution)/shard_map/all_to_all | solution.py:26
  124.8 0.2 multiply_reduce_fusion
  125.0 0.7 add_convert_fusion
  (56 shorter events, 2.2 us)
Async XLA Ops:
  0.6 28.3 %copy-start = (bf16[48,1024]{1,0:T(8,128)(2,1)S(1)}, bf16[48,1024]{1,0:T(8,128)(2,1)}, u32[]{:S(2)}) copy-start(bf16[48,1024]{1,0:T(8,128)(2,1)} %param.15) | copy-start | bytes 294916
  2.5 21.7 %all-to-all-start = ((bf16[16,192,128]{2,1,0:T(8,128)(2,1)}), bf16[16,192,128]{2,1,0:T(8,128)(2,1)S(1)}, u32[]{:S(2)}, u32[]{:S(2)}) async-start(bf16[16,192,128]{2,1,0:T(8,128)(2,1)} %tile.9), calls=%async_computation | async-start | bytes 1572864 | tf_op jit(solution)/shard_map/all_to_all | solution.py:32
  25.2 19.1 %all-to-all-start.1 = ((bf16[16,192,128]{2,1,0:T(8,128)(2,1)}), bf16[16,192,128]{2,1,0:T(8,128)(2,1)S(1)}, u32[]{:S(2)}, u32[]{:S(2)}) async-start(bf16[16,192,128]{2,1,0:T(8,128)(2,1)} %tile.10), calls=%async_computation.1 | async-start | bytes 1572864 | tf_op jit(solution)/shard_map/all_to_all | solution.py:169
  37.8 14.1 %copy-start.1 = (s32[768]{0:T(1024)S(1)}, s32[768]{0:T(1024)}, u32[]{:S(2)}) copy-start(s32[768]{0:T(1024)} %param.19) | copy-start | bytes 9220
  43.3 25.6 %copy-start.2 = (f32[1024]{0:T(1024)S(1)}, f32[1024]{0:T(1024)}, u32[]{:S(2)}) copy-start(f32[1024]{0:T(1024)} %param.27) | copy-start | bytes 12292
  43.3 25.6 %copy-start.3 = (f32[1024]{0:T(1024)S(1)}, f32[1024]{0:T(1024)}, u32[]{:S(2)}) copy-start(f32[1024]{0:T(1024)} %param.26) | copy-start | bytes 12292
  45.3 12.5 %all-to-all-start.2 = ((f32[48,8,128]{2,0,1:T(8,128)}), f32[48,8,128]{2,0,1:T(8,128)S(1)}, u32[]{:S(2)}, u32[]{:S(2)}) async-start(f32[48,8,128]{2,0,1:T(8,128)} %fusion.62), calls=%async_computation.2 | async-start | bytes 393216 | tf_op jit(solution)/shard_map/all_to_all | solution.py:20
  58.5 10.1 %all-to-all-start.3 = ((f32[8,48,128]{2,1,0:T(8,128)}), f32[8,48,128]{2,1,0:T(8,128)S(1)}, u32[]{:S(2)}, u32[]{:S(2)}) async-start(f32[8,48,128]{2,1,0:T(8,128)} %broadcast_in_dim.232), calls=%async_computation.3 | async-start | bytes 393216 | tf_op jit(solution)/shard_map/all_to_all | solution.py:26
  69.9 14.1 %all-to-all-start.4 = ((bf16[16,48,128]{2,1,0:T(8,128)(2,1)}), bf16[16,48,128]{2,1,0:T(8,128)(2,1)S(1)}, u32[]{:S(2)}, u32[]{:S(2)}) async-start(bf16[16,48,128]{2,1,0:T(8,128)(2,1)} %tile.11), calls=%async_computation.4 | async-start | bytes 393216 | tf_op jit(solution)/shard_map/all_to_all | solution.py:32
  88.3 36.7 %copy-start.4 = (f32[1024]{0:T(1024)S(1)}, f32[1024]{0:T(1024)}, u32[]{:S(2)}) copy-start(f32[1024]{0:T(1024)} %param.29) | copy-start | bytes 12292
  88.3 36.7 %copy-start.5 = (f32[1024]{0:T(1024)S(1)}, f32[1024]{0:T(1024)}, u32[]{:S(2)}) copy-start(f32[1024]{0:T(1024)} %param.28) | copy-start | bytes 12292
  114.5 10.1 %all-to-all-start.7 = ((f32[8,48,128]{2,1,0:T(8,128)}), f32[8,48,128]{2,1,0:T(8,128)S(1)}, u32[]{:S(2)}, u32[]{:S(2)}) async-start(f32[8,48,128]{2,1,0:T(8,128)} %broadcast_in_dim.245), calls=%async_computation.7 | async-start | bytes 393216 | tf_op jit(solution)/shard_map/all_to_all | solution.py:26

commit v8 on v7

--- a/solution.py
+++ b/solution.py
@@ -114,13 +114,19 @@
         member_rank[:, None, :] == jnp.arange(GMAX, dtype=jnp.int32)[None, :, None]
     )
     picker = picker.astype(jnp.bfloat16)
+    lane_head = jnp.arange(head_cols, dtype=jnp.int32) // HEAD_DIM
+    head_mask = lane_head[None, :] == jnp.arange(heads_here, dtype=jnp.int32)[:, None]
+    block_mask = jnp.broadcast_to(head_mask, (groups_here, GMAX, heads_here, head_cols))
+    block_mask = lax.optimization_barrier(block_mask)
+    lane = jnp.arange(2 * positions, dtype=jnp.int32)
+    is_key = (lane % 2 == 0)[None, None, :]
     group_query = jnp.einsum("gkr,rc->gkc", picker, every_query, preferred_element_type=jnp.float32)
     group_query = group_query.astype(jnp.bfloat16)
-    query_blocks, head_mask = head_blocks(group_query, head_cols)
+    query_blocks = jnp.where(
+        block_mask, group_query[..., None, :], jnp.zeros((), group_query.dtype)
+    )
     query_blocks = query_blocks.reshape(groups_here, GMAX * heads_here, head_cols)
     stored = enc_kv.reshape(groups_here, 2 * positions, head_cols)
-    lane = jnp.arange(2 * positions, dtype=jnp.int32)
-    is_key = (lane % 2 == 0)[None, None, :]
     scores = (
         jnp.einsum("gmc,gnc->gmn", query_blocks, stored, preferred_element_type=jnp.float32)
         * scale

time: 127 us -> 127 us (level)
  no operation moved by 1% of the time
where the time goes in v8:
time: 127 us; the launch traced here: 126 us
  starting transfers between devices  34.1 us (27%)
  waiting for transfers between devices  31.2 us (25%)
  matrix products  22.6 us (18%)
  blocking collectives  21.9 us (17%)
  local copies, waits for them, and re-layouts  8.05 us (6%)
  other arithmetic  6.98 us (5%)
    all_to_all x2, waiting for transfers between devices, gather_rows(): return lax.all_to_all(spread, axis_name, 0, 0, tiled=True)  15.9 us
    all_to_all x2, starting transfers between devices, gather_rows(): return lax.all_to_all(spread, axis_name, 0, 0, tiled=True)  15.3 us
    all_to_all x1, blocking collectives, head_total(): pieces = lax.all_to_all(partial_value, 'head', 1, 0, tiled=True)  11.7 us
    all_to_all x2, waiting for transfers between devices, head_total(): lax.all_to_all(spread.reshape(parts * rows, cols // parts), 'head', 0, 1,...  11 us
    all_to_all x1, blocking collectives, group_attention(): lax.all_to_all(placed.astype(jnp.bfloat16), 'req', 0, 0, tiled=True)  10.2 us
    all_to_all x2, starting transfers between devices, head_total(): lax.all_to_all(spread.reshape(parts * rows, cols // parts), 'head', 0, 1,...  8.49 us
    dot_general x1, matrix products, paged_attention(): jnp.einsum('phc,pnc->phn', query_blocks, stored, preferred_element_type=j...  6.88 us
    all_to_all x1, starting transfers between devices, head_total(): pieces = lax.all_to_all(partial_value, 'head', 1, 0, tiled=True)  6.62 us
  transfers between devices with their start and end apart: 6, of which 5 were waited for; matrix products, arithmetic and copies ran while one was open for 18% of the time, Pallas kernels for 0%

profile of v8, /device:TPU:1, one launch (start us, length us, event | category | flops | bytes accessed | tf_op | source)
XLA Modules:
  0.0 125.8 jit_solution(4805902508101998454)
XLA Ops:
  0.6 1.9 %tile.9 = bf16[16,192,128]{2,1,0:T(8,128)(2,1)} broadcast(bf16[192,128]{1,0:T(8,128)(2,1)} %bitcast.129), dimensions={1,2} | broadcast | bytes 835584 | tf_op jit(solution)/shard_map/tile | solution.py:31
  2.5 8.4 %all-to-all-start = ((bf16[16,192,128]{2,1,0:T(8,128)(2,1)}), bf16[16,192,128]{2,1,0:T(8,128)(2,1)S(1)}, u32[]{:S(2)}, u32[]{:S(2)}) async-start(bf16[16,192,128]{2,1,0:T(8,128)(2,1)} %tile.9), calls=%async_computation | async-start | bytes 1572864 | tf_op jit(solution)/shard_map/all_to_all | solution.py:32
  11.0 0.8 copy.56
  11.7 0.7 and_select_fusion.3
  12.5 0.2 fusion.13
  12.7 0.7 select_reduce_fusion.4
  13.5 0.8 copy.57
  14.2 0.2 select_reduce_fusion.1
  14.5 0.8 pad_maximum_fusion
  15.4 8.8 %all-to-all-done = bf16[16,192,128]{2,1,0:T(8,128)(2,1)S(1)} async-done(((bf16[16,192,128]{2,1,0:T(8,128)(2,1)}), bf16[16,192,128]{2,1,0:T(8,128)(2,1)S(1)}, u32[]{:S(2)}, u32[]{:S(2)}) %all-to-all-start) | async-done | bytes 786464 | tf_op jit(solution)/shard_map/all_to_all | solution.py:32
  24.2 1.0 tile.10
  25.2 3.7 %all-to-all-start.1 = ((bf16[16,192,128]{2,1,0:T(8,128)(2,1)}), bf16[16,192,128]{2,1,0:T(8,128)(2,1)S(1)}, u32[]{:S(2)}, u32[]{:S(2)}) async-start(bf16[16,192,128]{2,1,0:T(8,128)(2,1)} %tile.10), calls=%async_computation.1 | async-start | bytes 1572864 | tf_op jit(solution)/shard_map/all_to_all | solution.py:175
  29.0 0.2 convolution_convert_fusion.5
  29.1 0.2 convolution_convert_fusion
  29.4 6.9 %fusion.54 = (f32[160,2]{1,0:T(8,128)S(1)}, f32[160,2,256]{2,1,0:T(2,128)S(1)}) fusion(bf16[160,256,128]{2,1,0:T(8,128)(2,1)} %bitcast.109, pred[2,128]{1,0:T(4,128)(4,1)S(1)} %iota_compare_fusion.3, bf16[160,128]{1,0:T(8,128)(2,1)S(1)} %convolution_convert_fusion, pred[160,256]{1,0:T(8,128)(4,1)S(1)} %fusion.19), kind=kOutput, calls=%fused_computation.132 | convolution fusion | flops 21257920 | bytes 10896896 | tf_op jit(solution)/shard_map/phc,pnc->phn/dot_general | solution.py:71
  36.4 0.2 convert_multiply_fusion
  36.9 0.3 fusion.31
  37.2 0.6 fusion.51
  37.8 5.5 %fusion.7 = f32[160,128]{1,0:T(8,128)S(1)} fusion(bf16[160,256,128]{2,1,0:T(8,128)(2,1)} %bitcast.110, bf16[160,2,255]{2,1,0:T(2,128)(2,1)S(1)} %bitcast.122, pred[2,128]{1,0:T(4,128)(4,1)S(1)} %iota_compare_fusion.3), kind=kOutput, calls=%fused_computation.12 | convolution fusion | flops 21032960 | bytes 10731136 | tf_op jit(solution)/shard_map/phn,pnc->phc/dot_general | solution.py:93
  43.3 0.2 convolution_convert_fusion.3
  43.7 0.2 convolution_add_fusion.1
  44.0 0.2 fusion.9
  44.4 0.9 fusion.56
  45.3 6.6 %all-to-all-start.2 = ((f32[48,8,128]{2,0,1:T(8,128)}), f32[48,8,128]{2,0,1:T(8,128)S(1)}, u32[]{:S(2)}, u32[]{:S(2)}) async-start(f32[48,8,128]{2,0,1:T(8,128)} %fusion.56), calls=%async_computation.2 | async-start | bytes 393216 | tf_op jit(solution)/shard_map/all_to_all | solution.py:20
  52.0 1.1 reduce-window.6
  53.1 0.2 slice_reduce_fusion
  53.3 0.2 reduce-window.9
  53.5 4.3 %all-to-all-done.2 = f32[48,8,128]{2,0,1:T(8,128)S(1)} async-done(((f32[48,8,128]{2,0,1:T(8,128)}), f32[48,8,128]{2,0,1:T(8,128)S(1)}, u32[]{:S(2)}, u32[]{:S(2)}) %all-to-all-start.2) | async-done | bytes 196640 | tf_op jit(solution)/shard_map/all_to_all | solution.py:20
  57.8 0.7 broadcast_in_dim.225
  58.5 4.2 %all-to-all-start.3 = ((f32[8,48,128]{2,1,0:T(8,128)}), f32[8,48,128]{2,1,0:T(8,128)S(1)}, u32[]{:S(2)}, u32[]{:S(2)}) async-start(f32[8,48,128]{2,1,0:T(8,128)} %broadcast_in_dim.225), calls=%async_computation.3 | async-start | bytes 393216 | tf_op jit(solution)/shard_map/all_to_all | solution.py:26
  62.8 5.8 %all-to-all-done.3 = f32[8,48,128]{2,1,0:T(8,128)S(1)} async-done(((f32[8,48,128]{2,1,0:T(8,128)}), f32[8,48,128]{2,1,0:T(8,128)S(1)}, u32[]{:S(2)}, u32[]{:S(2)}) %all-to-all-start.3) | async-done | bytes 196640 | tf_op jit(solution)/shard_map/all_to_all | solution.py:26
  68.7 0.2 multiply_reduce_fusion.1
  69.0 0.2 convolution_convert_fusion.2
  69.2 0.7 tile.11
  69.9 6.9 %all-to-all-start.4 = ((bf16[16,48,128]{2,1,0:T(8,128)(2,1)}), bf16[16,48,128]{2,1,0:T(8,128)(2,1)S(1)}, u32[]{:S(2)}, u32[]{:S(2)}) async-start(bf16[16,48,128]{2,1,0:T(8,128)(2,1)} %tile.11), calls=%async_computation.4 | async-start | bytes 393216 | tf_op jit(solution)/shard_map/all_to_all | solution.py:32
  76.9 7.2 %all-to-all-done.4 = bf16[16,48,128]{2,1,0:T(8,128)(2,1)S(1)} async-done(((bf16[16,48,128]{2,1,0:T(8,128)(2,1)}), bf16[16,48,128]{2,1,0:T(8,128)(2,1)S(1)}, u32[]{:S(2)}, u32[]{:S(2)}) %all-to-all-start.4) | async-done | bytes 196640 | tf_op jit(solution)/shard_map/all_to_all | solution.py:32
  84.3 4.0 %fusion.55 = (f32[4,32]{1,0:T(4,128)S(1)}, bf16[4,32,4096]{2,1,0:T(8,128)(2,1)S(1)}) fusion(pred[4096]{0:T(1024)(128)(4,1)S(1)} %fusion.33, bf16[4,32,128]{2,1,0:T(8,128)(2,1)S(1)} %bitcast.130, bf16[4,4096,128]{2,1,0:T(8,128)(2,1)} %bitcast.111), kind=kOutput, calls=%fused_computation.133 | convolution fusion | flops 137367552 | bytes 5280256 | tf_op jit(solution)/shard_map/sub | solution.py:136
  88.3 3.0 %convolution_divide_fusion = f32[4,32,128]{2,1,0:T(8,128)S(1)} fusion(bf16[4,4096,128]{2,1,0:T(8,128)(2,1)} %bitcast.112, bf16[4,32,4095]{2,1,0:T(8,128)(2,1)S(1)} %bitcast.119, f32[4,32]{1,0:T(4,128)S(1)} %get-tuple-element.28), kind=kOutput, calls=%fused_computation.13 | convolution fusion | flops 134234112 | bytes 5308672 | tf_op jit(solution)/shard_map/gmn,gnc->gmc/dot_general | solution.py:139
  91.4 0.3 fusion.6
  91.7 10.2 %all_to_all.86 = bf16[16,48,128]{2,1,0:T(8,128)(2,1)S(1)} all-to-all(bf16[16,48,128]{2,1,0:T(8,128)(2,1)S(1)} %bitcast.126), channel_id=1, replica_groups=mesh['req'=16,'head'=8] {'req'}, dimensions={0} | all-to-all | bytes 393216 | tf_op jit(solution)/shard_map/all_to_all | solution.py:146
  101.9 0.2 fusion.38
  102.1 11.7 %all_to_all.87 = f32[48,8,128]{2,0,1:T(8,128)S(1)} all-to-all(f32[48,8,128]{2,0,1:T(8,128)S(1)} %fusion.38), channel_id=1, replica_groups=mesh['req'=16,'head'=8] {'head'}, dimensions={1} | all-to-all | bytes 393216 | tf_op jit(solution)/shard_map/all_to_all | solution.py:20
  113.9 0.7 broadcast_in_dim.234
  114.5 4.2 %all-to-all-start.7 = ((f32[8,48,128]{2,1,0:T(8,128)}), f32[8,48,128]{2,1,0:T(8,128)S(1)}, u32[]{:S(2)}, u32[]{:S(2)}) async-start(f32[8,48,128]{2,1,0:T(8,128)} %broadcast_in_dim.234), calls=%async_computation.7 | async-start | bytes 393216 | tf_op jit(solution)/shard_map/all_to_all | solution.py:26
  118.8 0.6 copy.66
  119.4 5.2 %all-to-all-done.7 = f32[8,48,128]{2,1,0:T(8,128)S(1)} async-done(((f32[8,48,128]{2,1,0:T(8,128)}), f32[8,48,128]{2,1,0:T(8,128)S(1)}, u32[]{:S(2)}, u32[]{:S(2)}) %all-to-all-start.7) | async-done | bytes 196640 | tf_op jit(solution)/shard_map/all_to_all | solution.py:26
  124.8 0.2 multiply_reduce_fusion
  125.0 0.7 add_convert_fusion
  (55 shorter events, 2.2 us)
Async XLA Ops:
  0.6 28.3 %copy-start = (bf16[48,1024]{1,0:T(8,128)(2,1)S(1)}, bf16[48,1024]{1,0:T(8,128)(2,1)}, u32[]{:S(2)}) copy-start(bf16[48,1024]{1,0:T(8,128)(2,1)} %param.15) | copy-start | bytes 294916
  2.5 21.7 %all-to-all-start = ((bf16[16,192,128]{2,1,0:T(8,128)(2,1)}), bf16[16,192,128]{2,1,0:T(8,128)(2,1)S(1)}, u32[]{:S(2)}, u32[]{:S(2)}) async-start(bf16[16,192,128]{2,1,0:T(8,128)(2,1)} %tile.9), calls=%async_computation | async-start | bytes 1572864 | tf_op jit(solution)/shard_map/all_to_all | solution.py:32
  25.2 19.1 %all-to-all-start.1 = ((bf16[16,192,128]{2,1,0:T(8,128)(2,1)}), bf16[16,192,128]{2,1,0:T(8,128)(2,1)S(1)}, u32[]{:S(2)}, u32[]{:S(2)}) async-start(bf16[16,192,128]{2,1,0:T(8,128)(2,1)} %tile.10), calls=%async_computation.1 | async-start | bytes 1572864 | tf_op jit(solution)/shard_map/all_to_all | solution.py:175
  37.8 14.1 %copy-start.1 = (s32[768]{0:T(1024)S(1)}, s32[768]{0:T(1024)}, u32[]{:S(2)}) copy-start(s32[768]{0:T(1024)} %param.19) | copy-start | bytes 9220
  43.3 25.6 %copy-start.2 = (f32[1024]{0:T(1024)S(1)}, f32[1024]{0:T(1024)}, u32[]{:S(2)}) copy-start(f32[1024]{0:T(1024)} %param.27) | copy-start | bytes 12292
  43.3 25.6 %copy-start.3 = (f32[1024]{0:T(1024)S(1)}, f32[1024]{0:T(1024)}, u32[]{:S(2)}) copy-start(f32[1024]{0:T(1024)} %param.26) | copy-start | bytes 12292
  45.3 12.5 %all-to-all-start.2 = ((f32[48,8,128]{2,0,1:T(8,128)}), f32[48,8,128]{2,0,1:T(8,128)S(1)}, u32[]{:S(2)}, u32[]{:S(2)}) async-start(f32[48,8,128]{2,0,1:T(8,128)} %fusion.56), calls=%async_computation.2 | async-start | bytes 393216 | tf_op jit(solution)/shard_map/all_to_all | solution.py:20
  58.5 10.1 %all-to-all-start.3 = ((f32[8,48,128]{2,1,0:T(8,128)}), f32[8,48,128]{2,1,0:T(8,128)S(1)}, u32[]{:S(2)}, u32[]{:S(2)}) async-start(f32[8,48,128]{2,1,0:T(8,128)} %broadcast_in_dim.225), calls=%async_computation.3 | async-start | bytes 393216 | tf_op jit(solution)/shard_map/all_to_all | solution.py:26
  69.9 14.1 %all-to-all-start.4 = ((bf16[16,48,128]{2,1,0:T(8,128)(2,1)}), bf16[16,48,128]{2,1,0:T(8,128)(2,1)S(1)}, u32[]{:S(2)}, u32[]{:S(2)}) async-start(bf16[16,48,128]{2,1,0:T(8,128)(2,1)} %tile.11), calls=%async_computation.4 | async-start | bytes 393216 | tf_op jit(solution)/shard_map/all_to_all | solution.py:32
  88.3 36.7 %copy-start.4 = (f32[1024]{0:T(1024)S(1)}, f32[1024]{0:T(1024)}, u32[]{:S(2)}) copy-start(f32[1024]{0:T(1024)} %param.29) | copy-start | bytes 12292
  88.3 36.7 %copy-start.5 = (f32[1024]{0:T(1024)S(1)}, f32[1024]{0:T(1024)}, u32[]{:S(2)}) copy-start(f32[1024]{0:T(1024)} %param.28) | copy-start | bytes 12292
  114.5 10.1 %all-to-all-start.7 = ((f32[8,48,128]{2,1,0:T(8,128)}), f32[8,48,128]{2,1,0:T(8,128)S(1)}, u32[]{:S(2)}, u32[]{:S(2)}) async-start(f32[8,48,128]{2,1,0:T(8,128)} %broadcast_in_dim.234), calls=%async_computation.7 | async-start | bytes 393216 | tf_op jit(solution)/shard_map/all_to_all | solution.py:26

commit v9 on v8

--- a/solution.py
+++ b/solution.py
@@ -44,7 +44,9 @@
     return jnp.concatenate([zero, weights[..., :-1]], axis=-1)
 
 
-def paged_attention(query, new_key, new_value, cache_len, page_table, page_live, kv_pool, scale):
+def paged_attention(
+    query, new_key, new_value, cache_len, page_table, page_live, kv_pool, scale, rider
+):
     pages_here, page_rows, _, head_cols = kv_pool.shape
     heads_here = head_cols // HEAD_DIM
     rows_here = query.shape[0]
@@ -71,6 +73,7 @@
         jnp.einsum("phc,pnc->phn", query_blocks, stored, preferred_element_type=jnp.float32)
         * scale
     )
+    scores, rider = lax.optimization_barrier((scores, rider))
     scores = jnp.where(counted[:, None, :], scores, -1e30)
     q_heads = query.astype(jnp.float32).reshape(rows_here, heads_here, HEAD_DIM)
     new_score = (
@@ -100,7 +103,8 @@
         rows_here, heads_here, HEAD_DIM
     )
     summed = summed.reshape(rows_here, heads_here, HEAD_DIM) + own_term
-    return (summed / total[:, :, None]).reshape(rows_here, head_cols).astype(jnp.bfloat16)
+    context = (summed / total[:, :, None]).reshape(rows_here, head_cols).astype(jnp.bfloat16)
+    return context, rider
 
 
 def group_attention(cross_query, group_of, enc_kv, scale):
@@ -172,18 +176,18 @@
     rest = jnp.concatenate([w_cross_q, w_self_out.T, w_cross_out.T], axis=0)
     parts = lax.psum(1, "req")
     rest = jnp.tile(rest[None], (parts, 1, 1))
-    rest = lax.all_to_all(rest, "req", 0, 0, tiled=True)
     full_in = [first[:, k * in_rows : (k + 1) * in_rows].reshape(-1, head_cols) for k in range(3)]
-    full_query = rest[:, :in_rows].reshape(-1, head_cols)
-    full_out = rest[:, in_rows : 2 * in_rows].reshape(-1, head_cols)
-    full_cross = rest[:, 2 * in_rows :].reshape(-1, head_cols)
     contract_cols = (((1,), (1,)), ((), ()))
     qkv = jnp.stack(
         [jnp.dot(tokens, part, preferred_element_type=jnp.float32) for part in full_in], axis=1
     ).astype(jnp.bfloat16)
-    self_ctx = paged_attention(
-        qkv[:, 0], qkv[:, 1], qkv[:, 2], cache_len, page_table, page_live, kv_pool, scale
-    )
+    self_ctx, rest = paged_attention(
+        qkv[:, 0], qkv[:, 1], qkv[:, 2], cache_len, page_table, page_live, kv_pool, scale, rest
+    )
+    rest = lax.all_to_all(rest, "req", 0, 0, tiled=True)
+    full_query = rest[:, :in_rows].reshape(-1, head_cols)
+    full_out = rest[:, in_rows : 2 * in_rows].reshape(-1, head_cols)
+    full_cross = rest[:, 2 * in_rows :].reshape(-1, head_cols)
     self_proj = head_total(
         lax.dot_general(self_ctx, full_out, contract_cols, preferred_element_type=jnp.float32)
     )

time: 127 us -> 136 us (1.071)
  waiting for transfers between devices: 31.2 us -> 42.5 us
  starting transfers between devices: 34.1 us -> 31.7 us
    all_to_all x1, waiting for transfers between devices: 0.01 us -> 11.4 us  [on_device(): rest = lax.all_to_all(rest, 'req', 0, 0, tiled=True)]
    all_to_all x2, starting transfers between devices: 15.3 us -> 11.9 us  [gather_rows(): return lax.all_to_all(spread, axis_name, 0, 0, tiled=True)]
  transfers between devices with their start and end apart: 6 -> 6, of which waited for: 5 -> 6; matrix products, arithmetic and copies ran while one was open for 18% -> 6% of each run, Pallas kernels for 0% -> 0%
where the time goes in v9:
time: 136 us; the launch traced here: 135 us
  waiting for transfers between devices  42.5 us (31%)
  starting transfers between devices  31.7 us (23%)
  matrix products  22.5 us (17%)
  blocking collectives  21.7 us (16%)
  local copies, waits for them, and re-layouts  8.05 us (6%)
  other arithmetic  7.48 us (6%)
    all_to_all x2, waiting for transfers between devices, gather_rows(): return lax.all_to_all(spread, axis_name, 0, 0, tiled=True)  15.8 us
    all_to_all x2, starting transfers between devices, gather_rows(): return lax.all_to_all(spread, axis_name, 0, 0, tiled=True)  11.9 us
    all_to_all x1, blocking collectives, head_total(): pieces = lax.all_to_all(partial_value, 'head', 1, 0, tiled=True)  11.5 us
    all_to_all x1, waiting for transfers between devices, on_device(): rest = lax.all_to_all(rest, 'req', 0, 0, tiled=True)  11.4 us
    all_to_all x2, waiting for transfers between devices, head_total(): lax.all_to_all(spread.reshape(parts * rows, cols // parts), 'head', 0, 1,...  11 us
    all_to_all x1, blocking collectives, group_attention(): lax.all_to_all(placed.astype(jnp.bfloat16), 'req', 0, 0, tiled=True)  10.2 us
    all_to_all x2, starting transfers between devices, head_total(): lax.all_to_all(spread.reshape(parts * rows, cols // parts), 'head', 0, 1,...  8.49 us
    all_to_all x1, starting transfers between devices, head_total(): pieces = lax.all_to_all(partial_value, 'head', 1, 0, tiled=True)  7.39 us
  transfers between devices with their start and end apart: 6, of which 6 were waited for; matrix products, arithmetic and copies ran while one was open for 6% of the time, Pallas kernels for 0%

profile of v9, /device:TPU:1, one launch (start us, length us, event | category | flops | bytes accessed | tf_op | source)
XLA Modules:
  0.0 134.9 jit_solution(11532136411349428031)
XLA Ops:
  0.6 1.9 %tile.9 = bf16[16,192,128]{2,1,0:T(8,128)(2,1)} broadcast(bf16[192,128]{1,0:T(8,128)(2,1)} %bitcast.129), dimensions={1,2} | broadcast | bytes 835584 | tf_op jit(solution)/shard_map/tile | solution.py:31
  2.5 8.4 %all-to-all-start = ((bf16[16,192,128]{2,1,0:T(8,128)(2,1)}), bf16[16,192,128]{2,1,0:T(8,128)(2,1)S(1)}, u32[]{:S(2)}, u32[]{:S(2)}) async-start(bf16[16,192,128]{2,1,0:T(8,128)(2,1)} %tile.9), calls=%async_computation | async-start | bytes 1572864 | tf_op jit(solution)/shard_map/all_to_all | solution.py:32
  11.0 0.8 copy.56
  11.7 0.7 and_select_fusion.3
  12.5 0.2 fusion.12
  12.7 0.7 select_reduce_fusion.4
  13.5 0.8 copy.57
  14.2 0.2 select_reduce_fusion.1
  14.5 0.8 pad_maximum_fusion
  15.4 8.8 %all-to-all-done = bf16[16,192,128]{2,1,0:T(8,128)(2,1)S(1)} async-done(((bf16[16,192,128]{2,1,0:T(8,128)(2,1)}), bf16[16,192,128]{2,1,0:T(8,128)(2,1)S(1)}, u32[]{:S(2)}, u32[]{:S(2)}) %all-to-all-start) | async-done | bytes 786464 | tf_op jit(solution)/shard_map/all_to_all | solution.py:32
  24.4 0.2 convolution_convert_fusion
  24.6 6.8 %convolution_multiply_fusion.1 = f32[160,2,256]{2,1,0:T(2,128)S(1)} fusion(bf16[160,256,128]{2,1,0:T(8,128)(2,1)} %bitcast.109, pred[2,128]{1,0:T(4,128)(4,1)S(1)} %iota_compare_fusion.3, bf16[160,128]{1,0:T(8,128)(2,1)S(1)} %convolution_convert_fusion), kind=kOutput, calls=%fused_computation.8 | convolution fusion | flops 21094400 | bytes 10854656 | tf_op jit(solution)/shard_map/phc,pnc->phn/dot_general | solution.py:73
  31.4 1.0 tile.10
  32.5 0.3 fusion.13
  33.0 0.2 convert_multiply_fusion
  33.5 0.3 fusion.31
  33.7 0.7 fusion.51
  34.5 5.5 %fusion.6 = f32[160,128]{1,0:T(8,128)S(1)} fusion(bf16[160,256,128]{2,1,0:T(8,128)(2,1)} %bitcast.110, bf16[160,2,255]{2,1,0:T(2,128)(2,1)S(1)} %bitcast.122, pred[2,128]{1,0:T(4,128)(4,1)S(1)} %iota_compare_fusion.3), kind=kOutput, calls=%fused_computation.11 | convolution fusion | flops 21032960 | bytes 10731136 | tf_op jit(solution)/shard_map/phn,pnc->phc/dot_general | solution.py:96
  40.1 3.8 %all-to-all-start.1 = ((bf16[16,192,128]{2,1,0:T(8,128)(2,1)}), bf16[16,192,128]{2,1,0:T(8,128)(2,1)S(1)}, u32[]{:S(2)}, u32[]{:S(2)}) async-start(bf16[16,192,128]{2,1,0:T(8,128)(2,1)} %tile.10), calls=%async_computation.1 | async-start | bytes 1572864 | tf_op jit(solution)/shard_map/all_to_all | solution.py:187
  44.0 0.2 convolution_convert_fusion.3
  44.3 0.2 convolution_add_fusion.1
  44.5 0.2 fusion.8
  44.9 11.4 %all-to-all-done.1 = bf16[16,192,128]{2,1,0:T(8,128)(2,1)S(1)} async-done(((bf16[16,192,128]{2,1,0:T(8,128)(2,1)}), bf16[16,192,128]{2,1,0:T(8,128)(2,1)S(1)}, u32[]{:S(2)}, u32[]{:S(2)}) %all-to-all-start.1) | async-done | bytes 786464 | tf_op jit(solution)/shard_map/all_to_all | solution.py:187
  56.4 0.9 fusion.55
  57.3 7.4 %all-to-all-start.2 = ((f32[48,8,128]{2,0,1:T(8,128)}), f32[48,8,128]{2,0,1:T(8,128)S(1)}, u32[]{:S(2)}, u32[]{:S(2)}) async-start(f32[48,8,128]{2,0,1:T(8,128)} %fusion.55), calls=%async_computation.2 | async-start | bytes 393216 | tf_op jit(solution)/shard_map/all_to_all | solution.py:20
  64.7 1.1 reduce-window.6
  65.8 0.2 slice_reduce_fusion
  66.1 0.2 reduce-window.9
  66.2 4.3 %all-to-all-done.2 = f32[48,8,128]{2,0,1:T(8,128)S(1)} async-done(((f32[48,8,128]{2,0,1:T(8,128)}), f32[48,8,128]{2,0,1:T(8,128)S(1)}, u32[]{:S(2)}, u32[]{:S(2)}) %all-to-all-start.2) | async-done | bytes 196640 | tf_op jit(solution)/shard_map/all_to_all | solution.py:20
  70.5 0.7 broadcast_in_dim.225
  71.2 4.2 %all-to-all-start.3 = ((f32[8,48,128]{2,1,0:T(8,128)}), f32[8,48,128]{2,1,0:T(8,128)S(1)}, u32[]{:S(2)}, u32[]{:S(2)}) async-start(f32[8,48,128]{2,1,0:T(8,128)} %broadcast_in_dim.225), calls=%async_computation.3 | async-start | bytes 393216 | tf_op jit(solution)/shard_map/all_to_all | solution.py:26
  75.6 5.8 %all-to-all-done.3 = f32[8,48,128]{2,1,0:T(8,128)S(1)} async-done(((f32[8,48,128]{2,1,0:T(8,128)}), f32[8,48,128]{2,1,0:T(8,128)S(1)}, u32[]{:S(2)}, u32[]{:S(2)}) %all-to-all-start.3) | async-done | bytes 196640 | tf_op jit(solution)/shard_map/all_to_all | solution.py:26
  81.5 0.2 multiply_reduce_fusion.1
  82.0 0.7 tile.11
  82.7 3.5 %all-to-all-start.4 = ((bf16[16,48,128]{2,1,0:T(8,128)(2,1)}), bf16[16,48,128]{2,1,0:T(8,128)(2,1)S(1)}, u32[]{:S(2)}, u32[]{:S(2)}) async-start(bf16[16,48,128]{2,1,0:T(8,128)(2,1)} %tile.11), calls=%async_computation.4 | async-start | bytes 393216 | tf_op jit(solution)/shard_map/all_to_all | solution.py:32
  86.3 7.1 %all-to-all-done.4 = bf16[16,48,128]{2,1,0:T(8,128)(2,1)S(1)} async-done(((bf16[16,48,128]{2,1,0:T(8,128)(2,1)}), bf16[16,48,128]{2,1,0:T(8,128)(2,1)S(1)}, u32[]{:S(2)}, u32[]{:S(2)}) %all-to-all-start.4) | async-done | bytes 196640 | tf_op jit(solution)/shard_map/all_to_all | solution.py:32
  93.6 4.0 %fusion.54 = (f32[4,32]{1,0:T(4,128)S(1)}, bf16[4,32,4096]{2,1,0:T(8,128)(2,1)S(1)}) fusion(pred[4096]{0:T(1024)(128)(4,1)S(1)} %fusion.33, bf16[4,32,128]{2,1,0:T(8,128)(2,1)S(1)} %bitcast.130, bf16[4,4096,128]{2,1,0:T(8,128)(2,1)} %bitcast.111), kind=kOutput, calls=%fused_computation.133 | convolution fusion | flops 137367552 | bytes 5280256 | tf_op jit(solution)/shard_map/sub | solution.py:140
  97.7 3.0 %convolution_divide_fusion = f32[4,32,128]{2,1,0:T(8,128)S(1)} fusion(bf16[4,4096,128]{2,1,0:T(8,128)(2,1)} %bitcast.112, bf16[4,32,4095]{2,1,0:T(8,128)(2,1)S(1)} %bitcast.119, f32[4,32]{1,0:T(4,128)S(1)} %get-tuple-element.30), kind=kOutput, calls=%fused_computation.12 | convolution fusion | flops 134234112 | bytes 5308672 | tf_op jit(solution)/shard_map/gmn,gnc->gmc/dot_general | solution.py:143
  100.7 0.3 fusion.5
  101.0 10.2 %all_to_all.86 = bf16[16,48,128]{2,1,0:T(8,128)(2,1)S(1)} all-to-all(bf16[16,48,128]{2,1,0:T(8,128)(2,1)S(1)} %bitcast.126), channel_id=1, replica_groups=mesh['req'=16,'head'=8] {'req'}, dimensions={0} | all-to-all | bytes 393216 | tf_op jit(solution)/shard_map/all_to_all | solution.py:150
  111.2 0.2 fusion.38
  111.4 11.5 %all_to_all.87 = f32[48,8,128]{2,0,1:T(8,128)S(1)} all-to-all(f32[48,8,128]{2,0,1:T(8,128)S(1)} %fusion.38), channel_id=1, replica_groups=mesh['req'=16,'head'=8] {'head'}, dimensions={1} | all-to-all | bytes 393216 | tf_op jit(solution)/shard_map/all_to_all | solution.py:20
  122.9 0.7 broadcast_in_dim.234
  123.6 4.2 %all-to-all-start.7 = ((f32[8,48,128]{2,1,0:T(8,128)}), f32[8,48,128]{2,1,0:T(8,128)S(1)}, u32[]{:S(2)}, u32[]{:S(2)}) async-start(f32[8,48,128]{2,1,0:T(8,128)} %broadcast_in_dim.234), calls=%async_computation.7 | async-start | bytes 393216 | tf_op jit(solution)/shard_map/all_to_all | solution.py:26
  127.9 0.6 copy.66
  128.5 5.2 %all-to-all-done.7 = f32[8,48,128]{2,1,0:T(8,128)S(1)} async-done(((f32[8,48,128]{2,1,0:T(8,128)}), f32[8,48,128]{2,1,0:T(8,128)S(1)}, u32[]{:S(2)}, u32[]{:S(2)}) %all-to-all-start.7) | async-done | bytes 196640 | tf_op jit(solution)/shard_map/all_to_all | solution.py:26
  133.9 0.2 multiply_reduce_fusion
  134.1 0.7 add_convert_fusion
  (56 shorter events, 2.5 us)
Async XLA Ops:
  0.6 23.6 %copy-start = (bf16[48,1024]{1,0:T(8,128)(2,1)S(1)}, bf16[48,1024]{1,0:T(8,128)(2,1)}, u32[]{:S(2)}) copy-start(bf16[48,1024]{1,0:T(8,128)(2,1)} %param.15) | copy-start | bytes 294916
  2.5 21.7 %all-to-all-start = ((bf16[16,192,128]{2,1,0:T(8,128)(2,1)}), bf16[16,192,128]{2,1,0:T(8,128)(2,1)S(1)}, u32[]{:S(2)}, u32[]{:S(2)}) async-start(bf16[16,192,128]{2,1,0:T(8,128)(2,1)} %tile.9), calls=%async_computation | async-start | bytes 1572864 | tf_op jit(solution)/shard_map/all_to_all | solution.py:32
  40.0 24.6 %copy-start.1 = (s32[768]{0:T(1024)S(1)}, s32[768]{0:T(1024)}, u32[]{:S(2)}) copy-start(s32[768]{0:T(1024)} %param.19) | copy-start | bytes 9220
  40.0 41.6 %copy-start.2 = (f32[1024]{0:T(1024)S(1)}, f32[1024]{0:T(1024)}, u32[]{:S(2)}) copy-start(f32[1024]{0:T(1024)} %param.27) | copy-start | bytes 12292
  40.0 41.6 %copy-start.3 = (f32[1024]{0:T(1024)S(1)}, f32[1024]{0:T(1024)}, u32[]{:S(2)}) copy-start(f32[1024]{0:T(1024)} %param.26) | copy-start | bytes 12292
  40.1 16.3 %all-to-all-start.1 = ((bf16[16,192,128]{2,1,0:T(8,128)(2,1)}), bf16[16,192,128]{2,1,0:T(8,128)(2,1)S(1)}, u32[]{:S(2)}, u32[]{:S(2)}) async-start(bf16[16,192,128]{2,1,0:T(8,128)(2,1)} %tile.10), calls=%async_computation.1 | async-start | bytes 1572864 | tf_op jit(solution)/shard_map/all_to_all | solution.py:187
  57.3 13.2 %all-to-all-start.2 = ((f32[48,8,128]{2,0,1:T(8,128)}), f32[48,8,128]{2,0,1:T(8,128)S(1)}, u32[]{:S(2)}, u32[]{:S(2)}) async-start(f32[48,8,128]{2,0,1:T(8,128)} %fusion.55), calls=%async_computation.2 | async-start | bytes 393216 | tf_op jit(solution)/shard_map/all_to_all | solution.py:20
  71.2 10.1 %all-to-all-start.3 = ((f32[8,48,128]{2,1,0:T(8,128)}), f32[8,48,128]{2,1,0:T(8,128)S(1)}, u32[]{:S(2)}, u32[]{:S(2)}) async-start(f32[8,48,128]{2,1,0:T(8,128)} %broadcast_in_dim.225), calls=%async_computation.3 | async-start | bytes 393216 | tf_op jit(solution)/shard_map/all_to_all | solution.py:26
  82.7 10.7 %all-to-all-start.4 = ((bf16[16,48,128]{2,1,0:T(8,128)(2,1)}), bf16[16,48,128]{2,1,0:T(8,128)(2,1)S(1)}, u32[]{:S(2)}, u32[]{:S(2)}) async-start(bf16[16,48,128]{2,1,0:T(8,128)(2,1)} %tile.11), calls=%async_computation.4 | async-start | bytes 393216 | tf_op jit(solution)/shard_map/all_to_all | solution.py:32
  97.6 36.4 %copy-start.4 = (f32[1024]{0:T(1024)S(1)}, f32[1024]{0:T(1024)}, u32[]{:S(2)}) copy-start(f32[1024]{0:T(1024)} %param.29) | copy-start | bytes 12292
  97.7 36.5 %copy-start.5 = (f32[1024]{0:T(1024)S(1)}, f32[1024]{0:T(1024)}, u32[]{:S(2)}) copy-start(f32[1024]{0:T(1024)} %param.28) | copy-start | bytes 12292
  123.6 10.1 %all-to-all-start.7 = ((f32[8,48,128]{2,1,0:T(8,128)}), f32[8,48,128]{2,1,0:T(8,128)S(1)}, u32[]{:S(2)}, u32[]{:S(2)}) async-start(f32[8,48,128]{2,1,0:T(8,128)} %broadcast_in_dim.234), calls=%async_computation.7 | async-start | bytes 393216 | tf_op jit(solution)/shard_map/all_to_all | solution.py:26

commit v10 on v8

--- a/solution.py
+++ b/solution.py
@@ -168,12 +168,15 @@
     head_cols = kv_pool.shape[3]
     scale = HEAD_DIM ** (-0.5)
     in_rows = w_self_in.shape[0]
-    first = gather_rows(w_self_in.transpose(1, 0, 2).reshape(-1, head_cols)[None], "req")
-    rest = jnp.concatenate([w_cross_q, w_self_out.T, w_cross_out.T], axis=0)
+    stacked_in = w_self_in.transpose(1, 0, 2)
+    first = gather_rows(stacked_in[:2].reshape(-1, head_cols)[None], "req")
+    rest = jnp.concatenate([stacked_in[2], w_cross_q, w_self_out.T, w_cross_out.T], axis=0)
     parts = lax.psum(1, "req")
     rest = jnp.tile(rest[None], (parts, 1, 1))
     rest = lax.all_to_all(rest, "req", 0, 0, tiled=True)
-    full_in = [first[:, k * in_rows : (k + 1) * in_rows].reshape(-1, head_cols) for k in range(3)]
+    full_in = [first[:, k * in_rows : (k + 1) * in_rows].reshape(-1, head_cols) for k in range(2)]
+    full_in.append(rest[:, :in_rows].reshape(-1, head_cols))
+    rest = rest[:, in_rows:]
     full_query = rest[:, :in_rows].reshape(-1, head_cols)
     full_out = rest[:, in_rows : 2 * in_rows].reshape(-1, head_cols)
     full_cross = rest[:, 2 * in_rows :].reshape(-1, head_cols)

time: 127 us -> 124 us (0.976)
  waiting for transfers between devices: 31.2 us -> 27.9 us
    all_to_all x2, waiting for transfers between devices: 15.9 us -> 12.4 us  [gather_rows(): return lax.all_to_all(spread, axis_name, 0, 0, tiled=True)]
    all_to_all x2, starting transfers between devices: 15.3 us -> 13.8 us  [gather_rows(): return lax.all_to_all(spread, axis_name, 0, 0, tiled=True)]
  transfers between devices with their start and end apart: 6 -> 6, of which waited for: 5 -> 6; matrix products, arithmetic and copies ran while one was open for 18% -> 18% of each run, Pallas kernels for 0% -> 0%
where the time goes in v10:
time: 124 us; the launch traced here: 123 us
  starting transfers between devices  33.7 us (27%)
  waiting for transfers between devices  27.9 us (22%)
  matrix products  22.6 us (18%)
  blocking collectives  21.9 us (18%)
  local copies, waits for them, and re-layouts  8.76 us (7%)
  other arithmetic  6.97 us (6%)
    all_to_all x2, starting transfers between devices, gather_rows(): return lax.all_to_all(spread, axis_name, 0, 0, tiled=True)  13.8 us
    all_to_all x2, waiting for transfers between devices, gather_rows(): return lax.all_to_all(spread, axis_name, 0, 0, tiled=True)  12.4 us
    all_to_all x1, blocking collectives, head_total(): pieces = lax.all_to_all(partial_value, 'head', 1, 0, tiled=True)  11.7 us
    all_to_all x2, waiting for transfers between devices, head_total(): lax.all_to_all(spread.reshape(parts * rows, cols // parts), 'head', 0, 1,...  11 us
    all_to_all x1, blocking collectives, group_attention(): lax.all_to_all(placed.astype(jnp.bfloat16), 'req', 0, 0, tiled=True)  10.2 us
    all_to_all x2, starting transfers between devices, head_total(): lax.all_to_all(spread.reshape(parts * rows, cols // parts), 'head', 0, 1,...  8.49 us
    all_to_all x1, starting transfers between devices, head_total(): pieces = lax.all_to_all(partial_value, 'head', 1, 0, tiled=True)  7.78 us
    dot_general x1, matrix products, paged_attention(): jnp.einsum('phc,pnc->phn', query_blocks, stored, preferred_element_type=j...  6.88 us
  transfers between devices with their start and end apart: 6, of which 6 were waited for; matrix products, arithmetic and copies ran while one was open for 18% of the time, Pallas kernels for 0%

profile of v10, /device:TPU:1, one launch (start us, length us, event | category | flops | bytes accessed | tf_op | source)
XLA Modules:
  0.0 122.8 jit_solution(15351719310386420627)
XLA Ops:
  0.6 0.8 slice.123
  1.4 0.9 tile.9
  2.3 8.4 %all-to-all-start = ((bf16[16,128,128]{2,1,0:T(8,128)(2,1)}), bf16[16,128,128]{2,1,0:T(8,128)(2,1)S(1)}, u32[]{:S(2)}, u32[]{:S(2)}) async-start(bf16[16,128,128]{2,1,0:T(8,128)(2,1)} %tile.9), calls=%async_computation | async-start | bytes 1048576 | tf_op jit(solution)/shard_map/all_to_all | solution.py:32
  10.8 0.7 slice_bitcast_fusion
  11.5 0.8 copy.56
  12.3 0.7 and_select_fusion.3
  13.0 0.2 fusion.13
  13.2 0.7 select_reduce_fusion.4
  14.0 0.8 copy.57
  14.8 0.2 select_reduce_fusion.1
  15.0 0.8 pad_maximum_fusion
  15.9 5.2 %all-to-all-done = bf16[16,128,128]{2,1,0:T(8,128)(2,1)S(1)} async-done(((bf16[16,128,128]{2,1,0:T(8,128)(2,1)}), bf16[16,128,128]{2,1,0:T(8,128)(2,1)S(1)}, u32[]{:S(2)}, u32[]{:S(2)}) %all-to-all-start) | async-done | bytes 524320 | tf_op jit(solution)/shard_map/all_to_all | solution.py:32
  21.2 1.2 tile.10
  22.4 3.7 %all-to-all-start.1 = ((bf16[16,256,128]{2,1,0:T(8,128)(2,1)}), bf16[16,256,128]{2,1,0:T(8,128)(2,1)S(1)}, u32[]{:S(2)}, u32[]{:S(2)}) async-start(bf16[16,256,128]{2,1,0:T(8,128)(2,1)} %tile.10), calls=%async_computation.1 | async-start | bytes 2097152 | tf_op jit(solution)/shard_map/all_to_all | solution.py:176
  26.1 0.2 convolution_convert_fusion.5
  26.3 0.2 convolution_convert_fusion
  26.5 6.9 %fusion.54 = (f32[160,2]{1,0:T(8,128)S(1)}, f32[160,2,256]{2,1,0:T(2,128)S(1)}) fusion(bf16[160,256,128]{2,1,0:T(8,128)(2,1)} %bitcast.113, pred[2,128]{1,0:T(4,128)(4,1)S(1)} %iota_compare_fusion.3, bf16[160,128]{1,0:T(8,128)(2,1)S(1)} %convolution_convert_fusion, pred[160,256]{1,0:T(8,128)(4,1)S(1)} %fusion.19), kind=kOutput, calls=%fused_computation.134 | convolution fusion | flops 21257920 | bytes 10896896 | tf_op jit(solution)/shard_map/phc,pnc->phn/dot_general | solution.py:71
  34.0 0.3 fusion.31
  34.3 0.6 fusion.51
  34.9 5.5 %fusion.7 = f32[160,128]{1,0:T(8,128)S(1)} fusion(bf16[160,256,128]{2,1,0:T(8,128)(2,1)} %bitcast.114, bf16[160,2,255]{2,1,0:T(2,128)(2,1)S(1)} %bitcast.126, pred[2,128]{1,0:T(4,128)(4,1)S(1)} %iota_compare_fusion.3), kind=kOutput, calls=%fused_computation.12 | convolution fusion | flops 21032960 | bytes 10731136 | tf_op jit(solution)/shard_map/phn,pnc->phc/dot_general | solution.py:93
  40.6 0.2 convolution_add_fusion.1
  40.8 0.3 all-to-all-done.1
  41.4 0.2 fusion.9
  41.8 0.9 fusion.56
  42.7 7.8 %all-to-all-start.2 = ((f32[48,8,128]{2,0,1:T(8,128)}), f32[48,8,128]{2,0,1:T(8,128)S(1)}, u32[]{:S(2)}, u32[]{:S(2)}) async-start(f32[48,8,128]{2,0,1:T(8,128)} %fusion.56), calls=%async_computation.2 | async-start | bytes 393216 | tf_op jit(solution)/shard_map/all_to_all | solution.py:20
  50.5 1.1 reduce-window.6
  51.6 0.2 slice_reduce_fusion
  51.9 0.2 reduce-window.9
  52.0 4.3 %all-to-all-done.2 = f32[48,8,128]{2,0,1:T(8,128)S(1)} async-done(((f32[48,8,128]{2,0,1:T(8,128)}), f32[48,8,128]{2,0,1:T(8,128)S(1)}, u32[]{:S(2)}, u32[]{:S(2)}) %all-to-all-start.2) | async-done | bytes 196640 | tf_op jit(solution)/shard_map/all_to_all | solution.py:20
  56.3 0.7 broadcast_in_dim.225
  57.0 4.2 %all-to-all-start.3 = ((f32[8,48,128]{2,1,0:T(8,128)}), f32[8,48,128]{2,1,0:T(8,128)S(1)}, u32[]{:S(2)}, u32[]{:S(2)}) async-start(f32[8,48,128]{2,1,0:T(8,128)} %broadcast_in_dim.225), calls=%async_computation.3 | async-start | bytes 393216 | tf_op jit(solution)/shard_map/all_to_all | solution.py:26
  61.4 5.8 %all-to-all-done.3 = f32[8,48,128]{2,1,0:T(8,128)S(1)} async-done(((f32[8,48,128]{2,1,0:T(8,128)}), f32[8,48,128]{2,1,0:T(8,128)S(1)}, u32[]{:S(2)}, u32[]{:S(2)}) %all-to-all-start.3) | async-done | bytes 196640 | tf_op jit(solution)/shard_map/all_to_all | solution.py:26
  67.3 0.2 multiply_reduce_fusion.1
  67.8 0.7 tile.11
  68.5 5.4 %all-to-all-start.4 = ((bf16[16,48,128]{2,1,0:T(8,128)(2,1)}), bf16[16,48,128]{2,1,0:T(8,128)(2,1)S(1)}, u32[]{:S(2)}, u32[]{:S(2)}) async-start(bf16[16,48,128]{2,1,0:T(8,128)(2,1)} %tile.11), calls=%async_computation.4 | async-start | bytes 393216 | tf_op jit(solution)/shard_map/all_to_all | solution.py:32
  73.9 7.2 %all-to-all-done.4 = bf16[16,48,128]{2,1,0:T(8,128)(2,1)S(1)} async-done(((bf16[16,48,128]{2,1,0:T(8,128)(2,1)}), bf16[16,48,128]{2,1,0:T(8,128)(2,1)S(1)}, u32[]{:S(2)}, u32[]{:S(2)}) %all-to-all-start.4) | async-done | bytes 196640 | tf_op jit(solution)/shard_map/all_to_all | solution.py:32
  81.3 4.1 %fusion.55 = (f32[4,32]{1,0:T(4,128)S(1)}, bf16[4,32,4096]{2,1,0:T(8,128)(2,1)S(1)}) fusion(pred[4096]{0:T(1024)(128)(4,1)S(1)} %fusion.33, bf16[4,32,128]{2,1,0:T(8,128)(2,1)S(1)} %bitcast.136, bf16[4,4096,128]{2,1,0:T(8,128)(2,1)} %bitcast.115), kind=kOutput, calls=%fused_computation.135 | convolution fusion | flops 137367552 | bytes 5280256 | tf_op jit(solution)/shard_map/sub | solution.py:136
  85.4 3.0 %convolution_divide_fusion = f32[4,32,128]{2,1,0:T(8,128)S(1)} fusion(bf16[4,4096,128]{2,1,0:T(8,128)(2,1)} %bitcast.116, bf16[4,32,4095]{2,1,0:T(8,128)(2,1)S(1)} %bitcast.119, f32[4,32]{1,0:T(4,128)S(1)} %get-tuple-element.30), kind=kOutput, calls=%fused_computation.13 | convolution fusion | flops 134234112 | bytes 5308672 | tf_op jit(solution)/shard_map/gmn,gnc->gmc/dot_general | solution.py:139
  88.4 0.3 fusion.6
  88.7 10.2 %all_to_all.86 = bf16[16,48,128]{2,1,0:T(8,128)(2,1)S(1)} all-to-all(bf16[16,48,128]{2,1,0:T(8,128)(2,1)S(1)} %bitcast.130), channel_id=1, replica_groups=mesh['req'=16,'head'=8] {'req'}, dimensions={0} | all-to-all | bytes 393216 | tf_op jit(solution)/shard_map/all_to_all | solution.py:146
  99.0 0.2 fusion.38
  99.2 11.7 %all_to_all.87 = f32[48,8,128]{2,0,1:T(8,128)S(1)} all-to-all(f32[48,8,128]{2,0,1:T(8,128)S(1)} %fusion.38), channel_id=1, replica_groups=mesh['req'=16,'head'=8] {'head'}, dimensions={1} | all-to-all | bytes 393216 | tf_op jit(solution)/shard_map/all_to_all | solution.py:20
  110.9 0.7 broadcast_in_dim.234
  111.6 4.2 %all-to-all-start.7 = ((f32[8,48,128]{2,1,0:T(8,128)}), f32[8,48,128]{2,1,0:T(8,128)S(1)}, u32[]{:S(2)}, u32[]{:S(2)}) async-start(f32[8,48,128]{2,1,0:T(8,128)} %broadcast_in_dim.234), calls=%async_computation.7 | async-start | bytes 393216 | tf_op jit(solution)/shard_map/all_to_all | solution.py:26
  115.8 0.6 copy.66
  116.5 5.2 %all-to-all-done.7 = f32[8,48,128]{2,1,0:T(8,128)S(1)} async-done(((f32[8,48,128]{2,1,0:T(8,128)}), f32[8,48,128]{2,1,0:T(8,128)S(1)}, u32[]{:S(2)}, u32[]{:S(2)}) %all-to-all-start.7) | async-done | bytes 196640 | tf_op jit(solution)/shard_map/all_to_all | solution.py:26
  121.9 0.2 multiply_reduce_fusion
  122.1 0.7 add_convert_fusion
  (57 shorter events, 2.7 us)
Async XLA Ops:
  0.6 25.4 %copy-start = (bf16[48,1024]{1,0:T(8,128)(2,1)S(1)}, bf16[48,1024]{1,0:T(8,128)(2,1)}, u32[]{:S(2)}) copy-start(bf16[48,1024]{1,0:T(8,128)(2,1)} %param.15) | copy-start | bytes 294916
  2.3 18.8 %all-to-all-start = ((bf16[16,128,128]{2,1,0:T(8,128)(2,1)}), bf16[16,128,128]{2,1,0:T(8,128)(2,1)S(1)}, u32[]{:S(2)}, u32[]{:S(2)}) async-start(bf16[16,128,128]{2,1,0:T(8,128)(2,1)} %tile.9), calls=%async_computation | async-start | bytes 1048576 | tf_op jit(solution)/shard_map/all_to_all | solution.py:32
  22.4 18.7 %all-to-all-start.1 = ((bf16[16,256,128]{2,1,0:T(8,128)(2,1)}), bf16[16,256,128]{2,1,0:T(8,128)(2,1)S(1)}, u32[]{:S(2)}, u32[]{:S(2)}) async-start(bf16[16,256,128]{2,1,0:T(8,128)(2,1)} %tile.10), calls=%async_computation.1 | async-start | bytes 2097152 | tf_op jit(solution)/shard_map/all_to_all | solution.py:176
  34.9 15.6 %copy-start.1 = (s32[768]{0:T(1024)S(1)}, s32[768]{0:T(1024)}, u32[]{:S(2)}) copy-start(s32[768]{0:T(1024)} %param.19) | copy-start | bytes 9220
  40.4 27.0 %copy-start.2 = (f32[1024]{0:T(1024)S(1)}, f32[1024]{0:T(1024)}, u32[]{:S(2)}) copy-start(f32[1024]{0:T(1024)} %param.27) | copy-start | bytes 12292
  40.4 27.0 %copy-start.3 = (f32[1024]{0:T(1024)S(1)}, f32[1024]{0:T(1024)}, u32[]{:S(2)}) copy-start(f32[1024]{0:T(1024)} %param.26) | copy-start | bytes 12292
  42.7 13.6 %all-to-all-start.2 = ((f32[48,8,128]{2,0,1:T(8,128)}), f32[48,8,128]{2,0,1:T(8,128)S(1)}, u32[]{:S(2)}, u32[]{:S(2)}) async-start(f32[48,8,128]{2,0,1:T(8,128)} %fusion.56), calls=%async_computation.2 | async-start | bytes 393216 | tf_op jit(solution)/shard_map/all_to_all | solution.py:20
  57.0 10.1 %all-to-all-start.3 = ((f32[8,48,128]{2,1,0:T(8,128)}), f32[8,48,128]{2,1,0:T(8,128)S(1)}, u32[]{:S(2)}, u32[]{:S(2)}) async-start(f32[8,48,128]{2,1,0:T(8,128)} %broadcast_in_dim.225), calls=%async_computation.3 | async-start | bytes 393216 | tf_op jit(solution)/shard_map/all_to_all | solution.py:26
  68.5 12.6 %all-to-all-start.4 = ((bf16[16,48,128]{2,1,0:T(8,128)(2,1)}), bf16[16,48,128]{2,1,0:T(8,128)(2,1)S(1)}, u32[]{:S(2)}, u32[]{:S(2)}) async-start(bf16[16,48,128]{2,1,0:T(8,128)(2,1)} %tile.11), calls=%async_computation.4 | async-start | bytes 393216 | tf_op jit(solution)/shard_map/all_to_all | solution.py:32
  85.4 36.7 %copy-start.4 = (f32[1024]{0:T(1024)S(1)}, f32[1024]{0:T(1024)}, u32[]{:S(2)}) copy-start(f32[1024]{0:T(1024)} %param.29) | copy-start | bytes 12292
  85.4 36.7 %copy-start.5 = (f32[1024]{0:T(1024)S(1)}, f32[1024]{0:T(1024)}, u32[]{:S(2)}) copy-start(f32[1024]{0:T(1024)} %param.28) | copy-start | bytes 12292
  111.6 10.1 %all-to-all-start.7 = ((f32[8,48,128]{2,1,0:T(8,128)}), f32[8,48,128]{2,1,0:T(8,128)S(1)}, u32[]{:S(2)}, u32[]{:S(2)}) async-start(f32[8,48,128]{2,1,0:T(8,128)} %broadcast_in_dim.234), calls=%async_computation.7 | async-start | bytes 393216 | tf_op jit(solution)/shard_map/all_to_all | solution.py:26
